TPU v7x, 512 devices: a whole 4x8x8 slice. The times are simulated.
512 devices in a mesh: gx: 32 (over y, x), az: 8 (over z), row: 2 (over core).
Axes of the slice: x: 4, y: 8, z: 8, core: 2. Of those that a mesh axis runs over, the one named last changes fastest.
Arguments:
- adjoint: float32 [5, 256, 32, 1024], P(None, 'gx', 'row', 'az'), may hold values from -6 to 6
- coeff: float32 [3, 256, 32, 1024], P(None, 'gx', 'row', 'az'), may hold values from 0.5 to 2
- flux: float32 [3, 5, 5], replicated, may hold values from -1.5 to 1.5
- target_cell: int32 [131072], P(('gx', 'az', 'row')), may hold values from 0 to 16383
- donor_owner: int32 [131072, 1], P(('gx', 'az', 'row')), may hold values from 0 to 31; in each aligned block of 256 rows (0 to 255, 256 to 511, ...) at most 32 rows name the same one
- donor_cell: int32 [131072], P(('gx', 'az', 'row')), may hold values from 0 to 16383
Outputs:
- gradient: float32 [5, 256, 32, 1024], P(None, 'gx', 'row', 'az')
Inputs may be any that keep to these rules, and one draw needn't show every extreme that they name: Each target point's donor lies on the slab donor_owner names; among the 256 target points of one device at most 32 name the same owner, and 32 is reached in every draw. `target_cell`: A flattened cell index inside one device's block. `donor_cell`: A flattened cell index inside the owner's block.
All inputs are finite; a program needn't handle non-finite values.
Results may differ from a plain program's by a relative error of at most 0.0003.
Values sent between devices are 32-bit elements; how exact they have to be, the bound alone decides.
No kernel may reach another device: no remote copies, remote signals or barrier semaphores. Data moves between devices by JAX's collectives and lax.ppermute only.
A program may use at most 64 MiB of HBM per device.

v0:
```python
import math

import jax
import jax.numpy as jnp
from jax import lax
from jax.sharding import PartitionSpec as P

filter_alpha = 0.49
sat_gain = 0.5
pade_coeffs = [
    (193.0 + 126.0 * filter_alpha) / 256.0,
    (105.0 + 302.0 * filter_alpha) / 256.0,
    15.0 * (2.0 * filter_alpha - 1.0) / 64.0,
    45.0 * (1.0 - 2.0 * filter_alpha) / 512.0,
    5.0 * (2.0 * filter_alpha - 1.0) / 256.0,
    (1.0 - 2.0 * filter_alpha) / 512.0,
]
root_value = (-1.0 + (1.0 - 4.0 * filter_alpha * filter_alpha) ** 0.5) / (2.0 * filter_alpha)
green_scale = 1.0 / (1.0 + 2.0 * filter_alpha * root_value)


def with_halo(value, sides, width, wrap):
    for axis, dim in sides:
        size, length = (lax.axis_size(axis), value.shape[dim])
        up = [(i, (i + 1) % size) for i in range(size if wrap else size - 1)]
        down = [(j, i) for i, j in up]
        last = lax.slice_in_dim(value, length - width, length, axis=dim)
        first = lax.slice_in_dim(value, 0, width, axis=dim)
        before = lax.ppermute(last, axis, up)
        after = lax.ppermute(first, axis, down)
        value = jnp.concatenate([before, value, after], axis=dim)
    return value


def root_power(exponent):
    parity = 1.0 - 2.0 * (exponent % 2).astype(jnp.float32)
    return parity * jnp.exp(exponent.astype(jnp.float32) * math.log(-root_value))


def stencil_weight(stencil_shift):
    if stencil_shift == 0:
        return pade_coeffs[0]
    return 0.5 * pade_coeffs[abs(stencil_shift)]


def loop_kernel(offset, length):
    closing = 1.0 - root_power(jnp.full((), length, jnp.int32))
    running = jnp.zeros(offset.shape, jnp.float32)
    for stencil_shift in range(-5, 6):
        wrapped = (offset - stencil_shift) % length
        images = root_power(wrapped) + root_power(length - wrapped)
        running = running + stencil_weight(stencil_shift) * green_scale * images / closing
    return running


def shards(adjoint, coeff, flux, target_cell, donor_owner, donor_cell):
    fields, rows_x, rows_r, cells_a = adjoint.shape
    loop_span = cells_a * lax.axis_size("az")
    block_count = loop_span // cells_a
    block_shifts = [-1, 0, 1]
    local_index = jnp.arange(cells_a, dtype=jnp.int32)
    block_tables = []
    for block_shift in block_shifts:
        offsets = (local_index[:, None] - local_index[None, :] - block_shift * cells_a) % loop_span
        block_tables.append(loop_kernel(offsets, loop_span))
    grouped = adjoint.reshape(fields * rows_x, rows_r, cells_a)
    line_block = lax.all_to_all(grouped, "az", split_axis=0, concat_axis=2, tiled=True)
    lead, inner, span = line_block.shape
    blocks = line_block.reshape(lead, inner, block_count, cells_a)
    smooth = jnp.zeros(blocks.shape, jnp.float32)
    for block_shift, table in zip(block_shifts, block_tables):
        moved = jnp.roll(blocks, -block_shift, axis=2)
        smooth = smooth + jnp.einsum("lijc,oc->lijo", moved, table, precision=lax.Precision.HIGHEST)
    smooth = smooth.reshape(lead, inner, span)
    filtered = lax.all_to_all(smooth, "az", split_axis=2, concat_axis=0, tiled=True).reshape(
        adjoint.shape
    )
    face_pad = with_halo(filtered, (("gx", 1), ("row", 2)), 1, False)
    along_x = face_pad[:, 2:, 1:-1, :] - face_pad[:, :-2, 1:-1, :]
    along_r = face_pad[:, 1:-1, 2:, :] - face_pad[:, 1:-1, :-2, :]
    cycle_pad = with_halo(filtered, (("az", 3),), 1, True)
    along_a = cycle_pad[:, :, :, 2:] - cycle_pad[:, :, :, :-2]
    gradient = filtered
    for direction, change in enumerate((along_x, along_r, along_a)):
        mixing = jnp.einsum(
            "fg,fxra->gxra", flux[direction], change, precision=lax.Precision.HIGHEST
        )
        gradient = gradient + coeff[direction][None] * mixing
    cell_count = rows_x * rows_r * cells_a
    source = sat_gain * jnp.take(filtered.reshape(fields, cell_count), target_cell, axis=1)
    flat_grad = gradient.reshape(fields, cell_count)
    flat_grad = flat_grad.at[:, target_cell].add(-source)
    owner_rows = donor_owner[:, 0]
    owners = lax.axis_size("gx")
    capacity = target_cell.shape[0] // 8
    onehot = (owner_rows[:, None] == jnp.arange(owners, dtype=jnp.int32)[None, :]).astype(jnp.int32)
    slot_rank = jnp.sum(onehot * (jnp.cumsum(onehot, axis=0) - 1), axis=1)
    slot_place = owner_rows * capacity + slot_rank
    packed = jnp.concatenate([source, donor_cell.astype(jnp.float32)[None, :]], axis=0)
    outbox = jnp.zeros((fields + 1, owners * capacity), jnp.float32).at[:, slot_place].set(packed)
    received = lax.all_to_all(
        outbox.reshape(fields + 1, owners, capacity), "gx", split_axis=1, concat_axis=1, tiled=True
    )
    received = received.reshape(fields + 1, owners * capacity)
    flat_grad = flat_grad.at[:, received[fields].astype(jnp.int32)].add(received[:fields])
    return flat_grad.reshape(adjoint.shape)


def solution(mesh):
    return jax.shard_map(
        shards,
        mesh=mesh,
        in_specs=(
            P(None, "gx", "row", "az"),
            P(None, "gx", "row", "az"),
            P(),
            P(("gx", "az", "row")),
            P(("gx", "az", "row"), None),
            P(("gx", "az", "row")),
        ),
        out_specs=P(None, "gx", "row", "az"),
        check_vma=False,
    )
```

profile of v0, /device:TPU:2, one launch (start us, length us, event | category | flops | bytes accessed | tf_op | source)
XLA Modules:
  0.0 140.9 jit_solution(15649608011117938644)
XLA Ops:
  0.0 10.3 %all-to-all-start = ((f32[40,16,128]{2,1,0:T(8,128)}), f32[40,16,128]{2,1,0:T(8,128)S(1)}, u32[]{:S(2)}, u32[]{:S(2)}) async-start(f32[40,16,128]{2,1,0:T(8,128)} %bitcast.125), calls=%async_computation | async-start | bytes 655360 | tf_op jit(solution)/shard_map/all_to_all | solution.py:67
  11.8 0.8 fusion.691
  14.0 9.6 %all-to-all-done = f32[40,16,128]{2,1,0:T(8,128)S(1)} async-done(((f32[40,16,128]{2,1,0:T(8,128)}), f32[40,16,128]{2,1,0:T(8,128)S(1)}, u32[]{:S(2)}, u32[]{:S(2)}) %all-to-all-start) | async-done | bytes 327712 | tf_op jit(solution)/shard_map/all_to_all | solution.py:67
  23.8 1.7 %fusion.13 = f32[5,16,8,128]{3,2,1,0:T(8,128)S(1)} fusion(f32[5,16,7,128]{3,2,1,0:T(8,128)S(1)} %get-tuple-element.15, f32[5,16,1,128]{3,2,1,0:T(1,128)S(1)} %get-tuple-element.17), kind=kOutput, calls=%fused_computation.32 | convolution fusion | flops 135102464 | bytes 655360 | tf_op jit(solution)/shard_map/lijc,oc->lijo/dot_general | solution.py:73
  25.5 1.7 %fusion.6 = f32[5,16,8,128]{3,2,1,0:T(8,128)S(1)} fusion(f32[5,16,8,128]{3,2,1,0:T(8,128)S(1)} %fusion.13, f32[8,5,16,128]{3,2,1,0:T(8,128)S(1)} %bitcast.121), kind=kOutput, calls=%fused_computation.15 | convolution fusion | flops 135086080 | bytes 983040 | tf_op jit(solution)/shard_map/lijc,oc->lijo/dot_general | solution.py:73
  27.3 1.7 %convolution_add_fusion = f32[5,16,8,128]{3,2,1,0:T(8,128)S(1)} fusion(f32[5,16,8,128]{3,2,1,0:T(8,128)S(1)} %fusion.6, f32[5,16,1,128]{3,2,1,0:T(1,128)S(1)} %get-tuple-element.16, f32[5,16,7,128]{3,2,1,0:T(8,128)S(1)} %get-tuple-element.14), kind=kOutput, calls=%fused_computation.13 | convolution fusion | flops 135184384 | bytes 983040 | tf_op jit(solution)/shard_map/lijc,oc->lijo/dot_general | solution.py:73
  29.0 3.1 %copy.108 = f32[5,16,8,128]{1,0,3,2:T(8,128)} copy(f32[5,16,8,128]{3,2,1,0:T(8,128)S(1)} %convolution_add_fusion) | data formatting | bytes 655360 | tf_op jit(solution)/shard_map/reshape | solution.py:74
  32.1 3.6 %reshape.129 = f32[8,1,10240]{2,1,0:T(1,128)} reshape(f32[1024,5,16]{2,1,0:T(8,128)} %bitcast.114) | data formatting | bytes 655360
  35.7 3.4 %all-to-all-start.1 = ((f32[8,1,10240]{2,1,0:T(1,128)}), f32[8,1,10240]{2,1,0:T(1,128)S(1)}, u32[]{:S(2)}, u32[]{:S(2)}) async-start(f32[8,1,10240]{2,1,0:T(1,128)} %reshape.129), calls=%async_computation.1 | async-start | bytes 655360 | tf_op jit(solution)/shard_map/all_to_all | solution.py:75
  39.2 11.7 %all-to-all-done.1 = f32[8,1,10240]{2,1,0:T(1,128)S(1)} async-done(((f32[8,1,10240]{2,1,0:T(1,128)}), f32[8,1,10240]{2,1,0:T(1,128)S(1)}, u32[]{:S(2)}, u32[]{:S(2)}) %all-to-all-start.1) | async-done | bytes 327712 | tf_op jit(solution)/shard_map/all_to_all | solution.py:75
  51.4 1.3 reduce.6
  52.8 3.3 %reshape.130 = f32[1024,5,16]{2,1,0:T(8,128)} reshape(f32[8,10240]{1,0:T(8,128)S(1)} %reduce.6) | data formatting | bytes 655360
  56.1 2.6 %copy.81 = f32[8,5,16,128]{3,2,1,0:T(8,128)S(1)} copy(f32[8,5,16,128]{2,1,3,0:T(8,128)} %bitcast.115) | data formatting | bytes 655360 | tf_op jit(solution)/shard_map/all_to_all | solution.py:75
  59.0 2.4 %collective-permute-start = (f32[5,1,16,128]{3,2,1,0:T(8,128)S(1)}, f32[5,1,16,128]{3,2,1,0:T(8,128)S(1)}, u32[]{:S(2)}, u32[]{:S(2)}) collective-permute-start(f32[5,1,16,128]{3,2,1,0:T(8,128)S(1)} %get-tuple-element.12), channel_id=1, source_target_pairs={{16,0},{32,16},{48,32},{64,48},{80,64},{96,80},{112,96},{128,112},... | collective-permute-start | bytes 122888 | tf_op jit(solution)/shard_map/ppermute | solution.py:30
  61.4 3.4 %collective-permute-start.1 = (f32[5,1,16,128]{3,2,1,0:T(8,128)S(1)}, f32[5,1,16,128]{3,2,1,0:T(8,128)S(1)}, u32[]{:S(2)}, u32[]{:S(2)}) collective-permute-start(f32[5,1,16,128]{3,2,1,0:T(8,128)S(1)} %get-tuple-element.13), channel_id=1, source_target_pairs={{0,16},{16,32},{32,48},{48,64},{64,80},{80,96},{96,112},{112,128},... | collective-permute-start | bytes 122888 | tf_op jit(solution)/shard_map/ppermute | solution.py:29
  64.8 2.0 %collective-permute-start.4 = (f32[5,8,16,1]{3,2,1,0:T(8,128)S(1)}, f32[5,8,16,1]{3,2,1,0:T(8,128)S(1)}, u32[]{:S(2)}, u32[]{:S(2)}) collective-permute-start(f32[5,8,16,1]{3,2,1,0:T(8,128)S(1)} %get-tuple-element.10), channel_id=1, source_target_pairs={{2,0},{4,2},{6,4},{8,6},{10,8},{12,10},{14,12},{0,14},{3,1},{5,3},... | collective-permute-start | bytes 7688 | tf_op jit(solution)/shard_map/ppermute | solution.py:30
  66.8 4.0 %collective-permute-start.5 = (f32[5,8,16,1]{3,2,1,0:T(8,128)S(1)}, f32[5,8,16,1]{3,2,1,0:T(8,128)S(1)}, u32[]{:S(2)}, u32[]{:S(2)}) collective-permute-start(f32[5,8,16,1]{3,2,1,0:T(8,128)S(1)} %get-tuple-element.11), channel_id=1, source_target_pairs={{0,2},{2,4},{4,6},{6,8},{8,10},{10,12},{12,14},{14,0},{1,3},{3,5},... | collective-permute-start | bytes 7688 | tf_op jit(solution)/shard_map/ppermute | solution.py:29
  70.9 5.3 %copy.93 = f32[5,16384]{0,1:T(8,128)} copy(f32[5,16384]{1,0:T(8,128)S(1)} %reshape_reshape.3) | data formatting | bytes 655360 | tf_op jit(solution)/shard_map/reshape;reshape | solution.py:90
  76.2 4.1 %gather_fusion = f32[256,5]{1,0:T(8,128)S(1)} fusion(f32[5,16384]{0,1:T(8,128)} %copy.93, s32[1024]{0:T(1024)S(1)} %pad_clamp_fusion), kind=kCustom, calls=%fused_computation | custom fusion | bytes 11264 | tf_op jit(solution)/shard_map/jit(_take)/gather | solution.py:90
  80.6 1.3 scatter_custom_fusion.1
  82.2 0.7 reshape.131
  82.9 12.1 %all-to-all-start.2 = ((f32[32,1,192]{2,1,0:T(1,128)}), f32[32,1,192]{2,1,0:T(1,128)S(1)}, u32[]{:S(2)}, u32[]{:S(2)}) async-start(f32[32,1,192]{2,1,0:T(1,128)} %reshape.131), calls=%async_computation.2 | async-start | bytes 65536 | tf_op jit(solution)/shard_map/all_to_all | solution.py:101
  95.1 1.3 collective-permute-start.2
  96.4 3.0 %collective-permute-start.3 = (f32[5,10,1,128]{3,2,1,0:T(1,128)S(1)}, f32[5,10,1,128]{3,2,1,0:T(1,128)S(1)}, u32[]{:S(2)}, u32[]{:S(2)}) collective-permute-start(f32[5,10,1,128]{3,2,1,0:T(1,128)S(1)} %get-tuple-element.8), channel_id=1, source_target_pairs={{0,1},{2,3},{4,5},{6,7},{8,9},{10,11},{12,13},{14,15},{16,17},{18,... | collective-permute-start | bytes 76808 | tf_op jit(solution)/shard_map/ppermute | solution.py:29
  99.4 4.2 %all-to-all-done.2 = f32[32,1,192]{2,1,0:T(1,128)S(1)} async-done(((f32[32,1,192]{2,1,0:T(1,128)}), f32[32,1,192]{2,1,0:T(1,128)S(1)}, u32[]{:S(2)}, u32[]{:S(2)}) %all-to-all-start.2) | async-done | bytes 24608 | tf_op jit(solution)/shard_map/all_to_all | solution.py:101
  105.3 0.9 fusion.5
  106.2 0.8 fusion.3
  107.0 0.8 fusion.1
  107.8 5.3 %copy.94 = f32[5,16384]{0,1:T(8,128)} copy(f32[5,16384]{1,0:T(8,128)S(1)} %bitcast.118) | data formatting | bytes 655360 | tf_op jit(solution)/shard_map/reshape | solution.py:91
  113.1 8.5 %scatter_custom_fusion = f32[5,16384]{0,1:T(8,128)} fusion(f32[5,16384]{0,1:T(8,128)} %copy.94, s32[256]{0:T(256)S(1)} %compare_select_fusion.2, f32[256,5]{1,0:T(8,128)S(1)} %gather_fusion, pred[256]{0:T(512)(128)(4,1)S(1)} %compare_and_fusion), kind=kCustom, calls=%fused_computation.42 | custom fusion | flops 5120 | bytes 459264 | tf_op jit(solution)/shard_map/scatter-add | solution.py:92
  121.6 13.4 %scatter_fusion = f32[5,16384]{0,1:T(8,128)} fusion(f32[5,16384]{0,1:T(8,128)} %scatter_custom_fusion, s32[1024]{0:T(1024)S(1)} %bitcast.127, f32[1024,5]{1,0:T(8,128)S(1)} %copy.100), kind=kCustom, calls=%fused_computation.3 | custom fusion | flops 5120 | bytes 65536 | tf_op jit(solution)/shard_map/scatter-add | solution.py:105
  134.9 5.9 %copy.101 = f32[5,8,16,128]{3,2,1,0:T(8,128)} copy(f32[5,8,16,128]{0,3,2,1:T(8,128)} %bitcast.108) | data formatting | bytes 655360 | tf_op jit(solution)/shard_map/reshape | solution.py:106
  (48 shorter events, 6.1 us)
Async XLA Ops:
  0.0 23.6 %all-to-all-start = ((f32[40,16,128]{2,1,0:T(8,128)}), f32[40,16,128]{2,1,0:T(8,128)S(1)}, u32[]{:S(2)}, u32[]{:S(2)}) async-start(f32[40,16,128]{2,1,0:T(8,128)} %bitcast.125), calls=%async_computation | async-start | bytes 655360 | tf_op jit(solution)/shard_map/all_to_all | solution.py:67
  27.2 11.9 %copy-start.2 = (s32[256]{0:T(256)S(1)}, s32[256]{0:T(256)}, u32[]{:S(2)}) copy-start(s32[256]{0:T(256)} %param.9) | copy-start | bytes 3076
  27.3 11.9 %copy-start.3 = (s32[256]{0:T(256)S(1)}, s32[256]{0:T(256)}, u32[]{:S(2)}) copy-start(s32[256]{0:T(256)} %param.11) | copy-start | bytes 3076
  27.3 11.9 %copy-start.1 = (f32[3,5,5]{2,0,1:T(4,128)S(1)}, f32[3,5,5]{2,0,1:T(4,128)}, u32[]{:S(2)}) copy-start(f32[3,5,5]{2,0,1:T(4,128)} %param.8) | copy-start | bytes 904
  27.3 11.9 %copy-start = (f32[3,8,16,128]{3,2,1,0:T(8,128)S(1)}, f32[3,8,16,128]{3,2,1,0:T(8,128)}, u32[]{:S(2)}) copy-start(f32[3,8,16,128]{3,2,1,0:T(8,128)} %param.7) | copy-start | bytes 589828
  35.7 15.3 %all-to-all-start.1 = ((f32[8,1,10240]{2,1,0:T(1,128)}), f32[8,1,10240]{2,1,0:T(1,128)S(1)}, u32[]{:S(2)}, u32[]{:S(2)}) async-start(f32[8,1,10240]{2,1,0:T(1,128)} %reshape.129), calls=%async_computation.1 | async-start | bytes 655360 | tf_op jit(solution)/shard_map/all_to_all | solution.py:75
  59.0 36.1 %collective-permute-start = (f32[5,1,16,128]{3,2,1,0:T(8,128)S(1)}, f32[5,1,16,128]{3,2,1,0:T(8,128)S(1)}, u32[]{:S(2)}, u32[]{:S(2)}) collective-permute-start(f32[5,1,16,128]{3,2,1,0:T(8,128)S(1)} %get-tuple-element.12), channel_id=1, source_target_pairs={{16,0},{32,16},{48,32},{64,48},{80,64},{96,80},{112,96},{128,112},... | collective-permute-start | bytes 122888 | tf_op jit(solution)/shard_map/ppermute | solution.py:30
  61.4 33.6 %collective-permute-start.1 = (f32[5,1,16,128]{3,2,1,0:T(8,128)S(1)}, f32[5,1,16,128]{3,2,1,0:T(8,128)S(1)}, u32[]{:S(2)}, u32[]{:S(2)}) collective-permute-start(f32[5,1,16,128]{3,2,1,0:T(8,128)S(1)} %get-tuple-element.13), channel_id=1, source_target_pairs={{0,16},{16,32},{32,48},{48,64},{64,80},{80,96},{96,112},{112,128},... | collective-permute-start | bytes 122888 | tf_op jit(solution)/shard_map/ppermute | solution.py:29
  64.8 40.1 %collective-permute-start.4 = (f32[5,8,16,1]{3,2,1,0:T(8,128)S(1)}, f32[5,8,16,1]{3,2,1,0:T(8,128)S(1)}, u32[]{:S(2)}, u32[]{:S(2)}) collective-permute-start(f32[5,8,16,1]{3,2,1,0:T(8,128)S(1)} %get-tuple-element.10), channel_id=1, source_target_pairs={{2,0},{4,2},{6,4},{8,6},{10,8},{12,10},{14,12},{0,14},{3,1},{5,3},... | collective-permute-start | bytes 7688 | tf_op jit(solution)/shard_map/ppermute | solution.py:30
  66.8 38.1 %collective-permute-start.5 = (f32[5,8,16,1]{3,2,1,0:T(8,128)S(1)}, f32[5,8,16,1]{3,2,1,0:T(8,128)S(1)}, u32[]{:S(2)}, u32[]{:S(2)}) collective-permute-start(f32[5,8,16,1]{3,2,1,0:T(8,128)S(1)} %get-tuple-element.11), channel_id=1, source_target_pairs={{0,2},{2,4},{4,6},{6,8},{8,10},{10,12},{12,14},{14,0},{1,3},{3,5},... | collective-permute-start | bytes 7688 | tf_op jit(solution)/shard_map/ppermute | solution.py:29
  82.9 20.7 %all-to-all-start.2 = ((f32[32,1,192]{2,1,0:T(1,128)}), f32[32,1,192]{2,1,0:T(1,128)S(1)}, u32[]{:S(2)}, u32[]{:S(2)}) async-start(f32[32,1,192]{2,1,0:T(1,128)} %reshape.131), calls=%async_computation.2 | async-start | bytes 65536 | tf_op jit(solution)/shard_map/all_to_all | solution.py:101
  95.1 9.8 %collective-permute-start.2 = (f32[5,10,1,128]{3,2,1,0:T(1,128)S(1)}, f32[5,10,1,128]{3,2,1,0:T(1,128)S(1)}, u32[]{:S(2)}, u32[]{:S(2)}) collective-permute-start(f32[5,10,1,128]{3,2,1,0:T(1,128)S(1)} %get-tuple-element.7), channel_id=1, source_target_pairs={{1,0},{3,2},{5,4},{7,6},{9,8},{11,10},{13,12},{15,14},{17,16},{19,... | collective-permute-start | bytes 76808 | tf_op jit(solution)/shard_map/ppermute | solution.py:30
  96.4 8.6 %collective-permute-start.3 = (f32[5,10,1,128]{3,2,1,0:T(1,128)S(1)}, f32[5,10,1,128]{3,2,1,0:T(1,128)S(1)}, u32[]{:S(2)}, u32[]{:S(2)}) collective-permute-start(f32[5,10,1,128]{3,2,1,0:T(1,128)S(1)} %get-tuple-element.8), channel_id=1, source_target_pairs={{0,1},{2,3},{4,5},{6,7},{8,9},{10,11},{12,13},{14,15},{16,17},{18,... | collective-permute-start | bytes 76808 | tf_op jit(solution)/shard_map/ppermute | solution.py:29
where the time goes:
time: 142 us; the launch traced here: 141 us
  starting transfers between devices  42 us (30%)
  local copies, waits for them, and re-layouts  37.4 us (26%)
  other arithmetic  27.9 us (20%)
  waiting for transfers between devices  25.6 us (18%)
  matrix products  7.59 us (5%)
    scatter-add x1, other arithmetic, shards(): flat_grad.at[:, received[fields].astype(jnp.int32)].add(received[:fields])  13.4 us
    all_to_all x1, starting transfers between devices, shards(): lax.all_to_all(outbox.reshape(fields + 1, owners, capacity), 'gx', split_...  12.1 us
    all_to_all x1, waiting for transfers between devices, shards(): lax.all_to_all(smooth, 'az', split_axis=2, concat_axis=0, tiled=True)  11.7 us
    ppermute x3, starting transfers between devices, with_halo(): before = lax.ppermute(last, axis, up)  10.5 us
    all_to_all x1, starting transfers between devices, shards(): lax.all_to_all(grouped, 'az', split_axis=0, concat_axis=2, tiled=True)  10.3 us
    all_to_all x1, waiting for transfers between devices, shards(): lax.all_to_all(grouped, 'az', split_axis=0, concat_axis=2, tiled=True)  9.65 us
    scatter-add x1, other arithmetic, shards(): flat_grad = flat_grad.at[:, target_cell].add(-source)  8.45 us
    unnamed x12, local copies, waits for them, and re-layouts  7.75 us
  transfers between devices with their start and end apart: 9, of which 3 were waited for; matrix products, arithmetic and copies ran while one was open for 12% of the time, Pallas kernels for 0%

commit v1 on v0

v1 whole, which is shorter than its diff:
```python
import jax
import jax.numpy as jnp
import numpy as np
from jax import lax
from jax.sharding import PartitionSpec as P

filter_alpha = 0.49
sat_gain = 0.5
pade_coeffs = [
    (193.0 + 126.0 * filter_alpha) / 256.0,
    (105.0 + 302.0 * filter_alpha) / 256.0,
    15.0 * (2.0 * filter_alpha - 1.0) / 64.0,
    45.0 * (1.0 - 2.0 * filter_alpha) / 512.0,
    5.0 * (2.0 * filter_alpha - 1.0) / 256.0,
    (1.0 - 2.0 * filter_alpha) / 512.0,
]
HI = lax.Precision.HIGHEST


def loop_weights(length):
    wave = np.arange(length // 2 + 1) * (2.0 * np.pi / length)
    numer = np.full(wave.shape, pade_coeffs[0])
    for order in range(1, 6):
        numer = numer + pade_coeffs[order] * np.cos(order * wave)
    denom = 1.0 + 2.0 * filter_alpha * np.cos(wave)
    return np.fft.irfft(numer / denom, n=length)


def block_tables(cells, length):
    w = loop_weights(length)
    c = np.arange(cells)[:, None]
    o = np.arange(cells)[None, :]
    tables = []
    for shift in (-1, 0, 1):
        base = o - c - shift * cells
        filt = w[base % length]
        diff = w[(base + 1) % length] - w[(base - 1) % length]
        tables.append(np.concatenate([filt, diff], axis=1).astype(np.float32))
    return tables


def neighbours(value, axis, wrap):
    size = lax.axis_size(axis)
    up = [(i, (i + 1) % size) for i in range(size if wrap else size - 1)]
    down = [(j, i) for i, j in up]
    return up, down


def shards(adjoint, coeff, flux, target_cell, donor_owner, donor_cell):
    fields, rows_x, rows_r, cells_a = adjoint.shape
    loop_span = cells_a * lax.axis_size("az")
    rows = rows_x * rows_r
    tables = block_tables(cells_a, loop_span)

    up, down = neighbours(adjoint, "az", True)
    left = lax.ppermute(adjoint, "az", up)
    right = lax.ppermute(adjoint, "az", down)
    both = jnp.zeros((fields, rows_x, rows_r, 2 * cells_a), jnp.float32)
    for block, table in zip((left, adjoint, right), tables):
        both = both + jnp.einsum("fxra,ao->fxro", block, jnp.asarray(table), precision=HI)
    filtered = both[..., :cells_a]
    along_a = both[..., cells_a:]

    up_x, down_x = neighbours(filtered, "gx", False)
    before_x = lax.ppermute(filtered[:, -1:], "gx", up_x)
    after_x = lax.ppermute(filtered[:, :1], "gx", down_x)
    up_r, down_r = neighbours(filtered, "row", False)
    before_r = lax.ppermute(filtered[:, :, -1:], "row", up_r)
    after_r = lax.ppermute(filtered[:, :, :1], "row", down_r)
    along_x = jnp.concatenate([filtered[:, 1:], after_x], axis=1) - jnp.concatenate(
        [before_x, filtered[:, :-1]], axis=1
    )
    along_r = jnp.concatenate([filtered[:, :, 1:], after_r], axis=2) - jnp.concatenate(
        [before_r, filtered[:, :, :-1]], axis=2
    )
    gradient = filtered
    for direction, change in enumerate((along_x, along_r, along_a)):
        mixing = jnp.einsum("fg,fxra->gxra", flux[direction], change, precision=HI)
        gradient = gradient + coeff[direction][None] * mixing

    row_ids = jnp.arange(rows, dtype=jnp.int32)
    lane_ids = jnp.arange(cells_a, dtype=jnp.int32)
    t_rows = (target_cell[:, None] // cells_a == row_ids[None, :]).astype(jnp.float32)
    t_lanes = (target_cell[:, None] % cells_a == lane_ids[None, :]).astype(jnp.float32)
    flat = filtered.reshape(fields, rows, cells_a)
    picked = jnp.einsum("tk,fka->fta", t_rows, flat, precision=HI)
    source = sat_gain * jnp.sum(picked * t_lanes[None], axis=2)

    owner_rows = donor_owner[:, 0]
    owners = lax.axis_size("gx")
    capacity = target_cell.shape[0] // 8
    onehot = (owner_rows[:, None] == jnp.arange(owners, dtype=jnp.int32)[None, :]).astype(jnp.int32)
    slot_rank = jnp.sum(onehot * (jnp.cumsum(onehot, axis=0) - 1), axis=1)
    slot_place = owner_rows * capacity + slot_rank
    packed = jnp.concatenate([source, donor_cell.astype(jnp.float32)[None, :]], axis=0)
    slots = (slot_place[:, None] == jnp.arange(owners * capacity, dtype=jnp.int32)[None, :]).astype(
        jnp.float32
    )
    outbox = jnp.einsum("pt,ts->ps", packed, slots, precision=HI)
    received = lax.all_to_all(
        outbox.reshape(fields + 1, owners, capacity), "gx", split_axis=1, concat_axis=1, tiled=True
    )
    received = received.reshape(fields + 1, owners * capacity)
    got_cell = received[fields].astype(jnp.int32)
    d_rows = (got_cell[:, None] // cells_a == row_ids[None, :]).astype(jnp.float32)
    d_lanes = (got_cell[:, None] % cells_a == lane_ids[None, :]).astype(jnp.float32)

    all_rows = jnp.concatenate([t_rows, d_rows], axis=0)
    all_lanes = jnp.concatenate([t_lanes, d_lanes], axis=0)
    amounts = jnp.concatenate([-source, received[:fields]], axis=1)
    spread = amounts[:, :, None] * all_lanes[None]
    update = jnp.einsum("nk,fna->fka", all_rows, spread, precision=HI)
    return gradient + update.reshape(adjoint.shape)


def solution(mesh):
    return jax.shard_map(
        shards,
        mesh=mesh,
        in_specs=(
            P(None, "gx", "row", "az"),
            P(None, "gx", "row", "az"),
            P(),
            P(("gx", "az", "row")),
            P(("gx", "az", "row"), None),
            P(("gx", "az", "row")),
        ),
        out_specs=P(None, "gx", "row", "az"),
        check_vma=False,
    )
```

time: 142 us -> 57.6 us (0.41)
  the two profiles are of different devices: /device:TPU:2 before, /device:TPU:31 now
where the time goes in v1:
time: 57.6 us; the launch traced here: 57.3 us
  starting transfers between devices  36.8 us (64%)
  matrix products  8.02 us (14%)
  waiting for transfers between devices  6.98 us (12%)
  other arithmetic  2.98 us (5%)
  local copies, waits for them, and re-layouts  2.17 us (4%)
    ppermute x1, starting transfers between devices, shards(): right = lax.ppermute(adjoint, 'az', down)  10.8 us
    all_to_all x1, starting transfers between devices, shards(): lax.all_to_all(outbox.reshape(fields + 1, owners, capacity), 'gx', split_...  9.3 us
    ppermute x1, starting transfers between devices, shards(): before_x = lax.ppermute(filtered[:, -1:], 'gx', up_x)  6.12 us
    ppermute x1, starting transfers between devices, shards(): after_r = lax.ppermute(filtered[:, :, :1], 'row', down_r)  4.89 us
    ppermute x1, waiting for transfers between devices, shards(): left = lax.ppermute(adjoint, 'az', up)  4.22 us
    dot_general x3, matrix products, shards(): jnp.einsum('fxra,ao->fxro', block, jnp.asarray(table), precision=HI)  3.13 us
    ppermute x1, starting transfers between devices, shards(): after_x = lax.ppermute(filtered[:, :1], 'gx', down_x)  2.48 us
    dot_general x3, matrix products, shards(): mixing = jnp.einsum('fg,fxra->gxra', flux[direction], change, precision=HI)  2.27 us
  transfers between devices with their start and end apart: 7, of which 3 were waited for; matrix products, arithmetic and copies ran while one was open for 10% of the time, Pallas kernels for 0%

profile of v1, /device:TPU:31, one launch (start us, length us, event | category | flops | bytes accessed | tf_op | source)
XLA Modules:
  0.0 57.3 jit_solution(17458834530357108749)
XLA Ops:
  0.0 10.8 %collective-permute-start.1 = (f32[5,8,16,128]{3,2,1,0:T(8,128)}, f32[5,8,16,128]{3,2,1,0:T(8,128)S(1)}, u32[]{:S(2)}, u32[]{:S(2)}) collective-permute-start(f32[5,8,16,128]{3,2,1,0:T(8,128)} %param.9), channel_id=1, source_target_pairs={{2,0},{4,2},{6,4},{8,6},{10,8},{12,10},{14,12},{0,14},{3,1},{5,3},... | collective-permute-start | bytes 983048 | tf_op jit(solution)/shard_map/ppermute | solution.py:57
  10.8 1.9 %collective-permute-start = (f32[5,8,16,128]{3,2,1,0:T(8,128)}, f32[5,8,16,128]{3,2,1,0:T(8,128)S(1)}, u32[]{:S(2)}, u32[]{:S(2)}) collective-permute-start(f32[5,8,16,128]{3,2,1,0:T(8,128)} %param.9), channel_id=1, source_target_pairs={{0,2},{2,4},{4,6},{6,8},{8,10},{10,12},{12,14},{14,0},{1,3},{3,5},... | collective-permute-start | bytes 983048 | tf_op jit(solution)/shard_map/ppermute | solution.py:56
  12.8 1.7 %fusion.40 = f32[256,5,8,16]{0,3,2,1:T(8,128)S(1)} fusion(f32[128,256,1,1]{1,0,3,2:T(8,128)} %constant.73, f32[5,8,16,128]{3,2,1,0:T(8,128)} %param.9), kind=kOutput, calls=%fused_computation.86 | convolution fusion | flops 251658240 | bytes 1114112 | tf_op jit(solution)/shard_map/fxra,ao->fxro/dot_general | solution.py:60
  14.6 0.6 %reduce-window.6 = s32[32,2,128]{2,0,1:T(8,128)S(1)} reduce-window(s32[32,2,128]{2,0,1:T(8,128)S(1)} %fusion.24, s32[]{:T(128)} %constant.56.clone.1), window={size=1x1x128 pad=0_0x0_0x127_0}, to_apply=%region_1.2 | reduce-window | flops 1040384 | bytes 65540 | tf_op jit(solution)/shard_map/reduce-window
  15.2 0.2 slice_reduce_fusion
  15.5 0.1 fusion.23
  15.6 0.1 copy.75
  15.7 1.8 %collective-permute-done.1 = f32[5,8,16,128]{3,2,1,0:T(8,128)S(1)} collective-permute-done((f32[5,8,16,128]{3,2,1,0:T(8,128)}, f32[5,8,16,128]{3,2,1,0:T(8,128)S(1)}, u32[]{:S(2)}, u32[]{:S(2)}) %collective-permute-start.1) | collective-permute-done | bytes 327712 | tf_op jit(solution)/shard_map/ppermute | solution.py:57
  17.5 0.7 %fusion.41 = f32[256,5,8,16]{0,3,2,1:T(8,128)S(1)} fusion(f32[128,256,1,1]{1,0,3,2:T(8,128)S(1)} %copy-done.6, f32[5,8,16,128]{3,2,1,0:T(8,128)S(1)} %collective-permute-done.1), kind=kOutput, calls=%fused_computation.87 | convolution fusion | flops 251658240 | bytes 1114112 | tf_op jit(solution)/shard_map/fxra,ao->fxro/dot_general | solution.py:60
  18.2 4.2 %collective-permute-done = f32[5,8,16,128]{3,2,1,0:T(8,128)S(1)} collective-permute-done((f32[5,8,16,128]{3,2,1,0:T(8,128)}, f32[5,8,16,128]{3,2,1,0:T(8,128)S(1)}, u32[]{:S(2)}, u32[]{:S(2)}) %collective-permute-start) | collective-permute-done | bytes 327712 | tf_op jit(solution)/shard_map/ppermute | solution.py:56
  22.4 0.7 %fusion.6 = f32[5,8,16,256]{3,2,1,0:T(8,128)S(1)} fusion(f32[256,5,8,16]{0,3,2,1:T(8,128)S(1)} %fusion.41, f32[256,5,8,16]{0,3,2,1:T(8,128)S(1)} %fusion.40, f32[128,256,1,1]{1,0,3,2:T(8,128)S(1)} %copy-done.1, f32[5,8,16,128]{3,2,1,0:T(8,128)S(1)} %collective-permute-done), kind=kOutput, calls=%fused_computation.8 | convolution fusion | flops 251985920 | bytes 2424832 | tf_op jit(solution)/shard_map/fxra,ao->fxro/dot_general | solution.py:60
  23.3 0.5 fusion.7
  23.8 0.5 fusion.8
  24.3 0.1 reshape.139
  24.5 0.7 %reshape.157 = f32[32,1,192]{2,1,0:T(1,128)} reshape(f32[32,6,32]{2,1,0:T(8,128)S(1)} %bitcast.95) | data formatting | bytes 49152
  25.2 9.3 %all-to-all-start = ((f32[32,1,192]{2,1,0:T(1,128)}), f32[32,1,192]{2,1,0:T(1,128)S(1)}, u32[]{:S(2)}, u32[]{:S(2)}) async-start(f32[32,1,192]{2,1,0:T(1,128)} %reshape.157), calls=%async_computation | async-start | bytes 65536 | tf_op jit(solution)/shard_map/all_to_all | solution.py:100
  34.5 2.5 %collective-permute-start.2 = (f32[5,1,16,128]{3,2,1,0:T(8,128)S(1)}, f32[5,1,16,128]{3,2,1,0:T(8,128)S(1)}, u32[]{:S(2)}, u32[]{:S(2)}) collective-permute-start(f32[5,1,16,128]{3,2,1,0:T(8,128)S(1)} %get-tuple-element.6), channel_id=1, source_target_pairs={{16,0},{32,16},{48,32},{64,48},{80,64},{96,80},{112,96},{128,112},... | collective-permute-start | bytes 122888 | tf_op jit(solution)/shard_map/ppermute | solution.py:66
  37.0 6.1 %collective-permute-start.3 = (f32[5,1,16,128]{3,2,1,0:T(8,128)S(1)}, f32[5,1,16,128]{3,2,1,0:T(8,128)S(1)}, u32[]{:S(2)}, u32[]{:S(2)}) collective-permute-start(f32[5,1,16,128]{3,2,1,0:T(8,128)S(1)} %get-tuple-element.5), channel_id=1, source_target_pairs={{0,16},{16,32},{32,48},{48,64},{64,80},{80,96},{96,112},{112,128},... | collective-permute-start | bytes 122888 | tf_op jit(solution)/shard_map/ppermute | solution.py:65
  43.1 4.9 %collective-permute-start.4 = (f32[5,8,1,128]{3,2,1,0:T(1,128)S(1)}, f32[5,8,1,128]{3,2,1,0:T(1,128)S(1)}, u32[]{:S(2)}, u32[]{:S(2)}) collective-permute-start(f32[5,8,1,128]{3,2,1,0:T(1,128)S(1)} %get-tuple-element.10), channel_id=1, source_target_pairs={{1,0},{3,2},{5,4},{7,6},{9,8},{11,10},{13,12},{15,14},{17,16},{19,... | collective-permute-start | bytes 61448 | tf_op jit(solution)/shard_map/ppermute | solution.py:69
  48.0 1.3 %collective-permute-start.5 = (f32[5,8,1,128]{3,2,1,0:T(1,128)S(1)}, f32[5,8,1,128]{3,2,1,0:T(1,128)S(1)}, u32[]{:S(2)}, u32[]{:S(2)}) collective-permute-start(f32[5,8,1,128]{3,2,1,0:T(1,128)S(1)} %get-tuple-element.9), channel_id=1, source_target_pairs={{0,1},{2,3},{4,5},{6,7},{8,9},{10,11},{12,13},{14,15},{16,17},{18,... | collective-permute-start | bytes 61448 | tf_op jit(solution)/shard_map/ppermute | solution.py:68
  49.3 0.8 %fusion.11 = f32[8,16,128,5]{2,3,1,0:T(8,128)S(1)} fusion(f32[5,8,16,128]{3,2,1,0:T(8,128)S(1)} %get-tuple-element.13, f32[1,5,5]{2,0,1:T(1,128)S(1)} %get-tuple-element.20), kind=kOutput, calls=%fused_computation.16 | convolution fusion | flops 4915200 | bytes 655460 | tf_op jit(solution)/shard_map/fg,fxra->gxra/dot_general | solution.py:78
  50.1 1.0 %collective-permute-done.5 = f32[5,8,1,128]{3,2,1,0:T(1,128)S(1)} collective-permute-done((f32[5,8,1,128]{3,2,1,0:T(1,128)S(1)}, f32[5,8,1,128]{3,2,1,0:T(1,128)S(1)}, u32[]{:S(2)}, u32[]{:S(2)}) %collective-permute-start.5) | collective-permute-done | bytes 20512 | tf_op jit(solution)/shard_map/ppermute | solution.py:68
  51.1 0.1 maximum_subtract_fusion.1
  51.2 0.8 %fusion.13 = f32[8,16,128,5]{2,3,1,0:T(8,128)S(1)} fusion(f32[5,8,16,128]{3,2,1,0:T(8,128)S(1)} %maximum_subtract_fusion.1, f32[1,5,5]{2,0,1:T(1,128)S(1)} %get-tuple-element.19), kind=kOutput, calls=%fused_computation.18 | convolution fusion | flops 4915200 | bytes 655460 | tf_op jit(solution)/shard_map/fg,fxra->gxra/dot_general | solution.py:78
  52.0 0.8 %fusion.15 = f32[8,16,128,5]{2,3,1,0:T(8,128)S(1)} fusion(f32[5,8,16,128]{3,2,1,0:T(8,128)S(1)} %maximum_subtract_fusion, f32[1,5,5]{2,0,1:T(1,128)S(1)} %get-tuple-element.18), kind=kOutput, calls=%fused_computation.20 | convolution fusion | flops 4915200 | bytes 655460 | tf_op jit(solution)/shard_map/fg,fxra->gxra/dot_general | solution.py:78
  52.8 0.5 broadcast.171
  53.3 0.7 %reduce.6 = f32[32,192]{1,0:T(8,128)S(1)} reduce(f32[32,1,192]{2,1,0:T(1,128)S(1)} %all-to-all-done, f32[]{:T(128)} %broadcast.171), dimensions={1}, to_apply=%all_to_all.3.reduce_sub_computation | reduce | bytes 49156 | tf_op jit(solution)/shard_map/all_to_all | solution.py:100
  54.1 0.1 reshape.158
  54.2 0.1 slice.91
  54.4 0.2 fusion.18
  54.8 1.6 %fusion = f32[5,128,128]{1,2,0:T(8,128)S(1)} fusion(f32[1280,128]{1,0:T(8,128)S(1)} %pad_maximum_fusion, f32[5,1280]{1,0:T(8,128)S(1)} %pad_maximum_fusion.1, pred[1024,128]{0,1:T(32,128)(4,1)S(1)} %iota_compare_fusion.2, pred[256,128]{0,1:T(32,128)(4,1)S(1)} %get-tuple-element.27), kind=kOutput, calls=%fused_computation | convolution fusion | flops 1259274240 | bytes 1172480 | tf_op jit(solution)/shard_map/nk,fna->fka/dot_general | solution.py:112
  56.4 0.9 %fusion.19 = f32[5,8,16,128]{3,2,1,0:T(8,128)} fusion(f32[5,8,16,128]{3,2,1,0:T(8,128)S(1)} %bitcast.96, f32[8,16,128,5]{2,3,1,0:T(8,128)S(1)} %fusion.11, f32[8,16,128,5]{2,3,1,0:T(8,128)S(1)} %fusion.13, f32[8,16,128,5]{2,3,1,0:T(8,128)S(1)} %fusion.15, f32[8,16,128]{2,1,0:T(8,128)S(1)} %get-tuple-element.16, f32[8,16,128]{2,1,0:T(8,128)S(1)} %get-tuple-element.17, ...), kind=kLoop, calls=%fused_computation.29 | loop fusion | flops 573440 | bytes 2162688 | tf_op jit(solution)/shard_map/add | solution.py:113
  (42 shorter events, 0.8 us)
Async XLA Ops:
  0.0 14.5 %copy-start.4 = (s32[256]{0:T(256)S(1)}, s32[256]{0:T(256)}, u32[]{:S(2)}) copy-start(s32[256]{0:T(256)} %param.12) | copy-start | bytes 3076
  0.0 14.5 %copy-start.2 = (s32[256,1]{0,1:T(1,128)S(1)}, s32[256,1]{0,1:T(1,128)}, u32[]{:S(2)}) copy-start(s32[256,1]{0,1:T(1,128)} %param.13) | copy-start | bytes 3076
  0.0 15.4 %copy-start.3 = (f32[3,5,5]{2,0,1:T(4,128)S(1)}, f32[3,5,5]{2,0,1:T(4,128)}, u32[]{:S(2)}) copy-start(f32[3,5,5]{2,0,1:T(4,128)} %param.11) | copy-start | bytes 904
  0.0 15.4 %copy-start = (f32[3,8,16,128]{3,2,1,0:T(8,128)S(1)}, f32[3,8,16,128]{3,2,1,0:T(8,128)}, u32[]{:S(2)}) copy-start(f32[3,8,16,128]{3,2,1,0:T(8,128)} %param.10) | copy-start | bytes 589828
  0.0 17.5 %collective-permute-start.1 = (f32[5,8,16,128]{3,2,1,0:T(8,128)}, f32[5,8,16,128]{3,2,1,0:T(8,128)S(1)}, u32[]{:S(2)}, u32[]{:S(2)}) collective-permute-start(f32[5,8,16,128]{3,2,1,0:T(8,128)} %param.9), channel_id=1, source_target_pairs={{2,0},{4,2},{6,4},{8,6},{10,8},{12,10},{14,12},{0,14},{3,1},{5,3},... | collective-permute-start | bytes 983048 | tf_op jit(solution)/shard_map/ppermute | solution.py:57
  10.8 11.6 %collective-permute-start = (f32[5,8,16,128]{3,2,1,0:T(8,128)}, f32[5,8,16,128]{3,2,1,0:T(8,128)S(1)}, u32[]{:S(2)}, u32[]{:S(2)}) collective-permute-start(f32[5,8,16,128]{3,2,1,0:T(8,128)} %param.9), channel_id=1, source_target_pairs={{0,2},{2,4},{4,6},{6,8},{8,10},{10,12},{12,14},{14,0},{1,3},{3,5},... | collective-permute-start | bytes 983048 | tf_op jit(solution)/shard_map/ppermute | solution.py:56
  14.5 1.1 %copy-start.5 = (s32[256]{0:T(256)S(1)}, s32[256]{0:T(256)}, u32[]{:S(2)}) copy-start(s32[256]{0:T(256)} %param.14) | copy-start | bytes 3076
  14.5 3.0 %copy-start.6 = (f32[128,256,1,1]{1,0,3,2:T(8,128)S(1)}, f32[128,256,1,1]{1,0,3,2:T(8,128)}, u32[]{:S(2)}) copy-start(f32[128,256,1,1]{1,0,3,2:T(8,128)} %constant.74) | copy-start | bytes 393220
  15.7 6.7 %copy-start.1 = (f32[128,256,1,1]{1,0,3,2:T(8,128)S(1)}, f32[128,256,1,1]{1,0,3,2:T(8,128)}, u32[]{:S(2)}) copy-start(f32[128,256,1,1]{1,0,3,2:T(8,128)} %constant.72) | copy-start | bytes 393220
  25.2 27.6 %all-to-all-start = ((f32[32,1,192]{2,1,0:T(1,128)}), f32[32,1,192]{2,1,0:T(1,128)S(1)}, u32[]{:S(2)}, u32[]{:S(2)}) async-start(f32[32,1,192]{2,1,0:T(1,128)} %reshape.157), calls=%async_computation | async-start | bytes 65536 | tf_op jit(solution)/shard_map/all_to_all | solution.py:100
  34.5 17.5 %collective-permute-start.2 = (f32[5,1,16,128]{3,2,1,0:T(8,128)S(1)}, f32[5,1,16,128]{3,2,1,0:T(8,128)S(1)}, u32[]{:S(2)}, u32[]{:S(2)}) collective-permute-start(f32[5,1,16,128]{3,2,1,0:T(8,128)S(1)} %get-tuple-element.6), channel_id=1, source_target_pairs={{16,0},{32,16},{48,32},{64,48},{80,64},{96,80},{112,96},{128,112},... | collective-permute-start | bytes 122888 | tf_op jit(solution)/shard_map/ppermute | solution.py:66
  37.0 15.0 %collective-permute-start.3 = (f32[5,1,16,128]{3,2,1,0:T(8,128)S(1)}, f32[5,1,16,128]{3,2,1,0:T(8,128)S(1)}, u32[]{:S(2)}, u32[]{:S(2)}) collective-permute-start(f32[5,1,16,128]{3,2,1,0:T(8,128)S(1)} %get-tuple-element.5), channel_id=1, source_target_pairs={{0,16},{16,32},{32,48},{48,64},{64,80},{80,96},{96,112},{112,128},... | collective-permute-start | bytes 122888 | tf_op jit(solution)/shard_map/ppermute | solution.py:65
  43.1 7.0 %collective-permute-start.4 = (f32[5,8,1,128]{3,2,1,0:T(1,128)S(1)}, f32[5,8,1,128]{3,2,1,0:T(1,128)S(1)}, u32[]{:S(2)}, u32[]{:S(2)}) collective-permute-start(f32[5,8,1,128]{3,2,1,0:T(1,128)S(1)} %get-tuple-element.10), channel_id=1, source_target_pairs={{1,0},{3,2},{5,4},{7,6},{9,8},{11,10},{13,12},{15,14},{17,16},{19,... | collective-permute-start | bytes 61448 | tf_op jit(solution)/shard_map/ppermute | solution.py:69
  48.0 3.1 %collective-permute-start.5 = (f32[5,8,1,128]{3,2,1,0:T(1,128)S(1)}, f32[5,8,1,128]{3,2,1,0:T(1,128)S(1)}, u32[]{:S(2)}, u32[]{:S(2)}) collective-permute-start(f32[5,8,1,128]{3,2,1,0:T(1,128)S(1)} %get-tuple-element.9), channel_id=1, source_target_pairs={{0,1},{2,3},{4,5},{6,7},{8,9},{10,11},{12,13},{14,15},{16,17},{18,... | collective-permute-start | bytes 61448 | tf_op jit(solution)/shard_map/ppermute | solution.py:68

commit v2 on v1

--- a/solution.py
+++ b/solution.py
@@ -17,26 +17,56 @@
 HI = lax.Precision.HIGHEST
 
 
-def loop_weights(length):
-    wave = np.arange(length // 2 + 1) * (2.0 * np.pi / length)
-    numer = np.full(wave.shape, pade_coeffs[0])
-    for order in range(1, 6):
-        numer = numer + pade_coeffs[order] * np.cos(order * wave)
-    denom = 1.0 + 2.0 * filter_alpha * np.cos(wave)
-    return np.fft.irfft(numer / denom, n=length)
+root_value = (-1.0 + (1.0 - 4.0 * filter_alpha * filter_alpha) ** 0.5) / (2.0 * filter_alpha)
+green_scale = 1.0 / (1.0 + 2.0 * filter_alpha * root_value)
+EDGE = 7
 
 
-def block_tables(cells, length):
-    w = loop_weights(length)
+def stencil_weight(shift):
+    return pade_coeffs[0] if shift == 0 else 0.5 * pade_coeffs[abs(shift)]
+
+
+def loop_weight(offset, length):
+    total = np.zeros(np.shape(offset))
+    for shift in range(-5, 6):
+        n = np.mod(offset - shift, length)
+        images = root_value ** n + root_value ** (length - n)
+        total = total + stencil_weight(shift) * green_scale * images / (1.0 - root_value**length)
+    return total
+
+
+def halo_tables(cells, length):
+    r = root_value
+    tail = green_scale / (1.0 - r**length) * sum(stencil_weight(s) * r ** (-s) for s in range(-5, 6))
     c = np.arange(cells)[:, None]
     o = np.arange(cells)[None, :]
-    tables = []
-    for shift in (-1, 0, 1):
-        base = o - c - shift * cells
-        filt = w[base % length]
-        diff = w[(base + 1) % length] - w[(base - 1) % length]
-        tables.append(np.concatenate([filt, diff], axis=1).astype(np.float32))
-    return tables
+
+    def both(distance):
+        return np.concatenate(
+            [loop_weight(distance, length), loop_weight(distance + 1, length) - loop_weight(distance - 1, length)],
+            axis=-1,
+        )
+
+    own = both(o - c)
+    k = np.arange(EDGE)[:, None]
+    ov = np.arange(cells)[None, :]
+    send_right = np.zeros((cells, EDGE + 1))
+    send_right[cells - EDGE + np.arange(EDGE), np.arange(EDGE)] = 1.0
+    send_right[: cells - EDGE, EDGE] = r ** (cells - np.arange(cells - EDGE))
+    from_left = np.concatenate(
+        [both(ov + cells - (cells - EDGE + k)),
+         np.concatenate([tail * r**ov, tail * r**ov * (r - 1.0 / r)], axis=-1)],
+        axis=0,
+    )
+    send_left = np.zeros((cells, EDGE + 1))
+    send_left[np.arange(EDGE), np.arange(EDGE)] = 1.0
+    send_left[EDGE:, EDGE] = r ** (np.arange(EDGE, cells) + 1.0)
+    from_right = np.concatenate(
+        [both(ov - cells - k),
+         np.concatenate([tail * r ** (cells - 1 - ov), tail * r ** (cells - 1 - ov) * (1.0 / r - r)], axis=-1)],
+        axis=0,
+    )
+    return [np.asarray(t, np.float32) for t in (own, send_right, from_left, send_left, from_right)]
 
 
 def neighbours(value, axis, wrap):
@@ -50,14 +80,18 @@
     fields, rows_x, rows_r, cells_a = adjoint.shape
     loop_span = cells_a * lax.axis_size("az")
     rows = rows_x * rows_r
-    tables = block_tables(cells_a, loop_span)
+    own_t, send_right_t, from_left_t, send_left_t, from_right_t = halo_tables(cells_a, loop_span)
+    lines = adjoint.reshape(fields * rows, cells_a)
 
     up, down = neighbours(adjoint, "az", True)
-    left = lax.ppermute(adjoint, "az", up)
-    right = lax.ppermute(adjoint, "az", down)
-    both = jnp.zeros((fields, rows_x, rows_r, 2 * cells_a), jnp.float32)
-    for block, table in zip((left, adjoint, right), tables):
-        both = both + jnp.einsum("fxra,ao->fxro", block, jnp.asarray(table), precision=HI)
+    to_right = jnp.einsum("lc,ck->kl", lines, jnp.asarray(send_right_t), precision=HI)
+    to_left = jnp.einsum("lc,ck->kl", lines, jnp.asarray(send_left_t), precision=HI)
+    from_left = lax.ppermute(to_right, "az", up)
+    from_right = lax.ppermute(to_left, "az", down)
+    both = jnp.einsum("lc,co->lo", lines, jnp.asarray(own_t), precision=HI)
+    both = both + jnp.einsum("kl,ko->lo", from_left, jnp.asarray(from_left_t), precision=HI)
+    both = both + jnp.einsum("kl,ko->lo", from_right, jnp.asarray(from_right_t), precision=HI)
+    both = both.reshape(fields, rows_x, rows_r, 2 * cells_a)
     filtered = both[..., :cells_a]
     along_a = both[..., cells_a:]
 

time: 57.6 us -> 62 us (1.076)
  the two profiles are of different devices: /device:TPU:31 before, /device:TPU:1 now
where the time goes in v2:
time: 62 us; the launch traced here: 61.5 us
  starting transfers between devices  35.5 us (57%)
  matrix products  9.95 us (16%)
  waiting for transfers between devices  6.21 us (10%)
  local copies, waits for them, and re-layouts  6.14 us (10%)
  other arithmetic  3.21 us (5%)
    ppermute x1, starting transfers between devices, shards(): from_right = lax.ppermute(to_left, 'az', down)  11.5 us
    all_to_all x1, starting transfers between devices, shards(): lax.all_to_all(outbox.reshape(fields + 1, owners, capacity), 'gx', split_...  11.5 us
    all_to_all x1, waiting for transfers between devices, shards(): lax.all_to_all(outbox.reshape(fields + 1, owners, capacity), 'gx', split_...  6.19 us
    ppermute x1, starting transfers between devices, shards(): before_x = lax.ppermute(filtered[:, -1:], 'gx', up_x)  3.99 us
    ppermute x1, starting transfers between devices, shards(): after_r = lax.ppermute(filtered[:, :, :1], 'row', down_r)  3.82 us
    dot_general x3, matrix products, shards(): mixing = jnp.einsum('fg,fxra->gxra', flux[direction], change, precision=HI)  2.49 us
    unnamed x28, local copies, waits for them, and re-layouts  2.41 us
    ppermute x1, starting transfers between devices, shards(): from_left = lax.ppermute(to_right, 'az', up)  2.05 us
  transfers between devices with their start and end apart: 7, of which 1 were waited for; matrix products, arithmetic and copies ran while one was open for 15% of the time, Pallas kernels for 0%

profile of v2, /device:TPU:1, one launch (start us, length us, event | category | flops | bytes accessed | tf_op | source)
XLA Modules:
  0.0 61.5 jit_solution(6169837053699434779)
XLA Ops:
  0.0 1.0 %copy-done = f32[5,8,16,128]{3,2,1,0:T(8,128)S(1)} copy-done((f32[5,8,16,128]{3,2,1,0:T(8,128)S(1)}, f32[5,8,16,128]{3,2,1,0:T(8,128)}, u32[]{:S(2)}) %copy-start) | copy-done | bytes 327704
  1.0 1.3 %fusion.45 = f32[8,640]{1,0:T(8,128)S(1)} fusion(f32[128,8]{1,0:T(8,128)} %constant.69.clone, f32[640,128]{1,0:T(8,128)S(1)} %bitcast.92), kind=kOutput, calls=%fused_computation.88 | convolution fusion | flops 7864320 | bytes 352256 | tf_op jit(solution)/shard_map/lc,ck->kl/dot_general | solution.py:88
  2.2 11.5 %collective-permute-start.1 = (f32[8,640]{1,0:T(8,128)S(1)}, f32[8,640]{1,0:T(8,128)S(1)}, u32[]{:S(2)}, u32[]{:S(2)}) collective-permute-start(f32[8,640]{1,0:T(8,128)S(1)} %fusion.45), channel_id=1, source_target_pairs={{2,0},{4,2},{6,4},{8,6},{10,8},{12,10},{14,12},{0,14},{3,1},{5,3},... | collective-permute-start | bytes 61448 | tf_op jit(solution)/shard_map/ppermute | solution.py:90
  13.8 1.3 %fusion.44 = f32[8,640]{1,0:T(8,128)S(1)} fusion(f32[128,8]{1,0:T(8,128)} %constant.68.clone, f32[640,128]{1,0:T(8,128)S(1)} %bitcast.91), kind=kOutput, calls=%fused_computation.87 | convolution fusion | flops 7864320 | bytes 352256 | tf_op jit(solution)/shard_map/lc,ck->kl/dot_general | solution.py:87
  15.1 2.1 %collective-permute-start = (f32[8,640]{1,0:T(8,128)S(1)}, f32[8,640]{1,0:T(8,128)S(1)}, u32[]{:S(2)}, u32[]{:S(2)}) collective-permute-start(f32[8,640]{1,0:T(8,128)S(1)} %fusion.44), channel_id=1, source_target_pairs={{0,2},{2,4},{4,6},{6,8},{8,10},{10,12},{12,14},{14,0},{1,3},{3,5},... | collective-permute-start | bytes 61448 | tf_op jit(solution)/shard_map/ppermute | solution.py:89
  17.2 0.9 %convolution_bitcast_fusion.1 = f32[640,256]{0,1:T(8,128)S(1)} fusion(f32[128,256]{1,0:T(8,128)S(1)} %copy-done.2, f32[640,128]{1,0:T(8,128)S(1)} %bitcast.90), kind=kOutput, calls=%fused_computation.8 | convolution fusion | flops 251658240 | bytes 1114112 | tf_op jit(solution)/shard_map/lc,co->lo/dot_general | solution.py:91
  18.1 0.6 fusion.43
  18.7 0.6 reduce-window.6
  19.7 0.6 multiply_add_fusion
  20.3 0.6 convert_element_type.35
  21.0 0.7 %fusion.46 = f32[640,256]{0,1:T(8,128)S(1)} fusion(f32[8,640]{1,0:T(8,128)S(1)} %collective-permute-done.1, f32[8,256]{1,0:T(8,128)S(1)} %copy-done.7), kind=kOutput, calls=%fused_computation.89 | convolution fusion | flops 15728640 | bytes 684032 | tf_op jit(solution)/shard_map/kl,ko->lo/dot_general | solution.py:93
  21.7 0.7 %fusion.4 = f32[640,256]{0,1:T(8,128)S(1)} fusion(f32[640,256]{0,1:T(8,128)S(1)} %fusion.46, f32[640,256]{0,1:T(8,128)S(1)} %convolution_bitcast_fusion.1, f32[8,640]{1,0:T(8,128)S(1)} %collective-permute-done, f32[8,256]{1,0:T(8,128)S(1)} %copy-done.6), kind=kOutput, calls=%fused_computation.5 | convolution fusion | flops 16056320 | bytes 1994752 | tf_op jit(solution)/shard_map/kl,ko->lo/dot_general | solution.py:92
  22.5 0.2 copy.76
  22.8 0.6 %fusion.39 = (f32[5,8,1,128]{3,2,1,0:T(1,128)S(1)}, f32[5,8,1,128]{3,2,1,0:T(1,128)}) fusion(f32[5,8,16,256]{3,2,1,0:T(8,128)S(1)} %bitcast.96), kind=kLoop, calls=%fused_computation.81 | loop fusion | bytes 81920 | tf_op jit(solution)/shard_map/slice | solution.py:102
  23.5 1.3 %collective-permute-start.2 = (f32[5,1,16,128]{3,2,1,0:T(8,128)S(1)}, f32[5,1,16,128]{3,2,1,0:T(8,128)S(1)}, u32[]{:S(2)}, u32[]{:S(2)}) collective-permute-start(f32[5,1,16,128]{3,2,1,0:T(8,128)S(1)} %get-tuple-element.12), channel_id=1, source_target_pairs={{16,0},{32,16},{48,32},{64,48},{80,64},{96,80},{112,96},{128,112},... | collective-permute-start | bytes 122888 | tf_op jit(solution)/shard_map/ppermute | solution.py:100
  24.8 4.0 %collective-permute-start.3 = (f32[5,1,16,128]{3,2,1,0:T(8,128)S(1)}, f32[5,1,16,128]{3,2,1,0:T(8,128)S(1)}, u32[]{:S(2)}, u32[]{:S(2)}) collective-permute-start(f32[5,1,16,128]{3,2,1,0:T(8,128)S(1)} %get-tuple-element.11), channel_id=1, source_target_pairs={{0,16},{16,32},{32,48},{48,64},{64,80},{80,96},{96,112},{112,128},... | collective-permute-start | bytes 122888 | tf_op jit(solution)/shard_map/ppermute | solution.py:99
  28.8 3.8 %collective-permute-start.4 = (f32[5,8,1,128]{3,2,1,0:T(1,128)}, f32[5,8,1,128]{3,2,1,0:T(1,128)S(1)}, u32[]{:S(2)}, u32[]{:S(2)}) collective-permute-start(f32[5,8,1,128]{3,2,1,0:T(1,128)} %get-tuple-element.8), channel_id=1, source_target_pairs={{1,0},{3,2},{5,4},{7,6},{9,8},{11,10},{13,12},{15,14},{17,16},{19,... | collective-permute-start | bytes 61448 | tf_op jit(solution)/shard_map/ppermute | solution.py:103
  32.6 1.3 %collective-permute-start.5 = (f32[5,8,1,128]{3,2,1,0:T(1,128)S(1)}, f32[5,8,1,128]{3,2,1,0:T(1,128)S(1)}, u32[]{:S(2)}, u32[]{:S(2)}) collective-permute-start(f32[5,8,1,128]{3,2,1,0:T(1,128)S(1)} %get-tuple-element.7), channel_id=1, source_target_pairs={{0,1},{2,3},{4,5},{6,7},{8,9},{10,11},{12,13},{14,15},{16,17},{18,... | collective-permute-start | bytes 61448 | tf_op jit(solution)/shard_map/ppermute | solution.py:102
  33.9 0.5 fusion.12
  34.5 0.5 fusion.16
  35.1 0.7 %reshape.162 = f32[32,1,192]{2,1,0:T(1,128)} reshape(f32[32,6,32]{2,1,0:T(8,128)S(1)} %bitcast.102) | data formatting | bytes 49152
  35.8 11.5 %all-to-all-start = ((f32[32,1,192]{2,1,0:T(1,128)}), f32[32,1,192]{2,1,0:T(1,128)S(1)}, u32[]{:S(2)}, u32[]{:S(2)}) async-start(f32[32,1,192]{2,1,0:T(1,128)} %reshape.162), calls=%async_computation | async-start | bytes 65536 | tf_op jit(solution)/shard_map/all_to_all | solution.py:134
  47.6 0.6 copy-done.4
  48.1 0.8 %fusion.11 = f32[5,8,16,128]{3,0,2,1:T(8,128)S(1)} fusion(f32[5,8,16,128]{3,2,1,0:T(8,128)S(1)} %maximum_subtract_fusion, f32[8,16,128]{2,1,0:T(8,128)S(1)} %get-tuple-element.16, f32[1,5,5]{2,0,1:T(1,128)S(1)} %copy-done.4), kind=kOutput, calls=%fused_computation.17 | convolution fusion | flops 4997120 | bytes 720996 | tf_op jit(solution)/shard_map/fg,fxra->gxra/dot_general | solution.py:112
  48.9 0.9 %fusion.10 = f32[5,8,16,128]{3,0,2,1:T(8,128)S(1)} fusion(f32[5,8,16,128]{3,0,2,1:T(8,128)S(1)} %fusion.11, f32[5,8,16,128]{3,2,1,0:T(8,128)S(1)} %get-tuple-element.6, f32[5,8,16,128]{3,2,1,0:T(8,128)S(1)} %maximum_subtract_fusion.1, f32[8,16,128]{2,1,0:T(8,128)S(1)} %get-tuple-element.17, f32[1,5,5]{2,0,1:T(1,128)S(1)} %copy-done.3), kind=kOutput, calls=%fused_computation.15 | convolution fusion | flops 5160960 | bytes 1376356 | tf_op jit(solution)/shard_map/fg,fxra->gxra/dot_general | solution.py:112
  49.9 6.2 %all-to-all-done = f32[32,1,192]{2,1,0:T(1,128)S(1)} async-done(((f32[32,1,192]{2,1,0:T(1,128)}), f32[32,1,192]{2,1,0:T(1,128)S(1)}, u32[]{:S(2)}, u32[]{:S(2)}) %all-to-all-start) | async-done | bytes 24608 | tf_op jit(solution)/shard_map/all_to_all | solution.py:134
  56.1 0.5 broadcast.171
  56.6 0.7 %reduce.6 = f32[32,192]{1,0:T(8,128)S(1)} reduce(f32[32,1,192]{2,1,0:T(1,128)S(1)} %all-to-all-done, f32[]{:T(128)} %broadcast.171), dimensions={1}, to_apply=%all_to_all.3.reduce_sub_computation | reduce | bytes 49156 | tf_op jit(solution)/shard_map/all_to_all | solution.py:134
  58.0 1.6 %fusion.13 = f32[5,128,128]{2,1,0:T(8,128)S(1)} fusion(f32[1280,128]{1,0:T(8,128)S(1)} %pad_maximum_fusion, f32[5,1280]{1,0:T(8,128)S(1)} %pad_maximum_fusion.1, pred[1024,128]{0,1:T(32,128)(4,1)S(1)} %iota_compare_fusion.2, pred[256,128]{0,1:T(32,128)(4,1)S(1)} %get-tuple-element.27), kind=kOutput, calls=%fused_computation.19 | convolution fusion | flops 1259274240 | bytes 1172480 | tf_op jit(solution)/shard_map/nk,fna->fka/dot_general | solution.py:146
  59.7 0.2 copy.93
  59.9 0.8 %fusion.8 = f32[5,8,16,128]{3,0,2,1:T(8,128)S(1)} fusion(f32[5,8,16,128]{3,0,2,1:T(8,128)S(1)} %bitcast.99, f32[5,8,16,128]{3,0,2,1:T(8,128)S(1)} %fusion.10, f32[5,8,16,128]{3,2,1,0:T(8,128)S(1)} %get-tuple-element.5, f32[8,16,128]{2,1,0:T(8,128)S(1)} %get-tuple-element.15, f32[1,5,5]{2,0,1:T(1,128)S(1)} %get-tuple-element.18), kind=kOutput, calls=%fused_computation.12 | convolution fusion | flops 5160960 | bytes 1376356 | tf_op jit(solution)/shard_map/fg,fxra->gxra/dot_general | solution.py:112
  60.7 0.8 %copy.94 = f32[5,8,16,128]{3,2,1,0:T(8,128)} copy(f32[5,8,16,128]{3,0,2,1:T(8,128)S(1)} %fusion.8) | data formatting | bytes 655360 | tf_op jit(solution)/shard_map/add | solution.py:147
  (58 shorter events, 1.7 us)
Async XLA Ops:
  0.0 1.0 %copy-start = (f32[5,8,16,128]{3,2,1,0:T(8,128)S(1)}, f32[5,8,16,128]{3,2,1,0:T(8,128)}, u32[]{:S(2)}) copy-start(f32[5,8,16,128]{3,2,1,0:T(8,128)} %param.11) | copy-start | bytes 983044
  0.0 17.1 %copy-start.2 = (f32[128,256]{1,0:T(8,128)S(1)}, f32[128,256]{1,0:T(8,128)}, u32[]{:S(2)}) copy-start(f32[128,256]{1,0:T(8,128)} %constant.70.clone) | copy-start | bytes 393220
  2.2 18.7 %collective-permute-start.1 = (f32[8,640]{1,0:T(8,128)S(1)}, f32[8,640]{1,0:T(8,128)S(1)}, u32[]{:S(2)}, u32[]{:S(2)}) collective-permute-start(f32[8,640]{1,0:T(8,128)S(1)} %fusion.45), channel_id=1, source_target_pairs={{2,0},{4,2},{6,4},{8,6},{10,8},{12,10},{14,12},{0,14},{3,1},{5,3},... | collective-permute-start | bytes 61448 | tf_op jit(solution)/shard_map/ppermute | solution.py:90
  15.0 3.0 %copy-start.1 = (f32[3,8,16,128]{3,2,1,0:T(8,128)S(1)}, f32[3,8,16,128]{3,2,1,0:T(8,128)}, u32[]{:S(2)}) copy-start(f32[3,8,16,128]{3,2,1,0:T(8,128)} %param.12) | copy-start | bytes 589828
  15.0 3.0 %copy-start.8 = (f32[3,5,5]{2,0,1:T(4,128)S(1)}, f32[3,5,5]{2,0,1:T(4,128)}, u32[]{:S(2)}) copy-start(f32[3,5,5]{2,0,1:T(4,128)} %param.13) | copy-start | bytes 904
  15.1 3.6 %copy-start.9 = (s32[256]{0:T(256)S(1)}, s32[256]{0:T(256)}, u32[]{:S(2)}) copy-start(s32[256]{0:T(256)} %param.14) | copy-start | bytes 3076
  15.1 3.6 %copy-start.5 = (s32[256,1]{0,1:T(1,128)S(1)}, s32[256,1]{0,1:T(1,128)}, u32[]{:S(2)}) copy-start(s32[256,1]{0,1:T(1,128)} %param.15) | copy-start | bytes 3076
  15.1 6.6 %collective-permute-start = (f32[8,640]{1,0:T(8,128)S(1)}, f32[8,640]{1,0:T(8,128)S(1)}, u32[]{:S(2)}, u32[]{:S(2)}) collective-permute-start(f32[8,640]{1,0:T(8,128)S(1)} %fusion.44), channel_id=1, source_target_pairs={{0,2},{2,4},{4,6},{6,8},{8,10},{10,12},{12,14},{14,0},{1,3},{3,5},... | collective-permute-start | bytes 61448 | tf_op jit(solution)/shard_map/ppermute | solution.py:89
  18.0 2.2 %copy-start.11 = (s32[256]{0:T(256)S(1)}, s32[256]{0:T(256)}, u32[]{:S(2)}) copy-start(s32[256]{0:T(256)} %param.16) | copy-start | bytes 3076
  18.0 2.9 %copy-start.7 = (f32[8,256]{1,0:T(8,128)S(1)}, f32[8,256]{1,0:T(8,128)}, u32[]{:S(2)}) copy-start(f32[8,256]{1,0:T(8,128)} %constant.72.clone) | copy-start | bytes 24580
  18.7 3.0 %copy-start.6 = (f32[8,256]{1,0:T(8,128)S(1)}, f32[8,256]{1,0:T(8,128)}, u32[]{:S(2)}) copy-start(f32[8,256]{1,0:T(8,128)} %constant.71.clone) | copy-start | bytes 24580
  23.4 11.0 %copy-start.10 = (s32[256,1]{0,1:T(1,128)S(1)}, s32[256,1]{0,1:T(1,128)}, u32[]{:S(2)}) copy-start(s32[256,1]{0,1:T(1,128)} %multiply_add_fusion) | copy-start | bytes 3076
  23.4 11.0 %copy-start.12 = (f32[256]{0:T(256)S(1)}, f32[256]{0:T(256)}, u32[]{:S(2)}) copy-start(f32[256]{0:T(256)} %convert_element_type.35) | copy-start | bytes 3076
  23.5 24.0 %collective-permute-start.2 = (f32[5,1,16,128]{3,2,1,0:T(8,128)S(1)}, f32[5,1,16,128]{3,2,1,0:T(8,128)S(1)}, u32[]{:S(2)}, u32[]{:S(2)}) collective-permute-start(f32[5,1,16,128]{3,2,1,0:T(8,128)S(1)} %get-tuple-element.12), channel_id=1, source_target_pairs={{16,0},{32,16},{48,32},{64,48},{80,64},{96,80},{112,96},{128,112},... | collective-permute-start | bytes 122888 | tf_op jit(solution)/shard_map/ppermute | solution.py:100
  24.8 22.7 %collective-permute-start.3 = (f32[5,1,16,128]{3,2,1,0:T(8,128)S(1)}, f32[5,1,16,128]{3,2,1,0:T(8,128)S(1)}, u32[]{:S(2)}, u32[]{:S(2)}) collective-permute-start(f32[5,1,16,128]{3,2,1,0:T(8,128)S(1)} %get-tuple-element.11), channel_id=1, source_target_pairs={{0,16},{16,32},{32,48},{48,64},{64,80},{80,96},{96,112},{112,128},... | collective-permute-start | bytes 122888 | tf_op jit(solution)/shard_map/ppermute | solution.py:99
  28.8 18.6 %collective-permute-start.4 = (f32[5,8,1,128]{3,2,1,0:T(1,128)}, f32[5,8,1,128]{3,2,1,0:T(1,128)S(1)}, u32[]{:S(2)}, u32[]{:S(2)}) collective-permute-start(f32[5,8,1,128]{3,2,1,0:T(1,128)} %get-tuple-element.8), channel_id=1, source_target_pairs={{1,0},{3,2},{5,4},{7,6},{9,8},{11,10},{13,12},{15,14},{17,16},{19,... | collective-permute-start | bytes 61448 | tf_op jit(solution)/shard_map/ppermute | solution.py:103
  32.6 14.7 %collective-permute-start.5 = (f32[5,8,1,128]{3,2,1,0:T(1,128)S(1)}, f32[5,8,1,128]{3,2,1,0:T(1,128)S(1)}, u32[]{:S(2)}, u32[]{:S(2)}) collective-permute-start(f32[5,8,1,128]{3,2,1,0:T(1,128)S(1)} %get-tuple-element.7), channel_id=1, source_target_pairs={{0,1},{2,3},{4,5},{6,7},{8,9},{10,11},{12,13},{14,15},{16,17},{18,... | collective-permute-start | bytes 61448 | tf_op jit(solution)/shard_map/ppermute | solution.py:102
  35.8 20.2 %all-to-all-start = ((f32[32,1,192]{2,1,0:T(1,128)}), f32[32,1,192]{2,1,0:T(1,128)S(1)}, u32[]{:S(2)}, u32[]{:S(2)}) async-start(f32[32,1,192]{2,1,0:T(1,128)} %reshape.162), calls=%async_computation | async-start | bytes 65536 | tf_op jit(solution)/shard_map/all_to_all | solution.py:134
  47.5 0.7 %copy-start.4 = (f32[1,5,5]{2,0,1:T(1,128)S(1)}, f32[1,5,5]{2,0,1:T(1,128)}, u32[]{:S(2)}) copy-start(f32[1,5,5]{2,0,1:T(1,128)} %get-tuple-element.20) | copy-start | bytes 304
  47.6 1.3 %copy-start.3 = (f32[1,5,5]{2,0,1:T(1,128)S(1)}, f32[1,5,5]{2,0,1:T(1,128)}, u32[]{:S(2)}) copy-start(f32[1,5,5]{2,0,1:T(1,128)} %get-tuple-element.19) | copy-start | bytes 304

commit v3 on v2

--- a/solution.py
+++ b/solution.py
@@ -126,15 +126,17 @@
     onehot = (owner_rows[:, None] == jnp.arange(owners, dtype=jnp.int32)[None, :]).astype(jnp.int32)
     slot_rank = jnp.sum(onehot * (jnp.cumsum(onehot, axis=0) - 1), axis=1)
     slot_place = owner_rows * capacity + slot_rank
-    packed = jnp.concatenate([source, donor_cell.astype(jnp.float32)[None, :]], axis=0)
-    slots = (slot_place[:, None] == jnp.arange(owners * capacity, dtype=jnp.int32)[None, :]).astype(
-        jnp.float32
-    )
-    outbox = jnp.einsum("pt,ts->ps", packed, slots, precision=HI)
-    received = lax.all_to_all(
-        outbox.reshape(fields + 1, owners, capacity), "gx", split_axis=1, concat_axis=1, tiled=True
-    )
-    received = received.reshape(fields + 1, owners * capacity)
+    code = (slot_place).astype(jnp.float32)
+    pad = jnp.zeros((1, source.shape[1]), jnp.float32)
+    packed = jnp.concatenate([source, donor_cell.astype(jnp.float32)[None, :], code[None, :], pad], axis=0)
+    gathered = lax.all_gather(packed, "gx", axis=0)
+    first_slot = lax.axis_index("gx") * capacity
+    keep = (
+        gathered[:, fields + 1, :, None].astype(jnp.int32)
+        == first_slot + jnp.arange(capacity, dtype=jnp.int32)[None, None, :]
+    ).astype(jnp.float32)
+    compact = jnp.einsum("spt,stk->psk", gathered[:, : fields + 1], keep, precision=HI)
+    received = compact.reshape(fields + 1, owners * capacity)
     got_cell = received[fields].astype(jnp.int32)
     d_rows = (got_cell[:, None] // cells_a == row_ids[None, :]).astype(jnp.float32)
     d_lanes = (got_cell[:, None] % cells_a == lane_ids[None, :]).astype(jnp.float32)

time: 62 us -> 93.1 us (1.50)
  the two profiles are of different devices: /device:TPU:1 before, /device:TPU:24 now
where the time goes in v3:
time: 93.1 us; the launch traced here: 92.8 us
  blocking collectives  49.9 us (54%)
  starting transfers between devices  24.2 us (26%)
  matrix products  10.1 us (11%)
  local copies, waits for them, and re-layouts  4.12 us (4%)
  other arithmetic  3.92 us (4%)
    all_gather x1, blocking collectives, shards(): gathered = lax.all_gather(packed, 'gx', axis=0)  49.9 us
    ppermute x1, starting transfers between devices, shards(): from_right = lax.ppermute(to_left, 'az', down)  11 us
    ppermute x1, starting transfers between devices, shards(): after_x = lax.ppermute(filtered[:, :1], 'gx', down_x)  4.55 us
    ppermute x1, starting transfers between devices, shards(): before_x = lax.ppermute(filtered[:, -1:], 'gx', up_x)  3.4 us
    dot_general x3, matrix products, shards(): mixing = jnp.einsum('fg,fxra->gxra', flux[direction], change, precision=HI)  2.51 us
    ppermute x1, starting transfers between devices, shards(): before_r = lax.ppermute(filtered[:, :, -1:], 'row', up_r)  2.05 us
    ppermute x1, starting transfers between devices, shards(): from_left = lax.ppermute(to_right, 'az', up)  1.96 us
  transfers between devices with their start and end apart: 6, of which 0 were waited for; matrix products, arithmetic and copies ran while one was open for 12% of the time, Pallas kernels for 0%

profile of v3, /device:TPU:24, one launch (start us, length us, event | category | flops | bytes accessed | tf_op | source)
XLA Modules:
  0.0 92.8 jit_solution(13417918539349343669)
XLA Ops:
  0.0 0.9 %copy-done = f32[5,8,16,128]{3,2,1,0:T(8,128)S(1)} copy-done((f32[5,8,16,128]{3,2,1,0:T(8,128)S(1)}, f32[5,8,16,128]{3,2,1,0:T(8,128)}, u32[]{:S(2)}) %copy-start) | copy-done | bytes 327704
  1.0 1.3 %fusion.44 = f32[8,640]{1,0:T(8,128)S(1)} fusion(f32[128,8]{1,0:T(8,128)} %constant.77.clone, f32[640,128]{1,0:T(8,128)S(1)} %bitcast.98), kind=kOutput, calls=%fused_computation.90 | convolution fusion | flops 7864320 | bytes 352256 | tf_op jit(solution)/shard_map/lc,ck->kl/dot_general | solution.py:88
  2.3 11.0 %collective-permute-start.1 = (f32[8,640]{1,0:T(8,128)S(1)}, f32[8,640]{1,0:T(8,128)S(1)}, u32[]{:S(2)}, u32[]{:S(2)}) collective-permute-start(f32[8,640]{1,0:T(8,128)S(1)} %fusion.44), channel_id=1, source_target_pairs={{2,0},{4,2},{6,4},{8,6},{10,8},{12,10},{14,12},{0,14},{3,1},{5,3},... | collective-permute-start | bytes 61448 | tf_op jit(solution)/shard_map/ppermute | solution.py:90
  13.3 1.3 %fusion.43 = f32[8,640]{1,0:T(8,128)S(1)} fusion(f32[128,8]{1,0:T(8,128)} %constant.76.clone, f32[640,128]{1,0:T(8,128)S(1)} %bitcast.97), kind=kOutput, calls=%fused_computation.89 | convolution fusion | flops 7864320 | bytes 352256 | tf_op jit(solution)/shard_map/lc,ck->kl/dot_general | solution.py:87
  14.5 2.0 %collective-permute-start = (f32[8,640]{1,0:T(8,128)S(1)}, f32[8,640]{1,0:T(8,128)S(1)}, u32[]{:S(2)}, u32[]{:S(2)}) collective-permute-start(f32[8,640]{1,0:T(8,128)S(1)} %fusion.43), channel_id=1, source_target_pairs={{0,2},{2,4},{4,6},{6,8},{8,10},{10,12},{12,14},{14,0},{1,3},{3,5},... | collective-permute-start | bytes 61448 | tf_op jit(solution)/shard_map/ppermute | solution.py:89
  16.6 0.6 reduce-window.6
  17.2 0.2 slice_reduce_fusion
  17.4 0.1 fusion.29
  17.5 0.6 fusion.34
  18.1 0.9 convolution_bitcast_fusion.1
  19.1 0.5 iota_add_fusion
  19.6 0.6 convert_element_type.56
  20.3 0.6 pad.9.clone
  20.9 0.7 fusion.45
  21.7 0.7 fusion.4
  22.4 0.2 copy.37
  22.7 0.6 fusion.38
  23.5 2.1 %collective-permute-start.5 = (f32[5,8,1,128]{3,2,1,0:T(1,128)}, f32[5,8,1,128]{3,2,1,0:T(1,128)}, u32[]{:S(2)}, u32[]{:S(2)}) collective-permute-start(f32[5,8,1,128]{3,2,1,0:T(1,128)} %get-tuple-element.7), channel_id=1, source_target_pairs={{0,1},{2,3},{4,5},{6,7},{8,9},{10,11},{12,13},{14,15},{16,17},{18,... | collective-permute-start | bytes 61448 | tf_op jit(solution)/shard_map/ppermute | solution.py:102
  25.6 1.3 %collective-permute-start.4 = (f32[5,8,1,128]{3,2,1,0:T(1,128)S(1)}, f32[5,8,1,128]{3,2,1,0:T(1,128)}, u32[]{:S(2)}, u32[]{:S(2)}) collective-permute-start(f32[5,8,1,128]{3,2,1,0:T(1,128)S(1)} %get-tuple-element.8), channel_id=1, source_target_pairs={{1,0},{3,2},{5,4},{7,6},{9,8},{11,10},{13,12},{15,14},{17,16},{19,... | collective-permute-start | bytes 61448 | tf_op jit(solution)/shard_map/ppermute | solution.py:103
  26.9 3.4 %collective-permute-start.3 = (f32[5,1,16,128]{3,2,1,0:T(8,128)S(1)}, f32[5,1,16,128]{3,2,1,0:T(8,128)S(1)}, u32[]{:S(2)}, u32[]{:S(2)}) collective-permute-start(f32[5,1,16,128]{3,2,1,0:T(8,128)S(1)} %get-tuple-element.11), channel_id=1, source_target_pairs={{0,16},{16,32},{32,48},{48,64},{64,80},{80,96},{96,112},{112,128},... | collective-permute-start | bytes 122888 | tf_op jit(solution)/shard_map/ppermute | solution.py:99
  30.3 4.6 %collective-permute-start.2 = (f32[5,1,16,128]{3,2,1,0:T(8,128)S(1)}, f32[5,1,16,128]{3,2,1,0:T(8,128)S(1)}, u32[]{:S(2)}, u32[]{:S(2)}) collective-permute-start(f32[5,1,16,128]{3,2,1,0:T(8,128)S(1)} %get-tuple-element.12), channel_id=1, source_target_pairs={{16,0},{32,16},{48,32},{64,48},{80,64},{96,80},{112,96},{128,112},... | collective-permute-start | bytes 122888 | tf_op jit(solution)/shard_map/ppermute | solution.py:100
  34.8 0.5 fusion.12
  35.4 49.9 %all-gather = f32[256,256]{1,0:T(8,128)S(1)} all-gather(f32[8,256]{1,0:T(8,128)S(1)} %maximum_maximum_fusion), channel_id=2, replica_groups=mesh['gx'=32,'az'=8,'row'=2] {'gx'}, dimensions={0}, use_global_device_ids=true | all-gather | bytes 270336 | tf_op jit(solution)/shard_map/all_gather | solution.py:132
  85.4 0.6 convolution_bitcast_fusion.2
  86.4 0.2 fusion.24
  86.6 1.6 %fusion.13 = f32[5,128,128]{2,1,0:T(8,128)S(1)} fusion(f32[1280,128]{1,0:T(8,128)S(1)} %pad_maximum_fusion, f32[5,1280]{1,0:T(8,128)S(1)} %pad_maximum_fusion.1, pred[1024,128]{0,1:T(32,128)(4,1)S(1)} %iota_compare_fusion, pred[256,128]{0,1:T(32,128)(4,1)S(1)} %get-tuple-element.27), kind=kOutput, calls=%fused_computation.19 | convolution fusion | flops 1259274240 | bytes 1172480 | tf_op jit(solution)/shard_map/nk,fna->fka/dot_general | solution.py:148
  88.3 0.2 copy.53
  88.5 0.8 maximum_subtract_fusion.1
  89.4 0.8 fusion.11
  90.2 0.9 %fusion.10 = f32[5,8,16,128]{3,0,2,1:T(8,128)S(1)} fusion(f32[5,8,16,128]{3,0,2,1:T(8,128)S(1)} %fusion.11, f32[5,8,16,128]{3,2,1,0:T(8,128)S(1)} %get-tuple-element.6, f32[5,8,16,128]{3,2,1,0:T(8,128)S(1)} %maximum_subtract_fusion.1, f32[8,16,128]{2,1,0:T(8,128)S(1)} %get-tuple-element.17, f32[1,5,5]{2,0,1:T(1,128)S(1)} %get-tuple-element.19), kind=kOutput, calls=%fused_computation.15 | convolution fusion | flops 5160960 | bytes 1376356 | tf_op jit(solution)/shard_map/fg,fxra->gxra/dot_general | solution.py:112
  91.2 0.8 fusion.8
  92.0 0.8 copy.54
  (60 shorter events, 1.0 us)
Async XLA Ops:
  0.0 1.0 %copy-start = (f32[5,8,16,128]{3,2,1,0:T(8,128)S(1)}, f32[5,8,16,128]{3,2,1,0:T(8,128)}, u32[]{:S(2)}) copy-start(f32[5,8,16,128]{3,2,1,0:T(8,128)} %param.11) | copy-start | bytes 983044
  0.0 16.5 %copy-start.11 = (s32[256]{0:T(256)S(1)}, s32[256]{0:T(256)}, u32[]{:S(2)}) copy-start(s32[256]{0:T(256)} %param.14) | copy-start | bytes 3076
  0.0 16.5 %copy-start.8 = (f32[3,5,5]{2,0,1:T(4,128)S(1)}, f32[3,5,5]{2,0,1:T(4,128)}, u32[]{:S(2)}) copy-start(f32[3,5,5]{2,0,1:T(4,128)} %param.13) | copy-start | bytes 904
  0.0 16.5 %copy-start.3 = (s32[256,1]{0,1:T(1,128)S(1)}, s32[256,1]{0,1:T(1,128)}, u32[]{:S(2)}) copy-start(s32[256,1]{0,1:T(1,128)} %param.15) | copy-start | bytes 3076
  0.0 18.1 %copy-start.1 = (f32[3,8,16,128]{3,2,1,0:T(8,128)S(1)}, f32[3,8,16,128]{3,2,1,0:T(8,128)}, u32[]{:S(2)}) copy-start(f32[3,8,16,128]{3,2,1,0:T(8,128)} %param.12) | copy-start | bytes 589828
  1.0 17.1 %copy-start.2 = (f32[128,256]{1,0:T(8,128)S(1)}, f32[128,256]{1,0:T(8,128)}, u32[]{:S(2)}) copy-start(f32[128,256]{1,0:T(8,128)} %constant.78.clone) | copy-start | bytes 393220
  2.3 18.7 %collective-permute-start.1 = (f32[8,640]{1,0:T(8,128)S(1)}, f32[8,640]{1,0:T(8,128)S(1)}, u32[]{:S(2)}, u32[]{:S(2)}) collective-permute-start(f32[8,640]{1,0:T(8,128)S(1)} %fusion.44), channel_id=1, source_target_pairs={{2,0},{4,2},{6,4},{8,6},{10,8},{12,10},{14,12},{0,14},{3,1},{5,3},... | collective-permute-start | bytes 61448 | tf_op jit(solution)/shard_map/ppermute | solution.py:90
  14.5 7.1 %collective-permute-start = (f32[8,640]{1,0:T(8,128)S(1)}, f32[8,640]{1,0:T(8,128)S(1)}, u32[]{:S(2)}, u32[]{:S(2)}) collective-permute-start(f32[8,640]{1,0:T(8,128)S(1)} %fusion.43), channel_id=1, source_target_pairs={{0,2},{2,4},{4,6},{6,8},{8,10},{10,12},{12,14},{14,0},{1,3},{3,5},... | collective-permute-start | bytes 61448 | tf_op jit(solution)/shard_map/ppermute | solution.py:89
  16.5 2.5 %copy-start.4 = (s32[256]{0:T(256)}, s32[256]{0:T(256)S(1)}, u32[]{:S(2)}) copy-start(s32[256]{0:T(256)S(1)} %get-tuple-element.25) | copy-start | bytes 3076
  18.1 1.5 %copy-start.12 = (s32[256]{0:T(256)S(1)}, s32[256]{0:T(256)}, u32[]{:S(2)}) copy-start(s32[256]{0:T(256)} %param.16) | copy-start | bytes 3076
  18.1 2.8 %copy-start.7 = (f32[8,256]{1,0:T(8,128)S(1)}, f32[8,256]{1,0:T(8,128)}, u32[]{:S(2)}) copy-start(f32[8,256]{1,0:T(8,128)} %constant.80.clone) | copy-start | bytes 24580
  19.0 2.7 %copy-start.6 = (f32[8,256]{1,0:T(8,128)S(1)}, f32[8,256]{1,0:T(8,128)}, u32[]{:S(2)}) copy-start(f32[8,256]{1,0:T(8,128)} %constant.79.clone) | copy-start | bytes 24580
  23.4 11.4 %copy-start.5 = (s32[256]{0:T(256)S(1)}, s32[256]{0:T(256)}, u32[]{:S(2)}) copy-start(s32[256]{0:T(256)} %copy-done.4) | copy-start | bytes 3076
  23.4 11.9 %copy-start.9 = (f32[1,256]{1,0:T(1,128)S(1)}, f32[1,256]{1,0:T(1,128)}, u32[]{:S(2)}) copy-start(f32[1,256]{1,0:T(1,128)} %fusion.34) | copy-start | bytes 3076
  23.4 11.9 %copy-start.10 = (f32[256]{0:T(256)S(1)}, f32[256]{0:T(256)}, u32[]{:S(2)}) copy-start(f32[256]{0:T(256)} %convert_element_type.56) | copy-start | bytes 3076
  23.4 11.9 %copy-start.13 = (f32[8]{0:T(128)S(1)}, f32[8]{0:T(128)}, u32[]{:S(2)}) copy-start(f32[8]{0:T(128)} %pad.9.clone) | copy-start | bytes 100
  23.5 61.8 %copy-start.14 = (s32[32]{0:T(128)S(1)}, s32[32]{0:T(128)}, u32[]{:S(2)}) copy-start(s32[32]{0:T(128)} %iota_add_fusion) | copy-start | bytes 388
  23.5 65.0 %collective-permute-start.5 = (f32[5,8,1,128]{3,2,1,0:T(1,128)}, f32[5,8,1,128]{3,2,1,0:T(1,128)}, u32[]{:S(2)}, u32[]{:S(2)}) collective-permute-start(f32[5,8,1,128]{3,2,1,0:T(1,128)} %get-tuple-element.7), channel_id=1, source_target_pairs={{0,1},{2,3},{4,5},{6,7},{8,9},{10,11},{12,13},{14,15},{16,17},{18,... | collective-permute-start | bytes 61448 | tf_op jit(solution)/shard_map/ppermute | solution.py:102
  25.6 62.9 %collective-permute-start.4 = (f32[5,8,1,128]{3,2,1,0:T(1,128)S(1)}, f32[5,8,1,128]{3,2,1,0:T(1,128)}, u32[]{:S(2)}, u32[]{:S(2)}) collective-permute-start(f32[5,8,1,128]{3,2,1,0:T(1,128)S(1)} %get-tuple-element.8), channel_id=1, source_target_pairs={{1,0},{3,2},{5,4},{7,6},{9,8},{11,10},{13,12},{15,14},{17,16},{19,... | collective-permute-start | bytes 61448 | tf_op jit(solution)/shard_map/ppermute | solution.py:103
  26.9 62.5 %collective-permute-start.3 = (f32[5,1,16,128]{3,2,1,0:T(8,128)S(1)}, f32[5,1,16,128]{3,2,1,0:T(8,128)S(1)}, u32[]{:S(2)}, u32[]{:S(2)}) collective-permute-start(f32[5,1,16,128]{3,2,1,0:T(8,128)S(1)} %get-tuple-element.11), channel_id=1, source_target_pairs={{0,16},{16,32},{32,48},{48,64},{64,80},{80,96},{96,112},{112,128},... | collective-permute-start | bytes 122888 | tf_op jit(solution)/shard_map/ppermute | solution.py:99
  30.3 59.1 %collective-permute-start.2 = (f32[5,1,16,128]{3,2,1,0:T(8,128)S(1)}, f32[5,1,16,128]{3,2,1,0:T(8,128)S(1)}, u32[]{:S(2)}, u32[]{:S(2)}) collective-permute-start(f32[5,1,16,128]{3,2,1,0:T(8,128)S(1)} %get-tuple-element.12), channel_id=1, source_target_pairs={{16,0},{32,16},{48,32},{64,48},{80,64},{96,80},{112,96},{128,112},... | collective-permute-start | bytes 122888 | tf_op jit(solution)/shard_map/ppermute | solution.py:100

commit v4 on v2

--- a/solution.py
+++ b/solution.py
@@ -84,8 +84,14 @@
     lines = adjoint.reshape(fields * rows, cells_a)
 
     up, down = neighbours(adjoint, "az", True)
-    to_right = jnp.einsum("lc,ck->kl", lines, jnp.asarray(send_right_t), precision=HI)
-    to_left = jnp.einsum("lc,ck->kl", lines, jnp.asarray(send_left_t), precision=HI)
+    right_moment = jnp.asarray(send_right_t[:, EDGE])
+    left_moment = jnp.asarray(send_left_t[:, EDGE])
+    to_right = jnp.concatenate(
+        [lines[:, cells_a - EDGE :], jnp.sum(lines * right_moment[None], axis=1, keepdims=True)], axis=1
+    ).T
+    to_left = jnp.concatenate(
+        [lines[:, :EDGE], jnp.sum(lines * left_moment[None], axis=1, keepdims=True)], axis=1
+    ).T
     from_left = lax.ppermute(to_right, "az", up)
     from_right = lax.ppermute(to_left, "az", down)
     both = jnp.einsum("lc,co->lo", lines, jnp.asarray(own_t), precision=HI)
@@ -94,23 +100,6 @@
     both = both.reshape(fields, rows_x, rows_r, 2 * cells_a)
     filtered = both[..., :cells_a]
     along_a = both[..., cells_a:]
-
-    up_x, down_x = neighbours(filtered, "gx", False)
-    before_x = lax.ppermute(filtered[:, -1:], "gx", up_x)
-    after_x = lax.ppermute(filtered[:, :1], "gx", down_x)
-    up_r, down_r = neighbours(filtered, "row", False)
-    before_r = lax.ppermute(filtered[:, :, -1:], "row", up_r)
-    after_r = lax.ppermute(filtered[:, :, :1], "row", down_r)
-    along_x = jnp.concatenate([filtered[:, 1:], after_x], axis=1) - jnp.concatenate(
-        [before_x, filtered[:, :-1]], axis=1
-    )
-    along_r = jnp.concatenate([filtered[:, :, 1:], after_r], axis=2) - jnp.concatenate(
-        [before_r, filtered[:, :, :-1]], axis=2
-    )
-    gradient = filtered
-    for direction, change in enumerate((along_x, along_r, along_a)):
-        mixing = jnp.einsum("fg,fxra->gxra", flux[direction], change, precision=HI)
-        gradient = gradient + coeff[direction][None] * mixing
 
     row_ids = jnp.arange(rows, dtype=jnp.int32)
     lane_ids = jnp.arange(cells_a, dtype=jnp.int32)
@@ -127,23 +116,44 @@
     slot_rank = jnp.sum(onehot * (jnp.cumsum(onehot, axis=0) - 1), axis=1)
     slot_place = owner_rows * capacity + slot_rank
     packed = jnp.concatenate([source, donor_cell.astype(jnp.float32)[None, :]], axis=0)
-    slots = (slot_place[:, None] == jnp.arange(owners * capacity, dtype=jnp.int32)[None, :]).astype(
-        jnp.float32
+    slots = (
+        slot_place[:, None, None]
+        == (jnp.arange(owners, dtype=jnp.int32)[:, None] * capacity + jnp.arange(capacity, dtype=jnp.int32))[None]
+    ).astype(jnp.float32)
+    outbox = jnp.einsum("pt,tos->ops", packed, slots, precision=HI).reshape(owners, (fields + 1) * capacity)
+    received = lax.all_to_all(outbox, "gx", split_axis=0, concat_axis=0, tiled=True)
+    taken = jnp.einsum("nk,fna->fka", t_rows, -source[:, :, None] * t_lanes[None], precision=HI)
+    up_x, down_x = neighbours(filtered, "gx", False)
+    last_x, first_x, last_r, first_r = filtered[:, -1], filtered[:, 0], filtered[:, :, -1], filtered[:, :, 0]
+    before_x = lax.ppermute(last_x, "gx", up_x)[:, None]
+    after_x = lax.ppermute(first_x, "gx", down_x)[:, None]
+    if lax.axis_size("row") == 2:
+        band = lax.axis_index("row")
+        other = lax.ppermute(jnp.where(band == 0, last_r, first_r), "row", [(0, 1), (1, 0)])
+        before_r = jnp.where(band == 1, other, 0.0)[:, :, None]
+        after_r = jnp.where(band == 0, other, 0.0)[:, :, None]
+    else:
+        up_r, down_r = neighbours(filtered, "row", False)
+        before_r = lax.ppermute(last_r, "row", up_r)[:, :, None]
+        after_r = lax.ppermute(first_r, "row", down_r)[:, :, None]
+    along_x = jnp.concatenate([filtered[:, 1:], after_x], axis=1) - jnp.concatenate(
+        [before_x, filtered[:, :-1]], axis=1
     )
-    outbox = jnp.einsum("pt,ts->ps", packed, slots, precision=HI)
-    received = lax.all_to_all(
-        outbox.reshape(fields + 1, owners, capacity), "gx", split_axis=1, concat_axis=1, tiled=True
+    along_r = jnp.concatenate([filtered[:, :, 1:], after_r], axis=2) - jnp.concatenate(
+        [before_r, filtered[:, :, :-1]], axis=2
     )
-    received = received.reshape(fields + 1, owners * capacity)
+    gradient = filtered
+    for direction, change in enumerate((along_x, along_r, along_a)):
+        mixing = jnp.einsum("fg,fxra->gxra", flux[direction], change, precision=HI)
+        gradient = gradient + coeff[direction][None] * mixing
+    gradient = gradient + taken.reshape(adjoint.shape)
+
+    received = received.reshape(owners, fields + 1, capacity).transpose(1, 0, 2).reshape(fields + 1, owners * capacity)
     got_cell = received[fields].astype(jnp.int32)
     d_rows = (got_cell[:, None] // cells_a == row_ids[None, :]).astype(jnp.float32)
     d_lanes = (got_cell[:, None] % cells_a == lane_ids[None, :]).astype(jnp.float32)
-
-    all_rows = jnp.concatenate([t_rows, d_rows], axis=0)
-    all_lanes = jnp.concatenate([t_lanes, d_lanes], axis=0)
-    amounts = jnp.concatenate([-source, received[:fields]], axis=1)
-    spread = amounts[:, :, None] * all_lanes[None]
-    update = jnp.einsum("nk,fna->fka", all_rows, spread, precision=HI)
+    spread = received[:fields, :, None] * d_lanes[None]
+    update = jnp.einsum("nk,fna->fka", d_rows, spread, precision=HI)
     return gradient + update.reshape(adjoint.shape)
 
 

time: 62 us -> 56.6 us (0.913)
  matrix products: 9.95 us -> 8.38 us
  other arithmetic: 3.21 us -> 1.65 us
  local copies, waits for them, and re-layouts: 6.14 us -> 4.61 us
  starting transfers between devices: 35.5 us -> 34.2 us
  waiting for transfers between devices: 6.21 us -> 7 us
    unnamed x28 -> x22, local copies, waits for them, and re-layouts: 2.41 us -> 0.08 us
    dot_general x4 -> x3, matrix products: 4.65 us -> 3.07 us  [the longest x1 1.37 us: shards(): update = jnp.einsum('nk,fna->fka', d_rows, spread, precision=HI)]
    ppermute x4 -> x3, starting transfers between devices: 10.4 us -> 9.3 us  [the longest x1 4.02 us: shards(): lax.ppermute(jnp.where(band == 0, last_r, first_r), 'row', [(0, 1), (1, 0)])]
    ppermute x1, waiting for transfers between devices: 0.01 us -> 0.93 us  [shards(): from_left = lax.ppermute(to_right, 'az', up)]
    slice x5 -> x6, local copies, waits for them, and re-layouts: 0.93 us -> 1.75 us  [the longest x2 1.39 us: shards(): lines[:, cells_a - EDGE:]]
    all_to_all x1, other arithmetic: 0.72 us -> 0.08 us  [shards(): lax.all_to_all(outbox, 'gx', split_axis=0, concat_axis=0, tiled=True)]
  transfers between devices with their start and end apart: 7 -> 6, of which waited for: 1 -> 2; matrix products, arithmetic and copies ran while one was open for 15% -> 13% of each run, Pallas kernels for 0% -> 0%
where the time goes in v4:
time: 56.6 us; the launch traced here: 56.4 us
  starting transfers between devices  34.2 us (60%)
  matrix products  8.38 us (15%)
  waiting for transfers between devices  7 us (12%)
  local copies, waits for them, and re-layouts  4.61 us (8%)
  other arithmetic  1.65 us (3%)
    all_to_all x1, starting transfers between devices, shards(): lax.all_to_all(outbox, 'gx', split_axis=0, concat_axis=0, tiled=True)  11.5 us
    ppermute x1, starting transfers between devices, shards(): from_right = lax.ppermute(to_left, 'az', down)  11.5 us
    all_to_all x1, waiting for transfers between devices, shards(): lax.all_to_all(outbox, 'gx', split_axis=0, concat_axis=0, tiled=True)  6.06 us
    ppermute x1, starting transfers between devices, shards(): lax.ppermute(jnp.where(band == 0, last_r, first_r), 'row', [(0, 1), (1, 0)])  4.02 us
    ppermute x1, starting transfers between devices, shards(): before_x = lax.ppermute(last_x, 'gx', up_x)[:, None]  3.99 us
    dot_general x3, matrix products, shards(): mixing = jnp.einsum('fg,fxra->gxra', flux[direction], change, precision=HI)  2.51 us
    ppermute x1, starting transfers between devices, shards(): from_left = lax.ppermute(to_right, 'az', up)  1.92 us
    slice x2, local copies, waits for them, and re-layouts, shards(): lines[:, cells_a - EDGE:]  1.39 us
  transfers between devices with their start and end apart: 6, of which 2 were waited for; matrix products, arithmetic and copies ran while one was open for 13% of the time, Pallas kernels for 0%

profile of v4, /device:TPU:1, one launch (start us, length us, event | category | flops | bytes accessed | tf_op | source)
XLA Modules:
  0.0 56.4 jit_solution(17069237806861358586)
XLA Ops:
  0.0 1.3 %fusion.50 = (f32[640,7]{1,0:T(8,128)S(1)}, f32[640,7]{1,0:T(8,128)S(1)}) fusion(f32[640,128]{1,0:T(8,128)} %bitcast.120), kind=kLoop, calls=%fused_computation.99 | loop fusion | bytes 71680 | tf_op jit(solution)/shard_map/slice | solution.py:90
  1.3 0.1 copy.123
  1.4 0.2 multiply_reduce_fusion.1
  1.8 11.5 %collective-permute-start.1 = (f32[8,640]{1,0:T(8,128)S(1)}, f32[8,640]{1,0:T(8,128)S(1)}, u32[]{:S(2)}, u32[]{:S(2)}) collective-permute-start(f32[8,640]{1,0:T(8,128)S(1)} %maximum_bitcast_fusion.1), channel_id=1, source_target_pairs={{2,0},{4,2},{6,4},{8,6},{10,8},{12,10},{14,12},{0,14},{3,1},{5,3},... | collective-permute-start | bytes 61448 | tf_op jit(solution)/shard_map/ppermute | solution.py:96
  13.3 0.1 copy.121
  13.4 0.1 broadcast_in_dim.18
  13.6 1.9 %collective-permute-start = (f32[8,640]{1,0:T(8,128)S(1)}, f32[8,640]{1,0:T(8,128)S(1)}, u32[]{:S(2)}, u32[]{:S(2)}) collective-permute-start(f32[8,640]{1,0:T(8,128)S(1)} %maximum_bitcast_fusion), channel_id=1, source_target_pairs={{0,2},{2,4},{4,6},{6,8},{8,10},{10,12},{12,14},{14,0},{1,3},{3,5},... | collective-permute-start | bytes 61448 | tf_op jit(solution)/shard_map/ppermute | solution.py:95
  15.5 0.9 %convolution_bitcast_fusion.1 = f32[640,256]{0,1:T(8,128)S(1)} fusion(f32[128,256]{1,0:T(8,128)S(1)} %copy-done.2, f32[640,128]{1,0:T(8,128)S(1)} %bitcast.121), kind=kOutput, calls=%fused_computation.8 | convolution fusion | flops 251658240 | bytes 1114112 | tf_op jit(solution)/shard_map/lc,co->lo/dot_general | solution.py:97
  16.6 0.6 %reduce-window.6 = s32[32,2,128]{2,0,1:T(8,128)S(1)} reduce-window(s32[32,2,128]{2,0,1:T(8,128)S(1)} %fusion.38, s32[]{:T(128)} %constant.66.clone.1), window={size=1x1x128 pad=0_0x0_0x127_0}, to_apply=%region_3.4 | reduce-window | flops 1040384 | bytes 65540 | tf_op jit(solution)/shard_map/reduce-window
  17.2 0.2 slice_reduce_fusion
  17.5 0.1 fusion.37
  17.6 0.7 %fusion.52 = f32[640,256]{0,1:T(8,128)S(1)} fusion(f32[8,640]{1,0:T(8,128)S(1)} %collective-permute-done.1, f32[8,256]{1,0:T(8,128)S(1)} %copy-done.5), kind=kOutput, calls=%fused_computation.101 | convolution fusion | flops 15728640 | bytes 684032 | tf_op jit(solution)/shard_map/kl,ko->lo/dot_general | solution.py:99
  18.4 0.9 %collective-permute-done = f32[8,640]{1,0:T(8,128)S(1)} collective-permute-done((f32[8,640]{1,0:T(8,128)S(1)}, f32[8,640]{1,0:T(8,128)S(1)}, u32[]{:S(2)}, u32[]{:S(2)}) %collective-permute-start) | collective-permute-done | bytes 20512 | tf_op jit(solution)/shard_map/ppermute | solution.py:95
  19.3 0.7 %fusion.4 = f32[640,256]{0,1:T(8,128)S(1)} fusion(f32[640,256]{0,1:T(8,128)S(1)} %fusion.52, f32[640,256]{0,1:T(8,128)S(1)} %convolution_bitcast_fusion.1, f32[8,640]{1,0:T(8,128)S(1)} %collective-permute-done, f32[8,256]{1,0:T(8,128)S(1)} %copy-done.4), kind=kOutput, calls=%fused_computation.5 | convolution fusion | flops 16056320 | bytes 1994752 | tf_op jit(solution)/shard_map/kl,ko->lo/dot_general | solution.py:98
  20.1 0.2 copy.125
  20.5 4.0 %collective-permute-start.4 = (f32[5,8,128]{2,1,0:T(8,128)S(1)}, f32[5,8,128]{2,1,0:T(8,128)S(1)}, u32[]{:S(2)}, u32[]{:S(2)}) collective-permute-start(f32[5,8,128]{2,1,0:T(8,128)S(1)} %select_bitcast_fusion), channel_id=1, source_target_pairs={{0,1},{1,0},{2,3},{3,2},{4,5},{5,4},{6,7},{7,6},{8,9},{9,8},{10,11... | collective-permute-start | bytes 61448 | tf_op jit(solution)/shard_map/ppermute | solution.py:132
  24.6 1.3 %collective-permute-start.2 = (f32[5,16,128]{2,1,0:T(8,128)S(1)}, f32[5,16,128]{2,1,0:T(8,128)S(1)}, u32[]{:S(2)}, u32[]{:S(2)}) collective-permute-start(f32[5,16,128]{2,1,0:T(8,128)S(1)} %get-tuple-element.14), channel_id=1, source_target_pairs={{16,0},{32,16},{48,32},{64,48},{80,64},{96,80},{112,96},{128,112},... | collective-permute-start | bytes 122888 | tf_op jit(solution)/shard_map/ppermute | solution.py:129
  25.9 4.0 %collective-permute-start.3 = (f32[5,16,128]{2,1,0:T(8,128)S(1)}, f32[5,16,128]{2,1,0:T(8,128)S(1)}, u32[]{:S(2)}, u32[]{:S(2)}) collective-permute-start(f32[5,16,128]{2,1,0:T(8,128)S(1)} %get-tuple-element.13), channel_id=1, source_target_pairs={{0,16},{16,32},{32,48},{48,64},{64,80},{80,96},{96,112},{112,128},... | collective-permute-start | bytes 122888 | tf_op jit(solution)/shard_map/ppermute | solution.py:128
  29.8 0.5 fusion.13
  30.3 1.2 %convolution_bitcast_fusion.3 = f32[32,6,32]{2,1,0:T(8,128)S(1)} fusion(s32[32,32]{1,0:T(8,128)S(1)} %iota_add_fusion, s32[256]{0:T(256)S(1)} %multiply_add_fusion, f32[1,256]{1,0:T(1,128)S(1)} %bitcast.136, f32[5,256]{1,0:T(8,128)S(1)} %get-tuple-element.28), kind=kOutput, calls=%fused_computation.22 | convolution fusion | flops 19138048 | bytes 35840 | tf_op jit(solution)/shard_map/pt,tos->ops/dot_general | solution.py:123
  31.5 0.7 %all_to_all.8 = f32[32,1,192]{2,1,0:T(1,128)} reshape(f32[32,6,32]{2,1,0:T(8,128)S(1)} %convolution_bitcast_fusion.3) | data formatting | bytes 49152 | tf_op jit(solution)/shard_map/all_to_all | solution.py:124
  32.3 11.5 %all-to-all-start = ((f32[32,1,192]{2,1,0:T(1,128)}), f32[32,1,192]{2,1,0:T(1,128)S(1)}, u32[]{:S(2)}, u32[]{:S(2)}) async-start(f32[32,1,192]{2,1,0:T(1,128)} %all_to_all.8), calls=%async_computation | async-start | bytes 65536 | tf_op jit(solution)/shard_map/all_to_all | solution.py:124
  43.8 0.5 convolution_bitcast_fusion.2
  44.3 0.2 copy.144
  44.7 0.8 %fusion.12 = f32[5,8,16,128]{3,0,2,1:T(8,128)S(1)} fusion(f32[5,8,16,128]{3,2,1,0:T(8,128)S(1)} %maximum_subtract_fusion, f32[8,16,128]{2,1,0:T(8,128)S(1)} %get-tuple-element.20, f32[1,5,5]{2,0,1:T(1,128)S(1)} %get-tuple-element.26), kind=kOutput, calls=%fused_computation.18 | convolution fusion | flops 4997120 | bytes 720996 | tf_op jit(solution)/shard_map/fg,fxra->gxra/dot_general | solution.py:147
  45.5 0.9 %fusion.11 = f32[5,8,16,128]{3,0,2,1:T(8,128)S(1)} fusion(f32[5,8,16,128]{3,0,2,1:T(8,128)S(1)} %fusion.12, f32[5,8,16,128]{3,2,1,0:T(8,128)S(1)} %get-tuple-element.8, f32[5,8,16,128]{3,2,1,0:T(8,128)S(1)} %maximum_subtract_fusion.1, f32[8,16,128]{2,1,0:T(8,128)S(1)} %get-tuple-element.21, f32[1,5,5]{2,0,1:T(1,128)S(1)} %get-tuple-element.25), kind=kOutput, calls=%fused_computation.16 | convolution fusion | flops 5160960 | bytes 1376356 | tf_op jit(solution)/shard_map/fg,fxra->gxra/dot_general | solution.py:147
  46.4 6.1 %all-to-all-done = f32[32,1,192]{2,1,0:T(1,128)S(1)} async-done(((f32[32,1,192]{2,1,0:T(1,128)}), f32[32,1,192]{2,1,0:T(1,128)S(1)}, u32[]{:S(2)}, u32[]{:S(2)}) %all-to-all-start) | async-done | bytes 24608 | tf_op jit(solution)/shard_map/all_to_all | solution.py:124
  52.8 0.2 fusion.24
  53.2 1.4 %fusion.14 = f32[5,128,128]{2,1,0:T(8,128)S(1)} fusion(f32[1024,128]{1,0:T(8,128)S(1)} %fusion.24, f32[5,1024]{1,0:T(8,128)S(1)} %mul.152, s32[1024]{0:T(1024)S(1)} %get-tuple-element.29), kind=kOutput, calls=%fused_computation.20 | convolution fusion | flops 1007419392 | bytes 876544 | tf_op jit(solution)/shard_map/nk,fna->fka/dot_general | solution.py:156
  54.5 0.2 copy.148
  54.8 0.8 %fusion.9 = f32[5,8,16,128]{3,0,2,1:T(8,128)S(1)} fusion(f32[5,8,16,128]{3,0,2,1:T(8,128)S(1)} %bitcast.124, f32[5,8,16,128]{3,0,2,1:T(8,128)S(1)} %bitcast.123, f32[5,8,16,128]{3,0,2,1:T(8,128)S(1)} %fusion.11, f32[5,8,16,128]{3,2,1,0:T(8,128)S(1)} %get-tuple-element.7, f32[8,16,128]{2,1,0:T(8,128)S(1)} %get-tuple-element.19, ...), kind=kOutput, calls=%fused_computation.13 | convolution fusion | flops 5242880 | bytes 1704036 | tf_op jit(solution)/shard_map/fg,fxra->gxra/dot_general | solution.py:147
  55.6 0.8 %copy.149 = f32[5,8,16,128]{3,2,1,0:T(8,128)} copy(f32[5,8,16,128]{3,0,2,1:T(8,128)S(1)} %fusion.9) | data formatting | bytes 655360 | tf_op jit(solution)/shard_map/add | solution.py:157
  (57 shorter events, 1.2 us)
Async XLA Ops:
  0.0 1.4 %copy-start = (f32[5,8,16,128]{3,2,1,0:T(8,128)S(1)}, f32[5,8,16,128]{3,2,1,0:T(8,128)}, u32[]{:S(2)}) copy-start(f32[5,8,16,128]{3,2,1,0:T(8,128)} %param.11) | copy-start | bytes 983044
  0.0 1.4 %copy-start.9 = (f32[128]{0:T(128)S(1)}, f32[128]{0:T(128)}, u32[]{:S(2)}) copy-start(f32[128]{0:T(128)} %constant.74.clone) | copy-start | bytes 1540
  0.0 1.4 %copy-start.10 = (f32[128]{0:T(128)S(1)}, f32[128]{0:T(128)}, u32[]{:S(2)}) copy-start(f32[128]{0:T(128)} %constant.75.clone) | copy-start | bytes 1540
  1.3 14.2 %copy-start.2 = (f32[128,256]{1,0:T(8,128)S(1)}, f32[128,256]{1,0:T(8,128)}, u32[]{:S(2)}) copy-start(f32[128,256]{1,0:T(8,128)} %constant.76.clone) | copy-start | bytes 393220
  1.8 15.8 %collective-permute-start.1 = (f32[8,640]{1,0:T(8,128)S(1)}, f32[8,640]{1,0:T(8,128)S(1)}, u32[]{:S(2)}, u32[]{:S(2)}) collective-permute-start(f32[8,640]{1,0:T(8,128)S(1)} %maximum_bitcast_fusion.1), channel_id=1, source_target_pairs={{2,0},{4,2},{6,4},{8,6},{10,8},{12,10},{14,12},{0,14},{3,1},{5,3},... | collective-permute-start | bytes 61448 | tf_op jit(solution)/shard_map/ppermute | solution.py:96
  13.4 3.0 %copy-start.1 = (f32[3,8,16,128]{3,2,1,0:T(8,128)S(1)}, f32[3,8,16,128]{3,2,1,0:T(8,128)}, u32[]{:S(2)}) copy-start(f32[3,8,16,128]{3,2,1,0:T(8,128)} %param.12) | copy-start | bytes 589828
  13.6 5.7 %collective-permute-start = (f32[8,640]{1,0:T(8,128)S(1)}, f32[8,640]{1,0:T(8,128)S(1)}, u32[]{:S(2)}, u32[]{:S(2)}) collective-permute-start(f32[8,640]{1,0:T(8,128)S(1)} %maximum_bitcast_fusion), channel_id=1, source_target_pairs={{0,2},{2,4},{4,6},{6,8},{8,10},{10,12},{12,14},{14,0},{1,3},{3,5},... | collective-permute-start | bytes 61448 | tf_op jit(solution)/shard_map/ppermute | solution.py:95
  15.5 1.0 %copy-start.6 = (f32[3,5,5]{2,0,1:T(4,128)S(1)}, f32[3,5,5]{2,0,1:T(4,128)}, u32[]{:S(2)}) copy-start(f32[3,5,5]{2,0,1:T(4,128)} %param.13) | copy-start | bytes 904
  15.5 1.0 %copy-start.7 = (s32[256]{0:T(256)S(1)}, s32[256]{0:T(256)}, u32[]{:S(2)}) copy-start(s32[256]{0:T(256)} %param.14) | copy-start | bytes 3076
  15.5 1.0 %copy-start.3 = (s32[256,1]{0,1:T(1,128)S(1)}, s32[256,1]{0,1:T(1,128)}, u32[]{:S(2)}) copy-start(s32[256,1]{0,1:T(1,128)} %param.15) | copy-start | bytes 3076
  16.4 1.2 %copy-start.8 = (s32[256]{0:T(256)S(1)}, s32[256]{0:T(256)}, u32[]{:S(2)}) copy-start(s32[256]{0:T(256)} %param.16) | copy-start | bytes 3076
  16.4 1.2 %copy-start.5 = (f32[8,256]{1,0:T(8,128)S(1)}, f32[8,256]{1,0:T(8,128)}, u32[]{:S(2)}) copy-start(f32[8,256]{1,0:T(8,128)} %constant.78.clone) | copy-start | bytes 24580
  16.4 2.9 %copy-start.4 = (f32[8,256]{1,0:T(8,128)S(1)}, f32[8,256]{1,0:T(8,128)}, u32[]{:S(2)}) copy-start(f32[8,256]{1,0:T(8,128)} %constant.77.clone) | copy-start | bytes 24580
  20.5 24.0 %collective-permute-start.4 = (f32[5,8,128]{2,1,0:T(8,128)S(1)}, f32[5,8,128]{2,1,0:T(8,128)S(1)}, u32[]{:S(2)}, u32[]{:S(2)}) collective-permute-start(f32[5,8,128]{2,1,0:T(8,128)S(1)} %select_bitcast_fusion), channel_id=1, source_target_pairs={{0,1},{1,0},{2,3},{3,2},{4,5},{5,4},{6,7},{7,6},{8,9},{9,8},{10,11... | collective-permute-start | bytes 61448 | tf_op jit(solution)/shard_map/ppermute | solution.py:132
  24.6 20.1 %collective-permute-start.2 = (f32[5,16,128]{2,1,0:T(8,128)S(1)}, f32[5,16,128]{2,1,0:T(8,128)S(1)}, u32[]{:S(2)}, u32[]{:S(2)}) collective-permute-start(f32[5,16,128]{2,1,0:T(8,128)S(1)} %get-tuple-element.14), channel_id=1, source_target_pairs={{16,0},{32,16},{48,32},{64,48},{80,64},{96,80},{112,96},{128,112},... | collective-permute-start | bytes 122888 | tf_op jit(solution)/shard_map/ppermute | solution.py:129
  25.9 18.8 %collective-permute-start.3 = (f32[5,16,128]{2,1,0:T(8,128)S(1)}, f32[5,16,128]{2,1,0:T(8,128)S(1)}, u32[]{:S(2)}, u32[]{:S(2)}) collective-permute-start(f32[5,16,128]{2,1,0:T(8,128)S(1)} %get-tuple-element.13), channel_id=1, source_target_pairs={{0,16},{16,32},{32,48},{48,64},{64,80},{80,96},{96,112},{112,128},... | collective-permute-start | bytes 122888 | tf_op jit(solution)/shard_map/ppermute | solution.py:128
  32.3 20.2 %all-to-all-start = ((f32[32,1,192]{2,1,0:T(1,128)}), f32[32,1,192]{2,1,0:T(1,128)S(1)}, u32[]{:S(2)}, u32[]{:S(2)}) async-start(f32[32,1,192]{2,1,0:T(1,128)} %all_to_all.8), calls=%async_computation | async-start | bytes 65536 | tf_op jit(solution)/shard_map/all_to_all | solution.py:124

commit v5 on v4

--- a/solution.py
+++ b/solution.py
@@ -124,7 +124,9 @@
     received = lax.all_to_all(outbox, "gx", split_axis=0, concat_axis=0, tiled=True)
     taken = jnp.einsum("nk,fna->fka", t_rows, -source[:, :, None] * t_lanes[None], precision=HI)
     up_x, down_x = neighbours(filtered, "gx", False)
-    last_x, first_x, last_r, first_r = filtered[:, -1], filtered[:, 0], filtered[:, :, -1], filtered[:, :, 0]
+    last_x, first_x, last_r, first_r, received = lax.optimization_barrier(
+        (filtered[:, -1], filtered[:, 0], filtered[:, :, -1], filtered[:, :, 0], received)
+    )
     before_x = lax.ppermute(last_x, "gx", up_x)[:, None]
     after_x = lax.ppermute(first_x, "gx", down_x)[:, None]
     if lax.axis_size("row") == 2:

time: 56.6 us -> 60.2 us (1.064); the launches traced: 56.4 us -> 59.3 us
  local copies, waits for them, and re-layouts: 4.61 us -> 6.14 us
  waiting for transfers between devices: 7 us -> 8.34 us
    all_to_all x1, waiting for transfers between devices: 6.06 us -> 7.96 us  [shards(): lax.all_to_all(outbox, 'gx', split_axis=0, concat_axis=0, tiled=True)]
    all_to_all x1, starting transfers between devices: 11.5 us -> 9.67 us  [shards(): lax.all_to_all(outbox, 'gx', split_axis=0, concat_axis=0, tiled=True)]
    ppermute x1, starting transfers between devices: 4.02 us -> 5.44 us  [shards(): lax.ppermute(jnp.where(band == 0, last_r, first_r), 'row', [(0, 1), (1, 0)])]
    unnamed x22 -> x31, local copies, waits for them, and re-layouts: 0.08 us -> 1.01 us
  transfers between devices with their start and end apart: 6 -> 6, of which waited for: 2 -> 2; matrix products, arithmetic and copies ran while one was open for 13% -> 12% of each run, Pallas kernels for 0% -> 0%
where the time goes in v5:
time: 60.2 us; the launch traced here: 59.3 us
  starting transfers between devices  33.8 us (56%)
  matrix products  8.38 us (14%)
  waiting for transfers between devices  8.34 us (14%)
  local copies, waits for them, and re-layouts  6.14 us (10%)
  other arithmetic  2.15 us (4%)
    ppermute x1, starting transfers between devices, shards(): from_right = lax.ppermute(to_left, 'az', down)  11.5 us
    all_to_all x1, starting transfers between devices, shards(): lax.all_to_all(outbox, 'gx', split_axis=0, concat_axis=0, tiled=True)  9.67 us
    all_to_all x1, waiting for transfers between devices, shards(): lax.all_to_all(outbox, 'gx', split_axis=0, concat_axis=0, tiled=True)  7.96 us
    ppermute x1, starting transfers between devices, shards(): lax.ppermute(jnp.where(band == 0, last_r, first_r), 'row', [(0, 1), (1, 0)])  5.44 us
    ppermute x1, starting transfers between devices, shards(): before_x = lax.ppermute(last_x, 'gx', up_x)[:, None]  3.99 us
    dot_general x3, matrix products, shards(): mixing = jnp.einsum('fg,fxra->gxra', flux[direction], change, precision=HI)  2.51 us
    ppermute x1, starting transfers between devices, shards(): from_left = lax.ppermute(to_right, 'az', up)  1.92 us
    slice x2, local copies, waits for them, and re-layouts, shards(): lines[:, cells_a - EDGE:]  1.39 us
  transfers between devices with their start and end apart: 6, of which 2 were waited for; matrix products, arithmetic and copies ran while one was open for 12% of the time, Pallas kernels for 0%

profile of v5, /device:TPU:1, one launch (start us, length us, event | category | flops | bytes accessed | tf_op | source)
XLA Modules:
  0.0 59.3 jit_solution(8787918881944455690)
XLA Ops:
  0.0 1.3 %fusion.50 = (f32[640,7]{1,0:T(8,128)S(1)}, f32[640,7]{1,0:T(8,128)S(1)}) fusion(f32[640,128]{1,0:T(8,128)} %bitcast.125), kind=kLoop, calls=%fused_computation.100 | loop fusion | bytes 71680 | tf_op jit(solution)/shard_map/slice | solution.py:90
  1.4 0.2 multiply_reduce_fusion.1
  1.8 11.5 %collective-permute-start.1 = (f32[8,640]{1,0:T(8,128)S(1)}, f32[8,640]{1,0:T(8,128)S(1)}, u32[]{:S(2)}, u32[]{:S(2)}) collective-permute-start(f32[8,640]{1,0:T(8,128)S(1)} %maximum_bitcast_fusion.1), channel_id=1, source_target_pairs={{2,0},{4,2},{6,4},{8,6},{10,8},{12,10},{14,12},{0,14},{3,1},{5,3},... | collective-permute-start | bytes 61448 | tf_op jit(solution)/shard_map/ppermute | solution.py:96
  13.6 1.9 %collective-permute-start = (f32[8,640]{1,0:T(8,128)S(1)}, f32[8,640]{1,0:T(8,128)S(1)}, u32[]{:S(2)}, u32[]{:S(2)}) collective-permute-start(f32[8,640]{1,0:T(8,128)S(1)} %maximum_bitcast_fusion), channel_id=1, source_target_pairs={{0,2},{2,4},{4,6},{6,8},{8,10},{10,12},{12,14},{14,0},{1,3},{3,5},... | collective-permute-start | bytes 61448 | tf_op jit(solution)/shard_map/ppermute | solution.py:95
  15.5 0.9 %convolution_bitcast_fusion.1 = f32[640,256]{0,1:T(8,128)S(1)} fusion(f32[128,256]{1,0:T(8,128)S(1)} %copy-done.2, f32[640,128]{1,0:T(8,128)S(1)} %bitcast.126), kind=kOutput, calls=%fused_computation.8 | convolution fusion | flops 251658240 | bytes 1114112 | tf_op jit(solution)/shard_map/lc,co->lo/dot_general | solution.py:97
  16.5 0.6 reduce-window.6
  17.1 0.2 slice_reduce_fusion
  17.4 0.6 %fusion.51 = (f32[1,5,5]{2,0,1:T(1,128)}, f32[1,5,5]{2,0,1:T(1,128)}, f32[1,5,5]{2,0,1:T(1,128)}) fusion(f32[3,5,5]{2,0,1:T(4,128)S(1)} %copy-done.9), kind=kLoop, calls=%fused_computation.101 | loop fusion | bytes 600 | tf_op jit(solution)/shard_map/slice | solution.py:149
  18.2 0.7 %fusion.52 = f32[640,256]{0,1:T(8,128)S(1)} fusion(f32[8,640]{1,0:T(8,128)S(1)} %collective-permute-done.1, f32[8,256]{1,0:T(8,128)S(1)} %copy-done.8), kind=kOutput, calls=%fused_computation.102 | convolution fusion | flops 15728640 | bytes 684032 | tf_op jit(solution)/shard_map/kl,ko->lo/dot_general | solution.py:99
  18.9 0.4 collective-permute-done
  19.3 0.7 %fusion.4 = f32[640,256]{0,1:T(8,128)S(1)} fusion(f32[640,256]{0,1:T(8,128)S(1)} %fusion.52, f32[640,256]{0,1:T(8,128)S(1)} %convolution_bitcast_fusion.1, f32[8,640]{1,0:T(8,128)S(1)} %collective-permute-done, f32[8,256]{1,0:T(8,128)S(1)} %copy-done.7), kind=kOutput, calls=%fused_computation.5 | convolution fusion | flops 16056320 | bytes 1994752 | tf_op jit(solution)/shard_map/kl,ko->lo/dot_general | solution.py:98
  20.1 0.2 copy.128
  20.5 0.5 fusion.13
  21.0 1.2 %convolution_bitcast_fusion.3 = f32[32,6,32]{2,1,0:T(8,128)S(1)} fusion(s32[32,32]{1,0:T(8,128)S(1)} %iota_add_fusion, s32[256]{0:T(256)S(1)} %multiply_add_fusion, f32[1,256]{1,0:T(1,128)S(1)} %bitcast.142, f32[5,256]{1,0:T(8,128)S(1)} %get-tuple-element.38), kind=kOutput, calls=%fused_computation.22 | convolution fusion | flops 19138048 | bytes 35840 | tf_op jit(solution)/shard_map/pt,tos->ops/dot_general | solution.py:123
  22.2 0.7 %all_to_all.11 = f32[32,1,192]{2,1,0:T(1,128)} reshape(f32[32,6,32]{2,1,0:T(8,128)S(1)} %convolution_bitcast_fusion.3) | data formatting | bytes 49152 | tf_op jit(solution)/shard_map/all_to_all | solution.py:124
  22.9 9.7 %all-to-all-start = ((f32[32,1,192]{2,1,0:T(1,128)}), f32[32,1,192]{2,1,0:T(1,128)S(1)}, u32[]{:S(2)}, u32[]{:S(2)}) async-start(f32[32,1,192]{2,1,0:T(1,128)} %all_to_all.11), calls=%async_computation | async-start | bytes 65536 | tf_op jit(solution)/shard_map/all_to_all | solution.py:124
  32.6 0.5 convolution_bitcast_fusion.2
  33.1 0.2 copy.150
  33.3 8.0 %all-to-all-done = f32[32,1,192]{2,1,0:T(1,128)S(1)} async-done(((f32[32,1,192]{2,1,0:T(1,128)}), f32[32,1,192]{2,1,0:T(1,128)S(1)}, u32[]{:S(2)}, u32[]{:S(2)}) %all-to-all-start) | async-done | bytes 24608 | tf_op jit(solution)/shard_map/all_to_all | solution.py:124
  41.3 5.4 %collective-permute-start.4 = (f32[5,8,128]{2,1,0:T(8,128)S(1)}, f32[5,8,128]{2,1,0:T(8,128)S(1)}, u32[]{:S(2)}, u32[]{:S(2)}) collective-permute-start(f32[5,8,128]{2,1,0:T(8,128)S(1)} %broadcast_select_fusion.2), channel_id=1, source_target_pairs={{0,1},{1,0},{2,3},{3,2},{4,5},{5,4},{6,7},{7,6},{8,9},{9,8},{10,11... | collective-permute-start | bytes 61448 | tf_op jit(solution)/shard_map/ppermute | solution.py:134
  46.8 1.3 %collective-permute-start.2 = (f32[5,16,128]{2,1,0:T(8,128)S(1)}, f32[5,16,128]{2,1,0:T(8,128)S(1)}, u32[]{:S(2)}, u32[]{:S(2)}) collective-permute-start(f32[5,16,128]{2,1,0:T(8,128)S(1)} %get-tuple-element.10), channel_id=1, source_target_pairs={{16,0},{32,16},{48,32},{64,48},{80,64},{96,80},{112,96},{128,112},... | collective-permute-start | bytes 122888 | tf_op jit(solution)/shard_map/ppermute | solution.py:131
  48.1 4.0 %collective-permute-start.3 = (f32[5,16,128]{2,1,0:T(8,128)S(1)}, f32[5,16,128]{2,1,0:T(8,128)S(1)}, u32[]{:S(2)}, u32[]{:S(2)}) collective-permute-start(f32[5,16,128]{2,1,0:T(8,128)S(1)} %get-tuple-element.11), channel_id=1, source_target_pairs={{0,16},{16,32},{32,48},{48,64},{64,80},{80,96},{96,112},{112,128},... | collective-permute-start | bytes 122888 | tf_op jit(solution)/shard_map/ppermute | solution.py:130
  52.3 0.6 %add_select_fusion = (s32[1024]{0:T(1024)}, s32[1024]{0:T(1024)S(1)}) fusion(s32[1024]{0:T(1024)S(1)} %convert_element_type.42), kind=kLoop, calls=%fused_computation.73 | loop fusion | flops 19456 | bytes 12288 | tf_op jit(solution)/shard_map/jit(floor_divide)/jit(_where)/select_n | solution.py:155
  52.9 0.2 fusion.24
  53.2 0.4 copy-done.10
  53.6 1.4 %fusion.14 = f32[5,128,128]{2,1,0:T(8,128)S(1)} fusion(f32[1024,128]{1,0:T(8,128)S(1)} %fusion.24, f32[5,1024]{1,0:T(8,128)S(1)} %mul.152, s32[1024]{0:T(1024)S(1)} %copy-done.10), kind=kOutput, calls=%fused_computation.20 | convolution fusion | flops 1007419392 | bytes 876544 | tf_op jit(solution)/shard_map/nk,fna->fka/dot_general | solution.py:158
  55.0 0.2 copy.152
  55.4 0.6 copy-done.5
  56.0 0.8 %fusion.12 = f32[5,8,16,128]{3,0,2,1:T(8,128)S(1)} fusion(f32[5,8,16,128]{3,2,1,0:T(8,128)S(1)} %maximum_subtract_fusion, f32[8,16,128]{2,1,0:T(8,128)S(1)} %get-tuple-element.30, f32[1,5,5]{2,0,1:T(1,128)S(1)} %copy-done.5), kind=kOutput, calls=%fused_computation.18 | convolution fusion | flops 4997120 | bytes 720996 | tf_op jit(solution)/shard_map/fg,fxra->gxra/dot_general | solution.py:149
  56.8 0.9 %fusion.11 = f32[5,8,16,128]{3,0,2,1:T(8,128)S(1)} fusion(f32[5,8,16,128]{3,0,2,1:T(8,128)S(1)} %fusion.12, f32[5,8,16,128]{3,2,1,0:T(8,128)S(1)} %get-tuple-element.18, f32[5,8,16,128]{3,2,1,0:T(8,128)S(1)} %maximum_subtract_fusion.1, f32[8,16,128]{2,1,0:T(8,128)S(1)} %get-tuple-element.31, f32[1,5,5]{2,0,1:T(1,128)S(1)} %copy-done.4), kind=kOutput, calls=%fused_computation.16 | convolution fusion | flops 5160960 | bytes 1376356 | tf_op jit(solution)/shard_map/fg,fxra->gxra/dot_general | solution.py:149
  57.7 0.8 %fusion.9 = f32[5,8,16,128]{3,0,2,1:T(8,128)S(1)} fusion(f32[5,8,16,128]{3,0,2,1:T(8,128)S(1)} %bitcast.129, f32[5,8,16,128]{3,0,2,1:T(8,128)S(1)} %bitcast.128, f32[5,8,16,128]{3,0,2,1:T(8,128)S(1)} %fusion.11, f32[5,8,16,128]{3,2,1,0:T(8,128)S(1)} %get-tuple-element.17, f32[8,16,128]{2,1,0:T(8,128)S(1)} %get-tuple-element.29, f32[1,5,5]{2,0,1:T(1,128)S(1)} %copy-done.3), kind=kOutput, calls=%fused_computation.13 | convolution fusion | flops 5242880 | bytes 1704036 | tf_op jit(solution)/shard_map/fg,fxra->gxra/dot_general | solution.py:149
  58.5 0.8 %copy.153 = f32[5,8,16,128]{3,2,1,0:T(8,128)} copy(f32[5,8,16,128]{3,0,2,1:T(8,128)S(1)} %fusion.9) | data formatting | bytes 655360 | tf_op jit(solution)/shard_map/add | solution.py:159
  (65 shorter events, 1.5 us)
Async XLA Ops:
  0.0 1.4 %copy-start = (f32[5,8,16,128]{3,2,1,0:T(8,128)S(1)}, f32[5,8,16,128]{3,2,1,0:T(8,128)}, u32[]{:S(2)}) copy-start(f32[5,8,16,128]{3,2,1,0:T(8,128)} %param.11) | copy-start | bytes 983044
  0.0 1.4 %copy-start.13 = (f32[128]{0:T(128)S(1)}, f32[128]{0:T(128)}, u32[]{:S(2)}) copy-start(f32[128]{0:T(128)} %constant.74.clone) | copy-start | bytes 1540
  0.0 1.4 %copy-start.14 = (f32[128]{0:T(128)S(1)}, f32[128]{0:T(128)}, u32[]{:S(2)}) copy-start(f32[128]{0:T(128)} %constant.75.clone) | copy-start | bytes 1540
  1.3 14.2 %copy-start.2 = (f32[128,256]{1,0:T(8,128)S(1)}, f32[128,256]{1,0:T(8,128)}, u32[]{:S(2)}) copy-start(f32[128,256]{1,0:T(8,128)} %constant.76.clone) | copy-start | bytes 393220
  1.8 16.4 %collective-permute-start.1 = (f32[8,640]{1,0:T(8,128)S(1)}, f32[8,640]{1,0:T(8,128)S(1)}, u32[]{:S(2)}, u32[]{:S(2)}) collective-permute-start(f32[8,640]{1,0:T(8,128)S(1)} %maximum_bitcast_fusion.1), channel_id=1, source_target_pairs={{2,0},{4,2},{6,4},{8,6},{10,8},{12,10},{14,12},{0,14},{3,1},{5,3},... | collective-permute-start | bytes 61448 | tf_op jit(solution)/shard_map/ppermute | solution.py:96
  13.4 3.0 %copy-start.11 = (s32[256]{0:T(256)S(1)}, s32[256]{0:T(256)}, u32[]{:S(2)}) copy-start(s32[256]{0:T(256)} %param.14) | copy-start | bytes 3076
  13.4 3.1 %copy-start.6 = (s32[256,1]{0,1:T(1,128)S(1)}, s32[256,1]{0,1:T(1,128)}, u32[]{:S(2)}) copy-start(s32[256,1]{0,1:T(1,128)} %param.15) | copy-start | bytes 3076
  13.6 5.7 %collective-permute-start = (f32[8,640]{1,0:T(8,128)S(1)}, f32[8,640]{1,0:T(8,128)S(1)}, u32[]{:S(2)}, u32[]{:S(2)}) collective-permute-start(f32[8,640]{1,0:T(8,128)S(1)} %maximum_bitcast_fusion), channel_id=1, source_target_pairs={{0,2},{2,4},{4,6},{6,8},{8,10},{10,12},{12,14},{14,0},{1,3},{3,5},... | collective-permute-start | bytes 61448 | tf_op jit(solution)/shard_map/ppermute | solution.py:95
  15.5 1.9 %copy-start.1 = (f32[3,8,16,128]{3,2,1,0:T(8,128)S(1)}, f32[3,8,16,128]{3,2,1,0:T(8,128)}, u32[]{:S(2)}) copy-start(f32[3,8,16,128]{3,2,1,0:T(8,128)} %param.12) | copy-start | bytes 589828
  15.5 1.9 %copy-start.9 = (f32[3,5,5]{2,0,1:T(4,128)S(1)}, f32[3,5,5]{2,0,1:T(4,128)}, u32[]{:S(2)}) copy-start(f32[3,5,5]{2,0,1:T(4,128)} %param.13) | copy-start | bytes 904
  15.5 2.6 %copy-start.12 = (s32[256]{0:T(256)S(1)}, s32[256]{0:T(256)}, u32[]{:S(2)}) copy-start(s32[256]{0:T(256)} %param.16) | copy-start | bytes 3076
  16.4 1.8 %copy-start.8 = (f32[8,256]{1,0:T(8,128)S(1)}, f32[8,256]{1,0:T(8,128)}, u32[]{:S(2)}) copy-start(f32[8,256]{1,0:T(8,128)} %constant.78.clone) | copy-start | bytes 24580
  16.5 2.8 %copy-start.7 = (f32[8,256]{1,0:T(8,128)S(1)}, f32[8,256]{1,0:T(8,128)}, u32[]{:S(2)}) copy-start(f32[8,256]{1,0:T(8,128)} %constant.77.clone) | copy-start | bytes 24580
  22.9 18.4 %all-to-all-start = ((f32[32,1,192]{2,1,0:T(1,128)}), f32[32,1,192]{2,1,0:T(1,128)S(1)}, u32[]{:S(2)}, u32[]{:S(2)}) async-start(f32[32,1,192]{2,1,0:T(1,128)} %all_to_all.11), calls=%async_computation | async-start | bytes 65536 | tf_op jit(solution)/shard_map/all_to_all | solution.py:124
  41.3 13.9 %collective-permute-start.4 = (f32[5,8,128]{2,1,0:T(8,128)S(1)}, f32[5,8,128]{2,1,0:T(8,128)S(1)}, u32[]{:S(2)}, u32[]{:S(2)}) collective-permute-start(f32[5,8,128]{2,1,0:T(8,128)S(1)} %broadcast_select_fusion.2), channel_id=1, source_target_pairs={{0,1},{1,0},{2,3},{3,2},{4,5},{5,4},{6,7},{7,6},{8,9},{9,8},{10,11... | collective-permute-start | bytes 61448 | tf_op jit(solution)/shard_map/ppermute | solution.py:134
  46.8 8.5 %collective-permute-start.2 = (f32[5,16,128]{2,1,0:T(8,128)S(1)}, f32[5,16,128]{2,1,0:T(8,128)S(1)}, u32[]{:S(2)}, u32[]{:S(2)}) collective-permute-start(f32[5,16,128]{2,1,0:T(8,128)S(1)} %get-tuple-element.10), channel_id=1, source_target_pairs={{16,0},{32,16},{48,32},{64,48},{80,64},{96,80},{112,96},{128,112},... | collective-permute-start | bytes 122888 | tf_op jit(solution)/shard_map/ppermute | solution.py:131
  48.1 7.3 %collective-permute-start.3 = (f32[5,16,128]{2,1,0:T(8,128)S(1)}, f32[5,16,128]{2,1,0:T(8,128)S(1)}, u32[]{:S(2)}, u32[]{:S(2)}) collective-permute-start(f32[5,16,128]{2,1,0:T(8,128)S(1)} %get-tuple-element.11), channel_id=1, source_target_pairs={{0,16},{16,32},{32,48},{48,64},{64,80},{80,96},{96,112},{112,128},... | collective-permute-start | bytes 122888 | tf_op jit(solution)/shard_map/ppermute | solution.py:130
  52.9 0.7 %copy-start.10 = (s32[1024]{0:T(1024)S(1)}, s32[1024]{0:T(1024)}, u32[]{:S(2)}) copy-start(s32[1024]{0:T(1024)} %get-tuple-element.39) | copy-start | bytes 12292
  55.3 0.7 %copy-start.5 = (f32[1,5,5]{2,0,1:T(1,128)S(1)}, f32[1,5,5]{2,0,1:T(1,128)}, u32[]{:S(2)}) copy-start(f32[1,5,5]{2,0,1:T(1,128)} %get-tuple-element.36) | copy-start | bytes 304
  55.4 1.3 %copy-start.4 = (f32[1,5,5]{2,0,1:T(1,128)S(1)}, f32[1,5,5]{2,0,1:T(1,128)}, u32[]{:S(2)}) copy-start(f32[1,5,5]{2,0,1:T(1,128)} %get-tuple-element.35) | copy-start | bytes 304
  56.8 1.0 %copy-start.3 = (f32[1,5,5]{2,0,1:T(1,128)S(1)}, f32[1,5,5]{2,0,1:T(1,128)}, u32[]{:S(2)}) copy-start(f32[1,5,5]{2,0,1:T(1,128)} %get-tuple-element.34) | copy-start | bytes 304

commit v6 on v4

--- a/solution.py
+++ b/solution.py
@@ -116,11 +116,9 @@
     slot_rank = jnp.sum(onehot * (jnp.cumsum(onehot, axis=0) - 1), axis=1)
     slot_place = owner_rows * capacity + slot_rank
     packed = jnp.concatenate([source, donor_cell.astype(jnp.float32)[None, :]], axis=0)
-    slots = (
-        slot_place[:, None, None]
-        == (jnp.arange(owners, dtype=jnp.int32)[:, None] * capacity + jnp.arange(capacity, dtype=jnp.int32))[None]
-    ).astype(jnp.float32)
-    outbox = jnp.einsum("pt,tos->ops", packed, slots, precision=HI).reshape(owners, (fields + 1) * capacity)
+    by_rank = (slot_rank[None, :] == jnp.arange(capacity, dtype=jnp.int32)[:, None]).astype(jnp.float32)
+    spread_out = (packed[:, None, :] * by_rank[None]).reshape((fields + 1) * capacity, -1)
+    outbox = jnp.einsum("qt,to->oq", spread_out, onehot.astype(jnp.float32), precision=HI)
     received = lax.all_to_all(outbox, "gx", split_axis=0, concat_axis=0, tiled=True)
     taken = jnp.einsum("nk,fna->fka", t_rows, -source[:, :, None] * t_lanes[None], precision=HI)
     up_x, down_x = neighbours(filtered, "gx", False)
@@ -142,11 +140,17 @@
     along_r = jnp.concatenate([filtered[:, :, 1:], after_r], axis=2) - jnp.concatenate(
         [before_r, filtered[:, :, :-1]], axis=2
     )
-    gradient = filtered
-    for direction, change in enumerate((along_x, along_r, along_a)):
-        mixing = jnp.einsum("fg,fxra->gxra", flux[direction], change, precision=HI)
-        gradient = gradient + coeff[direction][None] * mixing
-    gradient = gradient + taken.reshape(adjoint.shape)
+    changes = (along_x, along_r, along_a)
+    out_fields = []
+    for g in range(fields):
+        total = filtered[g] + taken[g].reshape(rows_x, rows_r, cells_a)
+        for direction, change in enumerate(changes):
+            mixing = flux[direction, 0, g] * change[0]
+            for f in range(1, fields):
+                mixing = mixing + flux[direction, f, g] * change[f]
+            total = total + coeff[direction] * mixing
+        out_fields.append(total)
+    gradient = jnp.stack(out_fields)
 
     received = received.reshape(owners, fields + 1, capacity).transpose(1, 0, 2).reshape(fields + 1, owners * capacity)
     got_cell = received[fields].astype(jnp.int32)

time: 56.6 us -> 96.2 us (1.70)
  other arithmetic: 1.65 us -> 49.6 us
  waiting for transfers between devices: 7 us -> 0.02 us
  matrix products: 8.38 us -> 4.97 us
  local copies, waits for them, and re-layouts: 4.61 us -> 7 us
  starting transfers between devices: 34.2 us -> 33.1 us
    unnamed x0 -> x4, other arithmetic: none -> 37.8 us
    another operation x2 -> x3, other arithmetic: 0.63 us -> 10.1 us  [the longest x1 9.47 us: shards(): gradient = jnp.stack(out_fields)]
    all_to_all x1, waiting for transfers between devices: 6.06 us -> 0.01 us  [shards(): lax.all_to_all(outbox, 'gx', split_axis=0, concat_axis=0, tiled=True)]
    dot_general x4 -> x1, matrix products: 3.7 us -> 0.29 us  [shards(): jnp.einsum('qt,to->oq', spread_out, onehot.astype(jnp.float32), precision...]
    slice x3 -> x7, local copies, waits for them, and re-layouts: 0.25 us -> 3.1 us  [the longest x2 1.45 us: shards(): mixing = mixing + flux[direction, f, g] * change[f]]
    ppermute x1, starting transfers between devices: 4.02 us -> 2.86 us  [shards(): lax.ppermute(jnp.where(band == 0, last_r, first_r), 'row', [(0, 1), (1, 0)])]
  transfers between devices with their start and end apart: 6 -> 6, of which waited for: 2 -> 0; matrix products, arithmetic and copies ran while one was open for 13% -> 58% of each run, Pallas kernels for 0% -> 0%
where the time goes in v6:
time: 96.2 us; the launch traced here: 95.2 us
  other arithmetic  49.6 us (52%)
  starting transfers between devices  33.1 us (34%)
  local copies, waits for them, and re-layouts  7 us (7%)
  matrix products  4.97 us (5%)
    unnamed x4, other arithmetic  37.8 us
    all_to_all x1, starting transfers between devices, shards(): lax.all_to_all(outbox, 'gx', split_axis=0, concat_axis=0, tiled=True)  11.5 us
    ppermute x1, starting transfers between devices, shards(): from_right = lax.ppermute(to_left, 'az', down)  11.5 us
    another operation x1, other arithmetic, shards(): gradient = jnp.stack(out_fields)  9.47 us
    ppermute x1, starting transfers between devices, shards(): before_x = lax.ppermute(last_x, 'gx', up_x)[:, None]  3.99 us
    ppermute x1, starting transfers between devices, shards(): lax.ppermute(jnp.where(band == 0, last_r, first_r), 'row', [(0, 1), (1, 0)])  2.86 us
  transfers between devices with their start and end apart: 6, of which 0 were waited for; matrix products, arithmetic and copies ran while one was open for 58% of the time, Pallas kernels for 0%

profile of v6, /device:TPU:1, one launch (start us, length us, event | category | flops | bytes accessed | tf_op | source)
XLA Modules:
  0.0 95.2 jit_solution(6385941946073397035)
XLA Ops:
  0.0 1.3 %fusion.55 = (f32[640,7]{1,0:T(8,128)S(1)}, f32[640,7]{1,0:T(8,128)S(1)}) fusion(f32[640,128]{1,0:T(8,128)} %bitcast.167), kind=kLoop, calls=%fused_computation.100 | loop fusion | bytes 71680 | tf_op jit(solution)/shard_map/slice | solution.py:90
  1.3 0.1 copy.68
  1.5 0.2 multiply_reduce_fusion.1
  1.8 11.5 %collective-permute-start.1 = (f32[8,640]{1,0:T(8,128)S(1)}, f32[8,640]{1,0:T(8,128)S(1)}, u32[]{:S(2)}, u32[]{:S(2)}) collective-permute-start(f32[8,640]{1,0:T(8,128)S(1)} %maximum_bitcast_fusion.1), channel_id=1, source_target_pairs={{2,0},{4,2},{6,4},{8,6},{10,8},{12,10},{14,12},{0,14},{3,1},{5,3},... | collective-permute-start | bytes 61448 | tf_op jit(solution)/shard_map/ppermute | solution.py:96
  13.6 1.9 %collective-permute-start = (f32[8,640]{1,0:T(8,128)S(1)}, f32[8,640]{1,0:T(8,128)S(1)}, u32[]{:S(2)}, u32[]{:S(2)}) collective-permute-start(f32[8,640]{1,0:T(8,128)S(1)} %maximum_bitcast_fusion), channel_id=1, source_target_pairs={{0,2},{2,4},{4,6},{6,8},{8,10},{10,12},{12,14},{14,0},{1,3},{3,5},... | collective-permute-start | bytes 61448 | tf_op jit(solution)/shard_map/ppermute | solution.py:95
  15.5 0.7 fusion.58
  16.3 0.7 fusion.57
  17.0 0.7 fusion.56
  17.7 0.9 convolution_bitcast_fusion.1
  18.7 0.6 reduce-window.6
  19.3 0.2 slice_reduce_fusion
  19.6 0.7 fusion.59
  20.4 0.7 fusion.60
  21.1 0.7 fusion.4
  21.9 0.2 copy.70
  22.3 2.9 %collective-permute-start.4 = (f32[5,8,128]{2,1,0:T(8,128)S(1)}, f32[5,8,128]{2,1,0:T(8,128)S(1)}, u32[]{:S(2)}, u32[]{:S(2)}) collective-permute-start(f32[5,8,128]{2,1,0:T(8,128)S(1)} %select_bitcast_fusion), channel_id=1, source_target_pairs={{0,1},{1,0},{2,3},{3,2},{4,5},{5,4},{6,7},{7,6},{8,9},{9,8},{10,11... | collective-permute-start | bytes 61448 | tf_op jit(solution)/shard_map/ppermute | solution.py:130
  25.2 1.3 %collective-permute-start.2 = (f32[5,16,128]{2,1,0:T(8,128)S(1)}, f32[5,16,128]{2,1,0:T(8,128)S(1)}, u32[]{:S(2)}, u32[]{:S(2)}) collective-permute-start(f32[5,16,128]{2,1,0:T(8,128)S(1)} %get-tuple-element.8), channel_id=1, source_target_pairs={{16,0},{32,16},{48,32},{64,48},{80,64},{96,80},{112,96},{128,112},... | collective-permute-start | bytes 122888 | tf_op jit(solution)/shard_map/ppermute | solution.py:127
  26.5 4.0 %collective-permute-start.3 = (f32[5,16,128]{2,1,0:T(8,128)S(1)}, f32[5,16,128]{2,1,0:T(8,128)S(1)}, u32[]{:S(2)}, u32[]{:S(2)}) collective-permute-start(f32[5,16,128]{2,1,0:T(8,128)S(1)} %get-tuple-element.7), channel_id=1, source_target_pairs={{0,16},{16,32},{32,48},{48,64},{64,80},{80,96},{96,112},{112,128},... | collective-permute-start | bytes 122888 | tf_op jit(solution)/shard_map/ppermute | solution.py:126
  30.5 0.5 fusion.6
  31.0 0.5 convolution_bitcast_fusion.2
  31.6 0.3 convolution_bitcast_fusion.3
  31.9 0.6 copy.80
  32.5 11.5 %all-to-all-start = ((f32[32,1,192]{2,1,0:T(1,128)}), f32[32,1,192]{2,1,0:T(1,128)S(1)}, u32[]{:S(2)}, u32[]{:S(2)}) async-start(f32[32,1,192]{2,1,0:T(1,128)} %copy.80), calls=%async_computation | async-start | bytes 65536 | tf_op jit(solution)/shard_map/all_to_all | solution.py:122
  44.2 0.8 copy-done.1
  45.1 9.5 %fusion.37 = f32[5,8,16,128]{3,2,1,0:T(8,128)S(1)} fusion(f32[1,8,16,128]{3,2,1,0:T(8,128)S(1)} %bitcast.178, f32[5,8,16,256]{3,2,1,0:T(8,128)S(1)} %bitcast.162, f32[5,8,16,128]{3,2,1,0:T(8,128)S(1)} %maximum_subtract_fusion.1, f32[5,8,16,128]{3,2,1,0:T(8,128)S(1)} %maximum_subtract_fusion, f32[3,8,16,128]{3,2,1,0:T(8,128)S(1)} %copy-done.1, f32[]{:T(128)} %bitcast.33, ...), kind=kLoop, calls=%fused_computation.53 | loop fusion | flops 557055 | bytes 1376316
  54.6 9.5 %fusion.33 = f32[5,8,16,128]{3,2,1,0:T(8,128)S(1)} fusion(f32[5,8,16,128]{3,2,1,0:T(8,128)S(1)} %fusion.37, f32[1,8,16,128]{3,2,1,0:T(8,128)S(1)} %bitcast.177, f32[5,8,16,256]{3,2,1,0:T(8,128)S(1)} %bitcast.163, f32[5,8,16,128]{3,2,1,0:T(8,128)S(1)} %maximum_subtract_fusion.1, f32[5,8,16,128]{3,2,1,0:T(8,128)S(1)} %maximum_subtract_fusion, ...), kind=kLoop, calls=%fused_computation.48 | loop fusion | flops 557056 | bytes 1376316
  64.0 9.5 %fusion.29 = f32[5,8,16,128]{3,2,1,0:T(8,128)S(1)} fusion(f32[5,8,16,128]{3,2,1,0:T(8,128)S(1)} %fusion.33, f32[1,8,16,128]{3,2,1,0:T(8,128)S(1)} %bitcast.176, f32[5,8,16,256]{3,2,1,0:T(8,128)S(1)} %bitcast.164, f32[5,8,16,128]{3,2,1,0:T(8,128)S(1)} %maximum_subtract_fusion.1, f32[5,8,16,128]{3,2,1,0:T(8,128)S(1)} %maximum_subtract_fusion, ...), kind=kLoop, calls=%fused_computation.43 | loop fusion | flops 557056 | bytes 1376316
  73.5 9.4 %fusion.25 = f32[5,8,16,128]{3,2,1,0:T(8,128)S(1)} fusion(f32[5,8,16,128]{3,2,1,0:T(8,128)S(1)} %fusion.29, f32[1,8,16,128]{3,2,1,0:T(8,128)S(1)} %bitcast.175, f32[5,8,16,256]{3,2,1,0:T(8,128)S(1)} %bitcast.165, f32[5,8,16,128]{3,2,1,0:T(8,128)S(1)} %maximum_subtract_fusion.1, f32[5,8,16,128]{3,2,1,0:T(8,128)S(1)} %maximum_subtract_fusion, ...), kind=kLoop, calls=%fused_computation.38 | loop fusion | flops 557056 | bytes 1376316
  82.9 9.5 %fusion.21 = f32[5,8,16,128]{3,2,1,0:T(8,128)S(1)} fusion(f32[5,8,16,128]{3,2,1,0:T(8,128)S(1)} %fusion.25, f32[1,8,16,128]{3,2,1,0:T(8,128)S(1)} %bitcast.174, f32[5,8,16,256]{3,2,1,0:T(8,128)S(1)} %bitcast.166, f32[5,8,16,128]{3,2,1,0:T(8,128)S(1)} %maximum_subtract_fusion.1, f32[5,8,16,128]{3,2,1,0:T(8,128)S(1)} %maximum_subtract_fusion, ...), kind=kLoop, calls=%fused_computation.33 | loop fusion | flops 557056 | bytes 1376316 | tf_op jit(solution)/shard_map/stack | solution.py:153
  92.7 0.2 fusion.8
  93.1 1.4 %fusion = f32[5,128,128]{1,2,0:T(8,128)S(1)} fusion(f32[1024,128]{1,0:T(8,128)S(1)} %fusion.8, f32[5,1024]{1,0:T(8,128)S(1)} %mul.847, s32[1024]{0:T(1024)S(1)} %get-tuple-element.101), kind=kOutput, calls=%fused_computation | convolution fusion | flops 1007419392 | bytes 876544 | tf_op jit(solution)/shard_map/nk,fna->fka/dot_general | solution.py:160
  94.4 0.8 add.442
  (60 shorter events, 1.4 us)
Async XLA Ops:
  0.0 1.4 %copy-start = (f32[5,8,16,128]{3,2,1,0:T(8,128)S(1)}, f32[5,8,16,128]{3,2,1,0:T(8,128)}, u32[]{:S(2)}) copy-start(f32[5,8,16,128]{3,2,1,0:T(8,128)} %param.11) | copy-start | bytes 983044
  0.0 1.4 %copy-start.9 = (f32[128]{0:T(128)S(1)}, f32[128]{0:T(128)}, u32[]{:S(2)}) copy-start(f32[128]{0:T(128)} %constant.71.clone) | copy-start | bytes 1540
  0.0 1.4 %copy-start.10 = (f32[128]{0:T(128)S(1)}, f32[128]{0:T(128)}, u32[]{:S(2)}) copy-start(f32[128]{0:T(128)} %constant.72.clone) | copy-start | bytes 1540
  1.3 14.2 %copy-start.2 = (f32[3,5,5]{2,0,1:T(4,128)S(1)}, f32[3,5,5]{2,0,1:T(4,128)}, u32[]{:S(2)}) copy-start(f32[3,5,5]{2,0,1:T(4,128)} %param.13) | copy-start | bytes 904
  1.3 16.4 %copy-start.3 = (f32[128,256]{1,0:T(8,128)S(1)}, f32[128,256]{1,0:T(8,128)}, u32[]{:S(2)}) copy-start(f32[128,256]{1,0:T(8,128)} %constant.73.clone) | copy-start | bytes 393220
  1.8 18.5 %collective-permute-start.1 = (f32[8,640]{1,0:T(8,128)S(1)}, f32[8,640]{1,0:T(8,128)S(1)}, u32[]{:S(2)}, u32[]{:S(2)}) collective-permute-start(f32[8,640]{1,0:T(8,128)S(1)} %maximum_bitcast_fusion.1), channel_id=1, source_target_pairs={{2,0},{4,2},{6,4},{8,6},{10,8},{12,10},{14,12},{0,14},{3,1},{5,3},... | collective-permute-start | bytes 61448 | tf_op jit(solution)/shard_map/ppermute | solution.py:96
  13.4 5.2 %copy-start.7 = (s32[256]{0:T(256)S(1)}, s32[256]{0:T(256)}, u32[]{:S(2)}) copy-start(s32[256]{0:T(256)} %param.14) | copy-start | bytes 3076
  13.6 5.1 %copy-start.4 = (s32[256,1]{0,1:T(1,128)S(1)}, s32[256,1]{0,1:T(1,128)}, u32[]{:S(2)}) copy-start(s32[256,1]{0,1:T(1,128)} %param.15) | copy-start | bytes 3076
  13.6 7.5 %collective-permute-start = (f32[8,640]{1,0:T(8,128)S(1)}, f32[8,640]{1,0:T(8,128)S(1)}, u32[]{:S(2)}, u32[]{:S(2)}) collective-permute-start(f32[8,640]{1,0:T(8,128)S(1)} %maximum_bitcast_fusion), channel_id=1, source_target_pairs={{0,2},{2,4},{4,6},{6,8},{8,10},{10,12},{12,14},{14,0},{1,3},{3,5},... | collective-permute-start | bytes 61448 | tf_op jit(solution)/shard_map/ppermute | solution.py:95
  17.7 2.6 %copy-start.8 = (s32[256]{0:T(256)S(1)}, s32[256]{0:T(256)}, u32[]{:S(2)}) copy-start(s32[256]{0:T(256)} %param.16) | copy-start | bytes 3076
  17.7 2.6 %copy-start.6 = (f32[8,256]{1,0:T(8,128)S(1)}, f32[8,256]{1,0:T(8,128)}, u32[]{:S(2)}) copy-start(f32[8,256]{1,0:T(8,128)} %constant.75.clone) | copy-start | bytes 24580
  18.6 2.5 %copy-start.5 = (f32[8,256]{1,0:T(8,128)S(1)}, f32[8,256]{1,0:T(8,128)}, u32[]{:S(2)}) copy-start(f32[8,256]{1,0:T(8,128)} %constant.74.clone) | copy-start | bytes 24580
  22.3 21.7 %collective-permute-start.4 = (f32[5,8,128]{2,1,0:T(8,128)S(1)}, f32[5,8,128]{2,1,0:T(8,128)S(1)}, u32[]{:S(2)}, u32[]{:S(2)}) collective-permute-start(f32[5,8,128]{2,1,0:T(8,128)S(1)} %select_bitcast_fusion), channel_id=1, source_target_pairs={{0,1},{1,0},{2,3},{3,2},{4,5},{5,4},{6,7},{7,6},{8,9},{9,8},{10,11... | collective-permute-start | bytes 61448 | tf_op jit(solution)/shard_map/ppermute | solution.py:130
  25.2 19.0 %collective-permute-start.2 = (f32[5,16,128]{2,1,0:T(8,128)S(1)}, f32[5,16,128]{2,1,0:T(8,128)S(1)}, u32[]{:S(2)}, u32[]{:S(2)}) collective-permute-start(f32[5,16,128]{2,1,0:T(8,128)S(1)} %get-tuple-element.8), channel_id=1, source_target_pairs={{16,0},{32,16},{48,32},{64,48},{80,64},{96,80},{112,96},{128,112},... | collective-permute-start | bytes 122888 | tf_op jit(solution)/shard_map/ppermute | solution.py:127
  26.5 17.7 %collective-permute-start.3 = (f32[5,16,128]{2,1,0:T(8,128)S(1)}, f32[5,16,128]{2,1,0:T(8,128)S(1)}, u32[]{:S(2)}, u32[]{:S(2)}) collective-permute-start(f32[5,16,128]{2,1,0:T(8,128)S(1)} %get-tuple-element.7), channel_id=1, source_target_pairs={{0,16},{16,32},{32,48},{48,64},{64,80},{80,96},{96,112},{112,128},... | collective-permute-start | bytes 122888 | tf_op jit(solution)/shard_map/ppermute | solution.py:126
  32.5 59.9 %all-to-all-start = ((f32[32,1,192]{2,1,0:T(1,128)}), f32[32,1,192]{2,1,0:T(1,128)S(1)}, u32[]{:S(2)}, u32[]{:S(2)}) async-start(f32[32,1,192]{2,1,0:T(1,128)} %copy.80), calls=%async_computation | async-start | bytes 65536 | tf_op jit(solution)/shard_map/all_to_all | solution.py:122
  44.2 0.9 copy-start.1

commit v7 on v4

--- a/solution.py
+++ b/solution.py
@@ -116,11 +116,9 @@
     slot_rank = jnp.sum(onehot * (jnp.cumsum(onehot, axis=0) - 1), axis=1)
     slot_place = owner_rows * capacity + slot_rank
     packed = jnp.concatenate([source, donor_cell.astype(jnp.float32)[None, :]], axis=0)
-    slots = (
-        slot_place[:, None, None]
-        == (jnp.arange(owners, dtype=jnp.int32)[:, None] * capacity + jnp.arange(capacity, dtype=jnp.int32))[None]
-    ).astype(jnp.float32)
-    outbox = jnp.einsum("pt,tos->ops", packed, slots, precision=HI).reshape(owners, (fields + 1) * capacity)
+    by_rank = (slot_rank[None, :] == jnp.arange(capacity, dtype=jnp.int32)[:, None]).astype(jnp.float32)
+    spread_out = (packed[:, None, :] * by_rank[None]).reshape((fields + 1) * capacity, -1)
+    outbox = jnp.einsum("qt,to->oq", spread_out, onehot.astype(jnp.float32), precision=HI)
     received = lax.all_to_all(outbox, "gx", split_axis=0, concat_axis=0, tiled=True)
     taken = jnp.einsum("nk,fna->fka", t_rows, -source[:, :, None] * t_lanes[None], precision=HI)
     up_x, down_x = neighbours(filtered, "gx", False)

time: 56.6 us -> 55.9 us (0.988)
  matrix products: 8.38 us -> 7.47 us
    dot_general x1, matrix products: 1.19 us -> 0.29 us  [shards(): jnp.einsum('qt,to->oq', spread_out, onehot.astype(jnp.float32), precision...]
  transfers between devices with their start and end apart: 6 -> 6, of which waited for: 2 -> 2; matrix products, arithmetic and copies ran while one was open for 13% -> 12% of each run, Pallas kernels for 0% -> 0%
where the time goes in v7:
time: 55.9 us; the launch traced here: 55.6 us
  starting transfers between devices  34.4 us (62%)
  matrix products  7.47 us (13%)
  waiting for transfers between devices  7.12 us (13%)
  local copies, waits for them, and re-layouts  4.52 us (8%)
  other arithmetic  1.6 us (3%)
    all_to_all x1, starting transfers between devices, shards(): lax.all_to_all(outbox, 'gx', split_axis=0, concat_axis=0, tiled=True)  11.5 us
    ppermute x1, starting transfers between devices, shards(): from_right = lax.ppermute(to_left, 'az', down)  11.5 us
    all_to_all x1, waiting for transfers between devices, shards(): lax.all_to_all(outbox, 'gx', split_axis=0, concat_axis=0, tiled=True)  6.06 us
    ppermute x1, starting transfers between devices, shards(): lax.ppermute(jnp.where(band == 0, last_r, first_r), 'row', [(0, 1), (1, 0)])  4.01 us
    ppermute x1, starting transfers between devices, shards(): before_x = lax.ppermute(last_x, 'gx', up_x)[:, None]  3.99 us
    dot_general x3, matrix products, shards(): mixing = jnp.einsum('fg,fxra->gxra', flux[direction], change, precision=HI)  2.51 us
    ppermute x1, starting transfers between devices, shards(): from_left = lax.ppermute(to_right, 'az', up)  2.05 us
    slice x2, local copies, waits for them, and re-layouts, shards(): lines[:, cells_a - EDGE:]  1.39 us
  transfers between devices with their start and end apart: 6, of which 2 were waited for; matrix products, arithmetic and copies ran while one was open for 12% of the time, Pallas kernels for 0%

profile of v7, /device:TPU:1, one launch (start us, length us, event | category | flops | bytes accessed | tf_op | source)
XLA Modules:
  0.0 55.6 jit_solution(694025999111617743)
XLA Ops:
  0.0 1.3 %fusion.48 = (f32[640,7]{1,0:T(8,128)S(1)}, f32[640,7]{1,0:T(8,128)S(1)}) fusion(f32[640,128]{1,0:T(8,128)} %bitcast.119), kind=kLoop, calls=%fused_computation.96 | loop fusion | bytes 71680 | tf_op jit(solution)/shard_map/slice | solution.py:90
  1.3 0.1 copy.95
  1.4 0.2 multiply_reduce_fusion.1
  1.8 11.5 %collective-permute-start.1 = (f32[8,640]{1,0:T(8,128)S(1)}, f32[8,640]{1,0:T(8,128)S(1)}, u32[]{:S(2)}, u32[]{:S(2)}) collective-permute-start(f32[8,640]{1,0:T(8,128)S(1)} %maximum_bitcast_fusion.1), channel_id=1, source_target_pairs={{2,0},{4,2},{6,4},{8,6},{10,8},{12,10},{14,12},{0,14},{3,1},{5,3},... | collective-permute-start | bytes 61448 | tf_op jit(solution)/shard_map/ppermute | solution.py:96
  13.3 0.1 copy.93
  13.4 0.1 broadcast_in_dim.18
  13.6 2.1 %collective-permute-start = (f32[8,640]{1,0:T(8,128)S(1)}, f32[8,640]{1,0:T(8,128)S(1)}, u32[]{:S(2)}, u32[]{:S(2)}) collective-permute-start(f32[8,640]{1,0:T(8,128)S(1)} %maximum_bitcast_fusion), channel_id=1, source_target_pairs={{0,2},{2,4},{4,6},{6,8},{8,10},{10,12},{12,14},{14,0},{1,3},{3,5},... | collective-permute-start | bytes 61448 | tf_op jit(solution)/shard_map/ppermute | solution.py:95
  15.7 0.9 %convolution_bitcast_fusion.1 = f32[640,256]{0,1:T(8,128)S(1)} fusion(f32[128,256]{1,0:T(8,128)S(1)} %copy-done.2, f32[640,128]{1,0:T(8,128)S(1)} %bitcast.120), kind=kOutput, calls=%fused_computation.8 | convolution fusion | flops 251658240 | bytes 1114112 | tf_op jit(solution)/shard_map/lc,co->lo/dot_general | solution.py:97
  16.7 0.6 %reduce-window.6 = s32[32,2,128]{2,0,1:T(8,128)S(1)} reduce-window(s32[32,2,128]{2,0,1:T(8,128)S(1)} %fusion.37, s32[]{:T(128)} %constant.64.clone.1), window={size=1x1x128 pad=0_0x0_0x127_0}, to_apply=%region_3.4 | reduce-window | flops 1040384 | bytes 65540 | tf_op jit(solution)/shard_map/reduce-window
  17.3 0.2 slice_reduce_fusion
  17.5 0.1 fusion.34
  17.7 0.7 %fusion.50 = f32[640,256]{0,1:T(8,128)S(1)} fusion(f32[8,640]{1,0:T(8,128)S(1)} %collective-permute-done.1, f32[8,256]{1,0:T(8,128)S(1)} %copy-done.5), kind=kOutput, calls=%fused_computation.98 | convolution fusion | flops 15728640 | bytes 684032 | tf_op jit(solution)/shard_map/kl,ko->lo/dot_general | solution.py:99
  18.4 1.1 %collective-permute-done = f32[8,640]{1,0:T(8,128)S(1)} collective-permute-done((f32[8,640]{1,0:T(8,128)S(1)}, f32[8,640]{1,0:T(8,128)S(1)}, u32[]{:S(2)}, u32[]{:S(2)}) %collective-permute-start) | collective-permute-done | bytes 20512 | tf_op jit(solution)/shard_map/ppermute | solution.py:95
  19.5 0.7 %fusion.4 = f32[640,256]{0,1:T(8,128)S(1)} fusion(f32[640,256]{0,1:T(8,128)S(1)} %fusion.50, f32[640,256]{0,1:T(8,128)S(1)} %convolution_bitcast_fusion.1, f32[8,640]{1,0:T(8,128)S(1)} %collective-permute-done, f32[8,256]{1,0:T(8,128)S(1)} %copy-done.4), kind=kOutput, calls=%fused_computation.5 | convolution fusion | flops 16056320 | bytes 1994752 | tf_op jit(solution)/shard_map/kl,ko->lo/dot_general | solution.py:98
  20.2 0.2 copy.97
  20.7 4.0 %collective-permute-start.4 = (f32[5,8,128]{2,1,0:T(8,128)S(1)}, f32[5,8,128]{2,1,0:T(8,128)S(1)}, u32[]{:S(2)}, u32[]{:S(2)}) collective-permute-start(f32[5,8,128]{2,1,0:T(8,128)S(1)} %select_bitcast_fusion), channel_id=1, source_target_pairs={{0,1},{1,0},{2,3},{3,2},{4,5},{5,4},{6,7},{7,6},{8,9},{9,8},{10,11... | collective-permute-start | bytes 61448 | tf_op jit(solution)/shard_map/ppermute | solution.py:130
  24.7 1.3 %collective-permute-start.2 = (f32[5,16,128]{2,1,0:T(8,128)S(1)}, f32[5,16,128]{2,1,0:T(8,128)S(1)}, u32[]{:S(2)}, u32[]{:S(2)}) collective-permute-start(f32[5,16,128]{2,1,0:T(8,128)S(1)} %get-tuple-element.14), channel_id=1, source_target_pairs={{16,0},{32,16},{48,32},{64,48},{80,64},{96,80},{112,96},{128,112},... | collective-permute-start | bytes 122888 | tf_op jit(solution)/shard_map/ppermute | solution.py:127
  26.0 4.0 %collective-permute-start.3 = (f32[5,16,128]{2,1,0:T(8,128)S(1)}, f32[5,16,128]{2,1,0:T(8,128)S(1)}, u32[]{:S(2)}, u32[]{:S(2)}) collective-permute-start(f32[5,16,128]{2,1,0:T(8,128)S(1)} %get-tuple-element.13), channel_id=1, source_target_pairs={{0,16},{16,32},{32,48},{48,64},{64,80},{80,96},{96,112},{112,128},... | collective-permute-start | bytes 122888 | tf_op jit(solution)/shard_map/ppermute | solution.py:126
  30.0 0.5 fusion.13
  30.6 0.3 convolution_bitcast_fusion.3
  30.9 0.6 %copy.118 = f32[32,1,192]{2,1,0:T(1,128)} copy(f32[32,1,192]{2,0,1:T(8,128)S(1)} %convolution_bitcast_fusion.3) | data formatting | bytes 49152 | tf_op jit(solution)/shard_map/all_to_all | solution.py:122
  31.5 11.5 %all-to-all-start = ((f32[32,1,192]{2,1,0:T(1,128)}), f32[32,1,192]{2,1,0:T(1,128)S(1)}, u32[]{:S(2)}, u32[]{:S(2)}) async-start(f32[32,1,192]{2,1,0:T(1,128)} %copy.118), calls=%async_computation | async-start | bytes 65536 | tf_op jit(solution)/shard_map/all_to_all | solution.py:122
  43.0 0.5 convolution_bitcast_fusion.2
  43.5 0.2 copy.116
  44.0 0.8 %fusion.12 = f32[5,8,16,128]{3,0,2,1:T(8,128)S(1)} fusion(f32[5,8,16,128]{3,2,1,0:T(8,128)S(1)} %maximum_subtract_fusion, f32[8,16,128]{2,1,0:T(8,128)S(1)} %get-tuple-element.20, f32[1,5,5]{2,0,1:T(1,128)S(1)} %get-tuple-element.26), kind=kOutput, calls=%fused_computation.18 | convolution fusion | flops 4997120 | bytes 720996 | tf_op jit(solution)/shard_map/fg,fxra->gxra/dot_general | solution.py:145
  44.7 0.9 %fusion.11 = f32[5,8,16,128]{3,0,2,1:T(8,128)S(1)} fusion(f32[5,8,16,128]{3,0,2,1:T(8,128)S(1)} %fusion.12, f32[5,8,16,128]{3,2,1,0:T(8,128)S(1)} %get-tuple-element.8, f32[5,8,16,128]{3,2,1,0:T(8,128)S(1)} %maximum_subtract_fusion.1, f32[8,16,128]{2,1,0:T(8,128)S(1)} %get-tuple-element.21, f32[1,5,5]{2,0,1:T(1,128)S(1)} %get-tuple-element.25), kind=kOutput, calls=%fused_computation.16 | convolution fusion | flops 5160960 | bytes 1376356 | tf_op jit(solution)/shard_map/fg,fxra->gxra/dot_general | solution.py:145
  45.7 6.1 %all-to-all-done = f32[32,1,192]{2,1,0:T(1,128)S(1)} async-done(((f32[32,1,192]{2,1,0:T(1,128)}), f32[32,1,192]{2,1,0:T(1,128)S(1)}, u32[]{:S(2)}, u32[]{:S(2)}) %all-to-all-start) | async-done | bytes 24608 | tf_op jit(solution)/shard_map/all_to_all | solution.py:122
  52.0 0.2 fusion.21
  52.4 1.4 %fusion.14 = f32[5,128,128]{2,1,0:T(8,128)S(1)} fusion(f32[1024,128]{1,0:T(8,128)S(1)} %fusion.21, f32[5,1024]{1,0:T(8,128)S(1)} %mul.148, s32[1024]{0:T(1024)S(1)} %get-tuple-element.29), kind=kOutput, calls=%fused_computation.20 | convolution fusion | flops 1007419392 | bytes 876544 | tf_op jit(solution)/shard_map/nk,fna->fka/dot_general | solution.py:154
  53.8 0.2 copy.120
  54.0 0.8 %fusion.9 = f32[5,8,16,128]{3,0,2,1:T(8,128)S(1)} fusion(f32[5,8,16,128]{3,0,2,1:T(8,128)S(1)} %bitcast.123, f32[5,8,16,128]{3,0,2,1:T(8,128)S(1)} %bitcast.122, f32[5,8,16,128]{3,0,2,1:T(8,128)S(1)} %fusion.11, f32[5,8,16,128]{3,2,1,0:T(8,128)S(1)} %get-tuple-element.7, f32[8,16,128]{2,1,0:T(8,128)S(1)} %get-tuple-element.19, ...), kind=kOutput, calls=%fused_computation.13 | convolution fusion | flops 5242880 | bytes 1704036 | tf_op jit(solution)/shard_map/fg,fxra->gxra/dot_general | solution.py:145
  54.8 0.8 %copy.121 = f32[5,8,16,128]{3,2,1,0:T(8,128)} copy(f32[5,8,16,128]{3,0,2,1:T(8,128)S(1)} %fusion.9) | data formatting | bytes 655360 | tf_op jit(solution)/shard_map/add | solution.py:155
  (57 shorter events, 1.1 us)
Async XLA Ops:
  0.0 1.4 %copy-start = (f32[5,8,16,128]{3,2,1,0:T(8,128)S(1)}, f32[5,8,16,128]{3,2,1,0:T(8,128)}, u32[]{:S(2)}) copy-start(f32[5,8,16,128]{3,2,1,0:T(8,128)} %param.11) | copy-start | bytes 983044
  0.0 1.4 %copy-start.9 = (f32[128]{0:T(128)S(1)}, f32[128]{0:T(128)}, u32[]{:S(2)}) copy-start(f32[128]{0:T(128)} %constant.71.clone) | copy-start | bytes 1540
  0.0 1.4 %copy-start.10 = (f32[128]{0:T(128)S(1)}, f32[128]{0:T(128)}, u32[]{:S(2)}) copy-start(f32[128]{0:T(128)} %constant.72.clone) | copy-start | bytes 1540
  1.3 14.4 %copy-start.2 = (f32[128,256]{1,0:T(8,128)S(1)}, f32[128,256]{1,0:T(8,128)}, u32[]{:S(2)}) copy-start(f32[128,256]{1,0:T(8,128)} %constant.73.clone) | copy-start | bytes 393220
  1.8 15.9 %collective-permute-start.1 = (f32[8,640]{1,0:T(8,128)S(1)}, f32[8,640]{1,0:T(8,128)S(1)}, u32[]{:S(2)}, u32[]{:S(2)}) collective-permute-start(f32[8,640]{1,0:T(8,128)S(1)} %maximum_bitcast_fusion.1), channel_id=1, source_target_pairs={{2,0},{4,2},{6,4},{8,6},{10,8},{12,10},{14,12},{0,14},{3,1},{5,3},... | collective-permute-start | bytes 61448 | tf_op jit(solution)/shard_map/ppermute | solution.py:96
  13.4 3.1 %copy-start.1 = (f32[3,8,16,128]{3,2,1,0:T(8,128)S(1)}, f32[3,8,16,128]{3,2,1,0:T(8,128)}, u32[]{:S(2)}) copy-start(f32[3,8,16,128]{3,2,1,0:T(8,128)} %param.12) | copy-start | bytes 589828
  13.6 3.0 %copy-start.7 = (s32[256]{0:T(256)S(1)}, s32[256]{0:T(256)}, u32[]{:S(2)}) copy-start(s32[256]{0:T(256)} %param.14) | copy-start | bytes 3076
  13.6 3.1 %copy-start.3 = (s32[256,1]{0,1:T(1,128)S(1)}, s32[256,1]{0,1:T(1,128)}, u32[]{:S(2)}) copy-start(s32[256,1]{0,1:T(1,128)} %param.15) | copy-start | bytes 3076
  13.6 4.0 %copy-start.6 = (f32[3,5,5]{2,0,1:T(4,128)S(1)}, f32[3,5,5]{2,0,1:T(4,128)}, u32[]{:S(2)}) copy-start(f32[3,5,5]{2,0,1:T(4,128)} %param.13) | copy-start | bytes 904
  13.6 5.9 %collective-permute-start = (f32[8,640]{1,0:T(8,128)S(1)}, f32[8,640]{1,0:T(8,128)S(1)}, u32[]{:S(2)}, u32[]{:S(2)}) collective-permute-start(f32[8,640]{1,0:T(8,128)S(1)} %maximum_bitcast_fusion), channel_id=1, source_target_pairs={{0,2},{2,4},{4,6},{6,8},{8,10},{10,12},{12,14},{14,0},{1,3},{3,5},... | collective-permute-start | bytes 61448 | tf_op jit(solution)/shard_map/ppermute | solution.py:95
  16.5 1.1 %copy-start.8 = (s32[256]{0:T(256)S(1)}, s32[256]{0:T(256)}, u32[]{:S(2)}) copy-start(s32[256]{0:T(256)} %param.16) | copy-start | bytes 3076
  16.5 1.1 %copy-start.5 = (f32[8,256]{1,0:T(8,128)S(1)}, f32[8,256]{1,0:T(8,128)}, u32[]{:S(2)}) copy-start(f32[8,256]{1,0:T(8,128)} %constant.75.clone) | copy-start | bytes 24580
  16.6 2.9 %copy-start.4 = (f32[8,256]{1,0:T(8,128)S(1)}, f32[8,256]{1,0:T(8,128)}, u32[]{:S(2)}) copy-start(f32[8,256]{1,0:T(8,128)} %constant.74.clone) | copy-start | bytes 24580
  20.7 23.0 %collective-permute-start.4 = (f32[5,8,128]{2,1,0:T(8,128)S(1)}, f32[5,8,128]{2,1,0:T(8,128)S(1)}, u32[]{:S(2)}, u32[]{:S(2)}) collective-permute-start(f32[5,8,128]{2,1,0:T(8,128)S(1)} %select_bitcast_fusion), channel_id=1, source_target_pairs={{0,1},{1,0},{2,3},{3,2},{4,5},{5,4},{6,7},{7,6},{8,9},{9,8},{10,11... | collective-permute-start | bytes 61448 | tf_op jit(solution)/shard_map/ppermute | solution.py:130
  24.7 19.1 %collective-permute-start.2 = (f32[5,16,128]{2,1,0:T(8,128)S(1)}, f32[5,16,128]{2,1,0:T(8,128)S(1)}, u32[]{:S(2)}, u32[]{:S(2)}) collective-permute-start(f32[5,16,128]{2,1,0:T(8,128)S(1)} %get-tuple-element.14), channel_id=1, source_target_pairs={{16,0},{32,16},{48,32},{64,48},{80,64},{96,80},{112,96},{128,112},... | collective-permute-start | bytes 122888 | tf_op jit(solution)/shard_map/ppermute | solution.py:127
  26.0 17.9 %collective-permute-start.3 = (f32[5,16,128]{2,1,0:T(8,128)S(1)}, f32[5,16,128]{2,1,0:T(8,128)S(1)}, u32[]{:S(2)}, u32[]{:S(2)}) collective-permute-start(f32[5,16,128]{2,1,0:T(8,128)S(1)} %get-tuple-element.13), channel_id=1, source_target_pairs={{0,16},{16,32},{32,48},{48,64},{64,80},{80,96},{96,112},{112,128},... | collective-permute-start | bytes 122888 | tf_op jit(solution)/shard_map/ppermute | solution.py:126
  31.5 20.2 %all-to-all-start = ((f32[32,1,192]{2,1,0:T(1,128)}), f32[32,1,192]{2,1,0:T(1,128)S(1)}, u32[]{:S(2)}, u32[]{:S(2)}) async-start(f32[32,1,192]{2,1,0:T(1,128)} %copy.118), calls=%async_computation | async-start | bytes 65536 | tf_op jit(solution)/shard_map/all_to_all | solution.py:122

commit v8 on v7

--- a/solution.py
+++ b/solution.py
@@ -140,11 +140,14 @@
     along_r = jnp.concatenate([filtered[:, :, 1:], after_r], axis=2) - jnp.concatenate(
         [before_r, filtered[:, :, :-1]], axis=2
     )
-    gradient = filtered
-    for direction, change in enumerate((along_x, along_r, along_a)):
-        mixing = jnp.einsum("fg,fxra->gxra", flux[direction], change, precision=HI)
+    changes = lax.optimization_barrier((along_x, along_r, along_a))
+    gradient = filtered + taken.reshape(adjoint.shape)
+    for direction, change in enumerate(changes):
+        mixing = flux[direction, 0][:, None, None, None] * change[0][None]
+        for f in range(1, fields):
+            mixing = mixing + flux[direction, f][:, None, None, None] * change[f][None]
         gradient = gradient + coeff[direction][None] * mixing
-    gradient = gradient + taken.reshape(adjoint.shape)
+    gradient, received = lax.optimization_barrier((gradient, received))
 
     received = received.reshape(owners, fields + 1, capacity).transpose(1, 0, 2).reshape(fields + 1, owners * capacity)
     got_cell = received[fields].astype(jnp.int32)

time: 55.9 us -> 55.3 us (0.989)
  matrix products: 7.47 us -> 4.96 us
  waiting for transfers between devices: 7.12 us -> 8.95 us
  other arithmetic: 1.6 us -> 2.95 us
  local copies, waits for them, and re-layouts: 4.52 us -> 3.34 us
    dot_general x3 -> x0, matrix products: 2.51 us -> none  [shards(): mixing = jnp.einsum('fg,fxra->gxra', flux[direction], change, precision=HI)]
    all_to_all x1, waiting for transfers between devices: 6.06 us -> 7.89 us  [shards(): lax.all_to_all(outbox, 'gx', split_axis=0, concat_axis=0, tiled=True)]
    add x0 -> x2, other arithmetic: none -> 1.38 us  [the longest x1 0.77 us: shards(): return gradient + update.reshape(adjoint.shape)]
    add x1 -> x0, local copies, waits for them, and re-layouts: 0.78 us -> none  [shards(): return gradient + update.reshape(adjoint.shape)]
  transfers between devices with their start and end apart: 6 -> 6, of which waited for: 2 -> 2; matrix products, arithmetic and copies ran while one was open for 12% -> 10% of each run, Pallas kernels for 0% -> 0%
where the time goes in v8:
time: 55.3 us; the launch traced here: 55 us
  starting transfers between devices  34.4 us (62%)
  waiting for transfers between devices  8.95 us (16%)
  matrix products  4.96 us (9%)
  local copies, waits for them, and re-layouts  3.34 us (6%)
  other arithmetic  2.95 us (5%)
    all_to_all x1, starting transfers between devices, shards(): lax.all_to_all(outbox, 'gx', split_axis=0, concat_axis=0, tiled=True)  11.5 us
    ppermute x1, starting transfers between devices, shards(): from_right = lax.ppermute(to_left, 'az', down)  11.5 us
    all_to_all x1, waiting for transfers between devices, shards(): lax.all_to_all(outbox, 'gx', split_axis=0, concat_axis=0, tiled=True)  7.89 us
    ppermute x1, starting transfers between devices, shards(): lax.ppermute(jnp.where(band == 0, last_r, first_r), 'row', [(0, 1), (1, 0)])  4.01 us
    ppermute x1, starting transfers between devices, shards(): before_x = lax.ppermute(last_x, 'gx', up_x)[:, None]  3.99 us
    ppermute x1, starting transfers between devices, shards(): from_left = lax.ppermute(to_right, 'az', up)  2.05 us
    slice x2, local copies, waits for them, and re-layouts, shards(): lines[:, cells_a - EDGE:]  1.39 us
    dot_general x1, matrix products, shards(): update = jnp.einsum('nk,fna->fka', d_rows, spread, precision=HI)  1.37 us
  transfers between devices with their start and end apart: 6, of which 2 were waited for; matrix products, arithmetic and copies ran while one was open for 10% of the time, Pallas kernels for 0%

profile of v8, /device:TPU:1, one launch (start us, length us, event | category | flops | bytes accessed | tf_op | source)
XLA Modules:
  0.0 55.0 jit_solution(2735347301465249519)
XLA Ops:
  0.0 1.3 %fusion.36 = (f32[640,7]{1,0:T(8,128)S(1)}, f32[640,7]{1,0:T(8,128)S(1)}) fusion(f32[640,128]{1,0:T(8,128)} %bitcast.153), kind=kLoop, calls=%fused_computation.110 | loop fusion | bytes 71680 | tf_op jit(solution)/shard_map/slice | solution.py:90
  1.3 0.1 copy.70
  1.4 0.2 multiply_reduce_fusion.1
  1.7 0.1 broadcast_in_dim.19
  1.8 11.5 %collective-permute-start.1 = (f32[8,640]{1,0:T(8,128)S(1)}, f32[8,640]{1,0:T(8,128)S(1)}, u32[]{:S(2)}, u32[]{:S(2)}) collective-permute-start(f32[8,640]{1,0:T(8,128)S(1)} %maximum_bitcast_fusion.1), channel_id=1, source_target_pairs={{2,0},{4,2},{6,4},{8,6},{10,8},{12,10},{14,12},{0,14},{3,1},{5,3},... | collective-permute-start | bytes 61448 | tf_op jit(solution)/shard_map/ppermute | solution.py:96
  13.3 0.1 copy.68
  13.4 0.1 broadcast_in_dim.18
  13.6 2.1 %collective-permute-start = (f32[8,640]{1,0:T(8,128)S(1)}, f32[8,640]{1,0:T(8,128)S(1)}, u32[]{:S(2)}, u32[]{:S(2)}) collective-permute-start(f32[8,640]{1,0:T(8,128)S(1)} %maximum_bitcast_fusion), channel_id=1, source_target_pairs={{0,2},{2,4},{4,6},{6,8},{8,10},{10,12},{12,14},{14,0},{1,3},{3,5},... | collective-permute-start | bytes 61448 | tf_op jit(solution)/shard_map/ppermute | solution.py:95
  15.7 0.9 %convolution_bitcast_fusion.1 = f32[640,256]{0,1:T(8,128)S(1)} fusion(f32[128,256]{1,0:T(8,128)S(1)} %copy-done.2, f32[640,128]{1,0:T(8,128)S(1)} %bitcast.154), kind=kOutput, calls=%fused_computation.8 | convolution fusion | flops 251658240 | bytes 1114112 | tf_op jit(solution)/shard_map/lc,co->lo/dot_general | solution.py:97
  16.7 0.6 %reduce-window.6 = s32[32,2,128]{2,0,1:T(8,128)S(1)} reduce-window(s32[32,2,128]{2,0,1:T(8,128)S(1)} %fusion.25, s32[]{:T(128)} %constant.64.clone.1), window={size=1x1x128 pad=0_0x0_0x127_0}, to_apply=%region_3.4 | reduce-window | flops 1040384 | bytes 65540 | tf_op jit(solution)/shard_map/reduce-window
  17.3 0.2 slice_reduce_fusion
  17.5 0.1 fusion.22
  17.7 0.7 %fusion.37 = f32[640,256]{0,1:T(8,128)S(1)} fusion(f32[8,640]{1,0:T(8,128)S(1)} %collective-permute-done.1, f32[8,256]{1,0:T(8,128)S(1)} %copy-done.5), kind=kOutput, calls=%fused_computation.111 | convolution fusion | flops 15728640 | bytes 684032 | tf_op jit(solution)/shard_map/kl,ko->lo/dot_general | solution.py:99
  18.4 1.0 %collective-permute-done = f32[8,640]{1,0:T(8,128)S(1)} collective-permute-done((f32[8,640]{1,0:T(8,128)S(1)}, f32[8,640]{1,0:T(8,128)S(1)}, u32[]{:S(2)}, u32[]{:S(2)}) %collective-permute-start) | collective-permute-done | bytes 20512 | tf_op jit(solution)/shard_map/ppermute | solution.py:95
  19.5 0.7 %fusion.4 = f32[640,256]{0,1:T(8,128)S(1)} fusion(f32[640,256]{0,1:T(8,128)S(1)} %fusion.37, f32[640,256]{0,1:T(8,128)S(1)} %convolution_bitcast_fusion.1, f32[8,640]{1,0:T(8,128)S(1)} %collective-permute-done, f32[8,256]{1,0:T(8,128)S(1)} %copy-done.4), kind=kOutput, calls=%fused_computation.5 | convolution fusion | flops 16056320 | bytes 1994752 | tf_op jit(solution)/shard_map/kl,ko->lo/dot_general | solution.py:98
  20.2 0.2 copy.72
  20.6 4.0 %collective-permute-start.4 = (f32[5,8,128]{2,1,0:T(8,128)S(1)}, f32[5,8,128]{2,1,0:T(8,128)S(1)}, u32[]{:S(2)}, u32[]{:S(2)}) collective-permute-start(f32[5,8,128]{2,1,0:T(8,128)S(1)} %select_bitcast_fusion), channel_id=1, source_target_pairs={{0,1},{1,0},{2,3},{3,2},{4,5},{5,4},{6,7},{7,6},{8,9},{9,8},{10,11... | collective-permute-start | bytes 61448 | tf_op jit(solution)/shard_map/ppermute | solution.py:130
  24.6 1.3 %collective-permute-start.2 = (f32[5,16,128]{2,1,0:T(8,128)S(1)}, f32[5,16,128]{2,1,0:T(8,128)S(1)}, u32[]{:S(2)}, u32[]{:S(2)}) collective-permute-start(f32[5,16,128]{2,1,0:T(8,128)S(1)} %get-tuple-element.24), channel_id=1, source_target_pairs={{16,0},{32,16},{48,32},{64,48},{80,64},{96,80},{112,96},{128,112},... | collective-permute-start | bytes 122888 | tf_op jit(solution)/shard_map/ppermute | solution.py:127
  25.9 4.0 %collective-permute-start.3 = (f32[5,16,128]{2,1,0:T(8,128)S(1)}, f32[5,16,128]{2,1,0:T(8,128)S(1)}, u32[]{:S(2)}, u32[]{:S(2)}) collective-permute-start(f32[5,16,128]{2,1,0:T(8,128)S(1)} %get-tuple-element.23), channel_id=1, source_target_pairs={{0,16},{16,32},{32,48},{48,64},{64,80},{80,96},{96,112},{112,128},... | collective-permute-start | bytes 122888 | tf_op jit(solution)/shard_map/ppermute | solution.py:126
  30.0 0.1 fusion.32
  30.1 0.5 fusion.6
  30.6 0.5 fusion.7
  31.1 0.3 convolution_bitcast_fusion.2
  31.4 0.6 %copy.82 = f32[32,1,192]{2,1,0:T(1,128)} copy(f32[32,1,192]{2,0,1:T(8,128)S(1)} %convolution_bitcast_fusion.2) | data formatting | bytes 49152 | tf_op jit(solution)/shard_map/all_to_all | solution.py:122
  32.1 11.5 %all-to-all-start = ((f32[32,1,192]{2,1,0:T(1,128)}), f32[32,1,192]{2,1,0:T(1,128)S(1)}, u32[]{:S(2)}, u32[]{:S(2)}) async-start(f32[32,1,192]{2,1,0:T(1,128)} %copy.82), calls=%async_computation | async-start | bytes 65536 | tf_op jit(solution)/shard_map/all_to_all | solution.py:122
  43.8 0.6 %multiply_add_fusion = f32[5,8,16,128]{3,2,1,0:T(8,128)S(1)} fusion(f32[5,8,16,128]{3,2,1,0:T(8,128)S(1)} %bitcast.155, f32[8,16,128]{2,1,0:T(8,128)S(1)} %get-tuple-element.38, f32[5]{0:T(128)S(1)} %get-tuple-element.62, f32[8,16,128]{2,1,0:T(8,128)S(1)} %get-tuple-element.39, f32[5]{0:T(128)S(1)} %get-tuple-element.63, ...), kind=kLoop, calls=%fused_computation.19 | loop fusion | flops 2785280 | bytes 2162988 | tf_op jit(solution)/shard_map/add | solution.py:149
  44.4 7.9 %all-to-all-done = f32[32,1,192]{2,1,0:T(1,128)S(1)} async-done(((f32[32,1,192]{2,1,0:T(1,128)}), f32[32,1,192]{2,1,0:T(1,128)S(1)}, u32[]{:S(2)}, u32[]{:S(2)}) %all-to-all-start) | async-done | bytes 24608 | tf_op jit(solution)/shard_map/all_to_all | solution.py:122
  52.3 0.1 reshape.237
  52.6 0.2 fusion.9
  52.8 0.1 mul.466
  52.9 1.4 %fusion = f32[5,128,128]{1,2,0:T(8,128)S(1)} fusion(f32[1024,128]{1,0:T(8,128)S(1)} %fusion.9, f32[5,1024]{1,0:T(8,128)S(1)} %mul.466, s32[1024]{0:T(1024)S(1)} %get-tuple-element.66), kind=kOutput, calls=%fused_computation | convolution fusion | flops 1007419392 | bytes 876544 | tf_op jit(solution)/shard_map/nk,fna->fka/dot_general | solution.py:157
  54.3 0.8 %add.106 = f32[5,8,16,128]{3,2,1,0:T(8,128)} add(f32[5,8,16,128]{3,2,1,0:T(8,128)S(1)} %multiply_add_fusion, f32[5,8,16,128]{3,2,1,0:T(8,128)S(1)} %bitcast.160) | non-fusion elementwise | flops 81920 | bytes 983040 | tf_op jit(solution)/shard_map/add | solution.py:158
  (55 shorter events, 0.7 us)
Async XLA Ops:
  0.0 1.4 %copy-start = (f32[5,8,16,128]{3,2,1,0:T(8,128)S(1)}, f32[5,8,16,128]{3,2,1,0:T(8,128)}, u32[]{:S(2)}) copy-start(f32[5,8,16,128]{3,2,1,0:T(8,128)} %param.11) | copy-start | bytes 983044
  0.0 1.4 %copy-start.9 = (f32[128]{0:T(128)S(1)}, f32[128]{0:T(128)}, u32[]{:S(2)}) copy-start(f32[128]{0:T(128)} %constant.71.clone) | copy-start | bytes 1540
  0.0 1.4 %copy-start.10 = (f32[128]{0:T(128)S(1)}, f32[128]{0:T(128)}, u32[]{:S(2)}) copy-start(f32[128]{0:T(128)} %constant.72.clone) | copy-start | bytes 1540
  1.3 14.4 %copy-start.2 = (f32[128,256]{1,0:T(8,128)S(1)}, f32[128,256]{1,0:T(8,128)}, u32[]{:S(2)}) copy-start(f32[128,256]{1,0:T(8,128)} %constant.73.clone) | copy-start | bytes 393220
  1.8 15.9 %collective-permute-start.1 = (f32[8,640]{1,0:T(8,128)S(1)}, f32[8,640]{1,0:T(8,128)S(1)}, u32[]{:S(2)}, u32[]{:S(2)}) collective-permute-start(f32[8,640]{1,0:T(8,128)S(1)} %maximum_bitcast_fusion.1), channel_id=1, source_target_pairs={{2,0},{4,2},{6,4},{8,6},{10,8},{12,10},{14,12},{0,14},{3,1},{5,3},... | collective-permute-start | bytes 61448 | tf_op jit(solution)/shard_map/ppermute | solution.py:96
  13.4 3.1 %copy-start.7 = (s32[256]{0:T(256)S(1)}, s32[256]{0:T(256)}, u32[]{:S(2)}) copy-start(s32[256]{0:T(256)} %param.14) | copy-start | bytes 3076
  13.4 3.2 %copy-start.1 = (f32[3,8,16,128]{3,2,1,0:T(8,128)S(1)}, f32[3,8,16,128]{3,2,1,0:T(8,128)}, u32[]{:S(2)}) copy-start(f32[3,8,16,128]{3,2,1,0:T(8,128)} %param.12) | copy-start | bytes 589828
  13.6 3.1 %copy-start.3 = (s32[256,1]{0,1:T(1,128)S(1)}, s32[256,1]{0,1:T(1,128)}, u32[]{:S(2)}) copy-start(s32[256,1]{0,1:T(1,128)} %param.15) | copy-start | bytes 3076
  13.6 4.0 %copy-start.6 = (f32[3,5,5]{2,0,1:T(4,128)S(1)}, f32[3,5,5]{2,0,1:T(4,128)}, u32[]{:S(2)}) copy-start(f32[3,5,5]{2,0,1:T(4,128)} %param.13) | copy-start | bytes 904
  13.6 5.9 %collective-permute-start = (f32[8,640]{1,0:T(8,128)S(1)}, f32[8,640]{1,0:T(8,128)S(1)}, u32[]{:S(2)}, u32[]{:S(2)}) collective-permute-start(f32[8,640]{1,0:T(8,128)S(1)} %maximum_bitcast_fusion), channel_id=1, source_target_pairs={{0,2},{2,4},{4,6},{6,8},{8,10},{10,12},{12,14},{14,0},{1,3},{3,5},... | collective-permute-start | bytes 61448 | tf_op jit(solution)/shard_map/ppermute | solution.py:95
  16.5 1.1 %copy-start.8 = (s32[256]{0:T(256)S(1)}, s32[256]{0:T(256)}, u32[]{:S(2)}) copy-start(s32[256]{0:T(256)} %param.16) | copy-start | bytes 3076
  16.5 1.1 %copy-start.5 = (f32[8,256]{1,0:T(8,128)S(1)}, f32[8,256]{1,0:T(8,128)}, u32[]{:S(2)}) copy-start(f32[8,256]{1,0:T(8,128)} %constant.75.clone) | copy-start | bytes 24580
  16.6 2.9 %copy-start.4 = (f32[8,256]{1,0:T(8,128)S(1)}, f32[8,256]{1,0:T(8,128)}, u32[]{:S(2)}) copy-start(f32[8,256]{1,0:T(8,128)} %constant.74.clone) | copy-start | bytes 24580
  20.6 9.3 %collective-permute-start.4 = (f32[5,8,128]{2,1,0:T(8,128)S(1)}, f32[5,8,128]{2,1,0:T(8,128)S(1)}, u32[]{:S(2)}, u32[]{:S(2)}) collective-permute-start(f32[5,8,128]{2,1,0:T(8,128)S(1)} %select_bitcast_fusion), channel_id=1, source_target_pairs={{0,1},{1,0},{2,3},{3,2},{4,5},{5,4},{6,7},{7,6},{8,9},{9,8},{10,11... | collective-permute-start | bytes 61448 | tf_op jit(solution)/shard_map/ppermute | solution.py:130
  24.6 19.0 %collective-permute-start.2 = (f32[5,16,128]{2,1,0:T(8,128)S(1)}, f32[5,16,128]{2,1,0:T(8,128)S(1)}, u32[]{:S(2)}, u32[]{:S(2)}) collective-permute-start(f32[5,16,128]{2,1,0:T(8,128)S(1)} %get-tuple-element.24), channel_id=1, source_target_pairs={{16,0},{32,16},{48,32},{64,48},{80,64},{96,80},{112,96},{128,112},... | collective-permute-start | bytes 122888 | tf_op jit(solution)/shard_map/ppermute | solution.py:127
  25.9 17.7 %collective-permute-start.3 = (f32[5,16,128]{2,1,0:T(8,128)S(1)}, f32[5,16,128]{2,1,0:T(8,128)S(1)}, u32[]{:S(2)}, u32[]{:S(2)}) collective-permute-start(f32[5,16,128]{2,1,0:T(8,128)S(1)} %get-tuple-element.23), channel_id=1, source_target_pairs={{0,16},{16,32},{32,48},{48,64},{64,80},{80,96},{96,112},{112,128},... | collective-permute-start | bytes 122888 | tf_op jit(solution)/shard_map/ppermute | solution.py:126
  32.1 20.2 %all-to-all-start = ((f32[32,1,192]{2,1,0:T(1,128)}), f32[32,1,192]{2,1,0:T(1,128)S(1)}, u32[]{:S(2)}, u32[]{:S(2)}) async-start(f32[32,1,192]{2,1,0:T(1,128)} %copy.82), calls=%async_computation | async-start | bytes 65536 | tf_op jit(solution)/shard_map/all_to_all | solution.py:122

commit v9 on v8

--- a/solution.py
+++ b/solution.py
@@ -84,14 +84,9 @@
     lines = adjoint.reshape(fields * rows, cells_a)
 
     up, down = neighbours(adjoint, "az", True)
-    right_moment = jnp.asarray(send_right_t[:, EDGE])
-    left_moment = jnp.asarray(send_left_t[:, EDGE])
-    to_right = jnp.concatenate(
-        [lines[:, cells_a - EDGE :], jnp.sum(lines * right_moment[None], axis=1, keepdims=True)], axis=1
-    ).T
-    to_left = jnp.concatenate(
-        [lines[:, :EDGE], jnp.sum(lines * left_moment[None], axis=1, keepdims=True)], axis=1
-    ).T
+    selector = jnp.asarray(np.concatenate([send_right_t, send_left_t], axis=1).T)
+    payload = jnp.einsum("kc,lc->kl", selector, lines, precision=HI)
+    to_right, to_left = payload[: EDGE + 1], payload[EDGE + 1 :]
     from_left = lax.ppermute(to_right, "az", up)
     from_right = lax.ppermute(to_left, "az", down)
     both = jnp.einsum("lc,co->lo", lines, jnp.asarray(own_t), precision=HI)

time: 55.3 us -> 55.5 us (level)
  matrix products: 4.96 us -> 6.96 us
  waiting for transfers between devices: 8.95 us -> 8.05 us
  local copies, waits for them, and re-layouts: 3.34 us -> 2.58 us
    slice x4 -> x2, local copies, waits for them, and re-layouts: 1.7 us -> 0.19 us  [the longest x2 1.39 us: shards(): lines[:, cells_a - EDGE:]]
    dot_general x0 -> x1, matrix products: none -> 1.09 us  [shards(): payload = jnp.einsum('kc,lc->kl', selector, lines, precision=HI)]
    unnamed x23 -> x17, local copies, waits for them, and re-layouts: 0.08 us -> 1.02 us
    dot_general x1, matrix products: 0.85 us -> 1.76 us  [shards(): both = jnp.einsum('lc,co->lo', lines, jnp.asarray(own_t), precision=HI)]
    ppermute x1, waiting for transfers between devices: 1.05 us -> 0.15 us  [shards(): from_left = lax.ppermute(to_right, 'az', up)]
  transfers between devices with their start and end apart: 6 -> 6, of which waited for: 2 -> 2; matrix products, arithmetic and copies ran while one was open for 10% -> 11% of each run, Pallas kernels for 0% -> 0%
where the time goes in v9:
time: 55.5 us; the launch traced here: 55.1 us
  starting transfers between devices  34.4 us (62%)
  waiting for transfers between devices  8.05 us (15%)
  matrix products  6.96 us (13%)
  other arithmetic  2.67 us (5%)
  local copies, waits for them, and re-layouts  2.58 us (5%)
    ppermute x1, starting transfers between devices, shards(): from_right = lax.ppermute(to_left, 'az', down)  11.6 us
    all_to_all x1, starting transfers between devices, shards(): lax.all_to_all(outbox, 'gx', split_axis=0, concat_axis=0, tiled=True)  11.5 us
    all_to_all x1, waiting for transfers between devices, shards(): lax.all_to_all(outbox, 'gx', split_axis=0, concat_axis=0, tiled=True)  7.89 us
    ppermute x1, starting transfers between devices, shards(): lax.ppermute(jnp.where(band == 0, last_r, first_r), 'row', [(0, 1), (1, 0)])  4 us
    ppermute x1, starting transfers between devices, shards(): before_x = lax.ppermute(last_x, 'gx', up_x)[:, None]  3.99 us
    ppermute x1, starting transfers between devices, shards(): from_left = lax.ppermute(to_right, 'az', up)  1.92 us
    dot_general x1, matrix products, shards(): both = jnp.einsum('lc,co->lo', lines, jnp.asarray(own_t), precision=HI)  1.76 us
    dot_general x1, matrix products, shards(): update = jnp.einsum('nk,fna->fka', d_rows, spread, precision=HI)  1.37 us
  transfers between devices with their start and end apart: 6, of which 2 were waited for; matrix products, arithmetic and copies ran while one was open for 11% of the time, Pallas kernels for 0%

profile of v9, /device:TPU:1, one launch (start us, length us, event | category | flops | bytes accessed | tf_op | source)
XLA Modules:
  0.0 55.1 jit_solution(10893409916503089924)
XLA Ops:
  0.0 1.0 %copy-done = f32[5,8,16,128]{3,2,1,0:T(8,128)S(1)} copy-done((f32[5,8,16,128]{3,2,1,0:T(8,128)S(1)}, f32[5,8,16,128]{3,2,1,0:T(8,128)}, u32[]{:S(2)}) %copy-start) | copy-done | bytes 327704
  1.0 1.1 %fusion.37 = f32[16,640]{1,0:T(8,128)S(1)} fusion(f32[16,128]{1,0:T(8,128)} %constant.69.clone, f32[640,128]{1,0:T(8,128)S(1)} %bitcast.146), kind=kOutput, calls=%fused_computation.107 | convolution fusion | flops 15728640 | bytes 376832 | tf_op jit(solution)/shard_map/kc,lc->kl/dot_general | solution.py:88
  2.1 11.6 %collective-permute-start.1 = (f32[8,640]{1,0:T(8,128)S(1)}, f32[8,640]{1,0:T(8,128)S(1)}, u32[]{:S(2)}, u32[]{:S(2)}) collective-permute-start(f32[8,640]{1,0:T(8,128)S(1)} %get-tuple-element.44), channel_id=1, source_target_pairs={{2,0},{4,2},{6,4},{8,6},{10,8},{12,10},{14,12},{0,14},{3,1},{5,3},... | collective-permute-start | bytes 61448 | tf_op jit(solution)/shard_map/ppermute | solution.py:91
  13.8 1.9 %collective-permute-start = (f32[8,640]{1,0:T(8,128)S(1)}, f32[8,640]{1,0:T(8,128)S(1)}, u32[]{:S(2)}, u32[]{:S(2)}) collective-permute-start(f32[8,640]{1,0:T(8,128)S(1)} %get-tuple-element.43), channel_id=1, source_target_pairs={{0,2},{2,4},{4,6},{6,8},{8,10},{10,12},{12,14},{14,0},{1,3},{3,5},... | collective-permute-start | bytes 61448 | tf_op jit(solution)/shard_map/ppermute | solution.py:90
  15.7 1.8 %convolution_bitcast_fusion.1 = f32[640,256]{0,1:T(8,128)S(1)} fusion(f32[128,256]{1,0:T(8,128)} %constant.70.clone, f32[640,128]{1,0:T(8,128)S(1)} %bitcast.145), kind=kOutput, calls=%fused_computation.8 | convolution fusion | flops 251658240 | bytes 1114112 | tf_op jit(solution)/shard_map/lc,co->lo/dot_general | solution.py:92
  17.5 0.0 copy-start.4
  17.6 0.6 %reduce-window.6 = s32[32,2,128]{2,0,1:T(8,128)S(1)} reduce-window(s32[32,2,128]{2,0,1:T(8,128)S(1)} %fusion.25, s32[]{:T(128)} %constant.61.clone.1), window={size=1x1x128 pad=0_0x0_0x127_0}, to_apply=%region_1.2 | reduce-window | flops 1040384 | bytes 65540 | tf_op jit(solution)/shard_map/reduce-window
  18.2 0.2 slice_reduce_fusion
  18.4 0.1 fusion.22
  18.6 0.7 %fusion.38 = f32[640,256]{0,1:T(8,128)S(1)} fusion(f32[8,640]{1,0:T(8,128)S(1)} %collective-permute-done.1, f32[8,256]{1,0:T(8,128)S(1)} %copy-done.4), kind=kOutput, calls=%fused_computation.108 | convolution fusion | flops 15728640 | bytes 684032 | tf_op jit(solution)/shard_map/kl,ko->lo/dot_general | solution.py:94
  19.4 0.2 collective-permute-done
  19.5 0.7 %fusion.4 = f32[640,256]{0,1:T(8,128)S(1)} fusion(f32[640,256]{0,1:T(8,128)S(1)} %fusion.38, f32[640,256]{0,1:T(8,128)S(1)} %convolution_bitcast_fusion.1, f32[8,640]{1,0:T(8,128)S(1)} %collective-permute-done, f32[8,256]{1,0:T(8,128)S(1)} %copy-done.3), kind=kOutput, calls=%fused_computation.5 | convolution fusion | flops 16056320 | bytes 1994752 | tf_op jit(solution)/shard_map/kl,ko->lo/dot_general | solution.py:93
  20.3 0.2 copy.52
  20.7 4.0 %collective-permute-start.4 = (f32[5,8,128]{2,1,0:T(8,128)S(1)}, f32[5,8,128]{2,1,0:T(8,128)S(1)}, u32[]{:S(2)}, u32[]{:S(2)}) collective-permute-start(f32[5,8,128]{2,1,0:T(8,128)S(1)} %select_bitcast_fusion), channel_id=1, source_target_pairs={{0,1},{1,0},{2,3},{3,2},{4,5},{5,4},{6,7},{7,6},{8,9},{9,8},{10,11... | collective-permute-start | bytes 61448 | tf_op jit(solution)/shard_map/ppermute | solution.py:125
  24.7 1.3 %collective-permute-start.2 = (f32[5,16,128]{2,1,0:T(8,128)S(1)}, f32[5,16,128]{2,1,0:T(8,128)S(1)}, u32[]{:S(2)}, u32[]{:S(2)}) collective-permute-start(f32[5,16,128]{2,1,0:T(8,128)S(1)} %get-tuple-element.22), channel_id=1, source_target_pairs={{16,0},{32,16},{48,32},{64,48},{80,64},{96,80},{112,96},{128,112},... | collective-permute-start | bytes 122888 | tf_op jit(solution)/shard_map/ppermute | solution.py:122
  26.0 4.0 %collective-permute-start.3 = (f32[5,16,128]{2,1,0:T(8,128)S(1)}, f32[5,16,128]{2,1,0:T(8,128)S(1)}, u32[]{:S(2)}, u32[]{:S(2)}) collective-permute-start(f32[5,16,128]{2,1,0:T(8,128)S(1)} %get-tuple-element.21), channel_id=1, source_target_pairs={{0,16},{16,32},{32,48},{48,64},{64,80},{80,96},{96,112},{112,128},... | collective-permute-start | bytes 122888 | tf_op jit(solution)/shard_map/ppermute | solution.py:121
  30.0 0.1 fusion.32
  30.1 0.5 fusion.6
  30.6 0.5 fusion.7
  31.2 0.3 convolution_bitcast_fusion.2
  31.5 0.6 %copy.62 = f32[32,1,192]{2,1,0:T(1,128)} copy(f32[32,1,192]{2,0,1:T(8,128)S(1)} %convolution_bitcast_fusion.2) | data formatting | bytes 49152 | tf_op jit(solution)/shard_map/all_to_all | solution.py:117
  32.1 11.5 %all-to-all-start = ((f32[32,1,192]{2,1,0:T(1,128)}), f32[32,1,192]{2,1,0:T(1,128)S(1)}, u32[]{:S(2)}, u32[]{:S(2)}) async-start(f32[32,1,192]{2,1,0:T(1,128)} %copy.62), calls=%async_computation | async-start | bytes 65536 | tf_op jit(solution)/shard_map/all_to_all | solution.py:117
  43.7 0.1 maximum_subtract_fusion
  43.9 0.6 %multiply_add_fusion = f32[5,8,16,128]{3,2,1,0:T(8,128)S(1)} fusion(f32[5,8,16,128]{3,2,1,0:T(8,128)S(1)} %bitcast.153, f32[8,16,128]{2,1,0:T(8,128)S(1)} %get-tuple-element.36, f32[5]{0:T(128)S(1)} %get-tuple-element.60, f32[8,16,128]{2,1,0:T(8,128)S(1)} %get-tuple-element.37, f32[5]{0:T(128)S(1)} %get-tuple-element.61, ...), kind=kLoop, calls=%fused_computation.19 | loop fusion | flops 2785280 | bytes 2162988 | tf_op jit(solution)/shard_map/add | solution.py:144
  44.5 7.9 %all-to-all-done = f32[32,1,192]{2,1,0:T(1,128)S(1)} async-done(((f32[32,1,192]{2,1,0:T(1,128)}), f32[32,1,192]{2,1,0:T(1,128)S(1)}, u32[]{:S(2)}, u32[]{:S(2)}) %all-to-all-start) | async-done | bytes 24608 | tf_op jit(solution)/shard_map/all_to_all | solution.py:117
  52.4 0.1 reshape.221
  52.5 0.1 fusion.27
  52.5 0.1 convert_element_type.56
  52.6 0.2 fusion.9
  52.8 0.1 mul.444
  52.9 1.4 %fusion = f32[5,128,128]{1,2,0:T(8,128)S(1)} fusion(f32[1024,128]{1,0:T(8,128)S(1)} %fusion.9, f32[5,1024]{1,0:T(8,128)S(1)} %mul.444, s32[1024]{0:T(1024)S(1)} %get-tuple-element.64), kind=kOutput, calls=%fused_computation | convolution fusion | flops 1007419392 | bytes 876544 | tf_op jit(solution)/shard_map/nk,fna->fka/dot_general | solution.py:152
  54.3 0.8 %add.106 = f32[5,8,16,128]{3,2,1,0:T(8,128)} add(f32[5,8,16,128]{3,2,1,0:T(8,128)S(1)} %multiply_add_fusion, f32[5,8,16,128]{3,2,1,0:T(8,128)S(1)} %bitcast.158) | non-fusion elementwise | flops 81920 | bytes 983040 | tf_op jit(solution)/shard_map/add | solution.py:153
  (43 shorter events, 0.4 us)
Async XLA Ops:
  0.0 1.0 %copy-start = (f32[5,8,16,128]{3,2,1,0:T(8,128)S(1)}, f32[5,8,16,128]{3,2,1,0:T(8,128)}, u32[]{:S(2)}) copy-start(f32[5,8,16,128]{3,2,1,0:T(8,128)} %param.10) | copy-start | bytes 983044
  2.1 15.4 %copy-start.6 = (s32[256]{0:T(256)S(1)}, s32[256]{0:T(256)}, u32[]{:S(2)}) copy-start(s32[256]{0:T(256)} %param.13) | copy-start | bytes 3076
  2.1 15.5 %copy-start.1 = (f32[3,8,16,128]{3,2,1,0:T(8,128)S(1)}, f32[3,8,16,128]{3,2,1,0:T(8,128)}, u32[]{:S(2)}) copy-start(f32[3,8,16,128]{3,2,1,0:T(8,128)} %param.11) | copy-start | bytes 589828
  2.1 16.5 %collective-permute-start.1 = (f32[8,640]{1,0:T(8,128)S(1)}, f32[8,640]{1,0:T(8,128)S(1)}, u32[]{:S(2)}, u32[]{:S(2)}) collective-permute-start(f32[8,640]{1,0:T(8,128)S(1)} %get-tuple-element.44), channel_id=1, source_target_pairs={{2,0},{4,2},{6,4},{8,6},{10,8},{12,10},{14,12},{0,14},{3,1},{5,3},... | collective-permute-start | bytes 61448 | tf_op jit(solution)/shard_map/ppermute | solution.py:91
  13.7 3.8 %copy-start.2 = (s32[256,1]{0,1:T(1,128)S(1)}, s32[256,1]{0,1:T(1,128)}, u32[]{:S(2)}) copy-start(s32[256,1]{0,1:T(1,128)} %param.14) | copy-start | bytes 3076
  13.8 4.8 %copy-start.5 = (f32[3,5,5]{2,0,1:T(4,128)S(1)}, f32[3,5,5]{2,0,1:T(4,128)}, u32[]{:S(2)}) copy-start(f32[3,5,5]{2,0,1:T(4,128)} %param.12) | copy-start | bytes 904
  13.8 5.7 %collective-permute-start = (f32[8,640]{1,0:T(8,128)S(1)}, f32[8,640]{1,0:T(8,128)S(1)}, u32[]{:S(2)}, u32[]{:S(2)}) collective-permute-start(f32[8,640]{1,0:T(8,128)S(1)} %get-tuple-element.43), channel_id=1, source_target_pairs={{0,2},{2,4},{4,6},{6,8},{8,10},{10,12},{12,14},{14,0},{1,3},{3,5},... | collective-permute-start | bytes 61448 | tf_op jit(solution)/shard_map/ppermute | solution.py:90
  17.5 1.1 %copy-start.7 = (s32[256]{0:T(256)S(1)}, s32[256]{0:T(256)}, u32[]{:S(2)}) copy-start(s32[256]{0:T(256)} %param.15) | copy-start | bytes 3076
  17.5 1.1 %copy-start.4 = (f32[8,256]{1,0:T(8,128)S(1)}, f32[8,256]{1,0:T(8,128)}, u32[]{:S(2)}) copy-start(f32[8,256]{1,0:T(8,128)} %constant.72.clone) | copy-start | bytes 24580
  17.5 2.0 %copy-start.3 = (f32[8,256]{1,0:T(8,128)S(1)}, f32[8,256]{1,0:T(8,128)}, u32[]{:S(2)}) copy-start(f32[8,256]{1,0:T(8,128)} %constant.71.clone) | copy-start | bytes 24580
  20.7 9.3 %collective-permute-start.4 = (f32[5,8,128]{2,1,0:T(8,128)S(1)}, f32[5,8,128]{2,1,0:T(8,128)S(1)}, u32[]{:S(2)}, u32[]{:S(2)}) collective-permute-start(f32[5,8,128]{2,1,0:T(8,128)S(1)} %select_bitcast_fusion), channel_id=1, source_target_pairs={{0,1},{1,0},{2,3},{3,2},{4,5},{5,4},{6,7},{7,6},{8,9},{9,8},{10,11... | collective-permute-start | bytes 61448 | tf_op jit(solution)/shard_map/ppermute | solution.py:125
  24.7 19.0 %collective-permute-start.2 = (f32[5,16,128]{2,1,0:T(8,128)S(1)}, f32[5,16,128]{2,1,0:T(8,128)S(1)}, u32[]{:S(2)}, u32[]{:S(2)}) collective-permute-start(f32[5,16,128]{2,1,0:T(8,128)S(1)} %get-tuple-element.22), channel_id=1, source_target_pairs={{16,0},{32,16},{48,32},{64,48},{80,64},{96,80},{112,96},{128,112},... | collective-permute-start | bytes 122888 | tf_op jit(solution)/shard_map/ppermute | solution.py:122
  26.0 17.7 %collective-permute-start.3 = (f32[5,16,128]{2,1,0:T(8,128)S(1)}, f32[5,16,128]{2,1,0:T(8,128)S(1)}, u32[]{:S(2)}, u32[]{:S(2)}) collective-permute-start(f32[5,16,128]{2,1,0:T(8,128)S(1)} %get-tuple-element.21), channel_id=1, source_target_pairs={{0,16},{16,32},{32,48},{48,64},{64,80},{80,96},{96,112},{112,128},... | collective-permute-start | bytes 122888 | tf_op jit(solution)/shard_map/ppermute | solution.py:121
  32.1 20.2 %all-to-all-start = ((f32[32,1,192]{2,1,0:T(1,128)}), f32[32,1,192]{2,1,0:T(1,128)S(1)}, u32[]{:S(2)}, u32[]{:S(2)}) async-start(f32[32,1,192]{2,1,0:T(1,128)} %copy.62), calls=%async_computation | async-start | bytes 65536 | tf_op jit(solution)/shard_map/all_to_all | solution.py:117

commit v10 on v8

--- a/solution.py
+++ b/solution.py
@@ -14,7 +14,7 @@
     5.0 * (2.0 * filter_alpha - 1.0) / 256.0,
     (1.0 - 2.0 * filter_alpha) / 512.0,
 ]
-HI = lax.Precision.HIGHEST
+HI = lax.Precision.HIGH
 
 
 root_value = (-1.0 + (1.0 - 4.0 * filter_alpha * filter_alpha) ** 0.5) / (2.0 * filter_alpha)

time: 55.3 us -> 54.6 us (0.987)
  matrix products: 4.96 us -> 3.65 us
  waiting for transfers between devices: 8.95 us -> 9.55 us
    ppermute x1, waiting for transfers between devices: 1.05 us -> 1.65 us  [shards(): from_left = lax.ppermute(to_right, 'az', up)]
  transfers between devices with their start and end apart: 6 -> 6, of which waited for: 2 -> 2; matrix products, arithmetic and copies ran while one was open for 10% -> 9% of each run, Pallas kernels for 0% -> 0%
where the time goes in v10:
time: 54.6 us; the launch traced here: 54.3 us
  starting transfers between devices  34.4 us (63%)
  waiting for transfers between devices  9.55 us (17%)
  matrix products  3.65 us (7%)
  local copies, waits for them, and re-layouts  3.34 us (6%)
  other arithmetic  2.95 us (5%)
    all_to_all x1, starting transfers between devices, shards(): lax.all_to_all(outbox, 'gx', split_axis=0, concat_axis=0, tiled=True)  11.5 us
    ppermute x1, starting transfers between devices, shards(): from_right = lax.ppermute(to_left, 'az', down)  11.5 us
    all_to_all x1, waiting for transfers between devices, shards(): lax.all_to_all(outbox, 'gx', split_axis=0, concat_axis=0, tiled=True)  7.89 us
    ppermute x1, starting transfers between devices, shards(): lax.ppermute(jnp.where(band == 0, last_r, first_r), 'row', [(0, 1), (1, 0)])  4.01 us
    ppermute x1, starting transfers between devices, shards(): before_x = lax.ppermute(last_x, 'gx', up_x)[:, None]  3.99 us
    ppermute x1, starting transfers between devices, shards(): from_left = lax.ppermute(to_right, 'az', up)  2.05 us
    ppermute x1, waiting for transfers between devices, shards(): from_left = lax.ppermute(to_right, 'az', up)  1.65 us
    slice x2, local copies, waits for them, and re-layouts, shards(): lines[:, cells_a - EDGE:]  1.39 us
  transfers between devices with their start and end apart: 6, of which 2 were waited for; matrix products, arithmetic and copies ran while one was open for 9% of the time, Pallas kernels for 0%

profile of v10, /device:TPU:1, one launch (start us, length us, event | category | flops | bytes accessed | tf_op | source)
XLA Modules:
  0.0 54.3 jit_solution(2853585367242603541)
XLA Ops:
  0.0 1.3 %fusion.36 = (f32[640,7]{1,0:T(8,128)S(1)}, f32[640,7]{1,0:T(8,128)S(1)}) fusion(f32[640,128]{1,0:T(8,128)} %bitcast.153), kind=kLoop, calls=%fused_computation.110 | loop fusion | bytes 71680 | tf_op jit(solution)/shard_map/slice | solution.py:90
  1.3 0.1 copy.70
  1.4 0.2 multiply_reduce_fusion.1
  1.7 0.1 broadcast_in_dim.19
  1.8 11.5 %collective-permute-start.1 = (f32[8,640]{1,0:T(8,128)S(1)}, f32[8,640]{1,0:T(8,128)S(1)}, u32[]{:S(2)}, u32[]{:S(2)}) collective-permute-start(f32[8,640]{1,0:T(8,128)S(1)} %maximum_bitcast_fusion.1), channel_id=1, source_target_pairs={{2,0},{4,2},{6,4},{8,6},{10,8},{12,10},{14,12},{0,14},{3,1},{5,3},... | collective-permute-start | bytes 61448 | tf_op jit(solution)/shard_map/ppermute | solution.py:96
  13.3 0.1 copy.68
  13.4 0.1 broadcast_in_dim.18
  13.6 2.1 %collective-permute-start = (f32[8,640]{1,0:T(8,128)S(1)}, f32[8,640]{1,0:T(8,128)S(1)}, u32[]{:S(2)}, u32[]{:S(2)}) collective-permute-start(f32[8,640]{1,0:T(8,128)S(1)} %maximum_bitcast_fusion), channel_id=1, source_target_pairs={{0,2},{2,4},{4,6},{6,8},{8,10},{10,12},{12,14},{14,0},{1,3},{3,5},... | collective-permute-start | bytes 61448 | tf_op jit(solution)/shard_map/ppermute | solution.py:95
  15.7 0.5 convolution_bitcast_fusion.1
  16.3 0.6 %reduce-window.6 = s32[32,2,128]{2,0,1:T(8,128)S(1)} reduce-window(s32[32,2,128]{2,0,1:T(8,128)S(1)} %fusion.25, s32[]{:T(128)} %constant.64.clone.1), window={size=1x1x128 pad=0_0x0_0x127_0}, to_apply=%region_3.4 | reduce-window | flops 1040384 | bytes 65540 | tf_op jit(solution)/shard_map/reduce-window
  16.9 0.2 slice_reduce_fusion
  17.1 0.1 fusion.22
  17.3 0.5 fusion.37
  17.8 1.7 %collective-permute-done = f32[8,640]{1,0:T(8,128)S(1)} collective-permute-done((f32[8,640]{1,0:T(8,128)S(1)}, f32[8,640]{1,0:T(8,128)S(1)}, u32[]{:S(2)}, u32[]{:S(2)}) %collective-permute-start) | collective-permute-done | bytes 20512 | tf_op jit(solution)/shard_map/ppermute | solution.py:95
  19.5 0.5 fusion.4
  20.0 0.2 copy.72
  20.4 4.0 %collective-permute-start.4 = (f32[5,8,128]{2,1,0:T(8,128)S(1)}, f32[5,8,128]{2,1,0:T(8,128)S(1)}, u32[]{:S(2)}, u32[]{:S(2)}) collective-permute-start(f32[5,8,128]{2,1,0:T(8,128)S(1)} %select_bitcast_fusion), channel_id=1, source_target_pairs={{0,1},{1,0},{2,3},{3,2},{4,5},{5,4},{6,7},{7,6},{8,9},{9,8},{10,11... | collective-permute-start | bytes 61448 | tf_op jit(solution)/shard_map/ppermute | solution.py:130
  24.4 1.3 %collective-permute-start.2 = (f32[5,16,128]{2,1,0:T(8,128)S(1)}, f32[5,16,128]{2,1,0:T(8,128)S(1)}, u32[]{:S(2)}, u32[]{:S(2)}) collective-permute-start(f32[5,16,128]{2,1,0:T(8,128)S(1)} %get-tuple-element.24), channel_id=1, source_target_pairs={{16,0},{32,16},{48,32},{64,48},{80,64},{96,80},{112,96},{128,112},... | collective-permute-start | bytes 122888 | tf_op jit(solution)/shard_map/ppermute | solution.py:127
  25.7 4.0 %collective-permute-start.3 = (f32[5,16,128]{2,1,0:T(8,128)S(1)}, f32[5,16,128]{2,1,0:T(8,128)S(1)}, u32[]{:S(2)}, u32[]{:S(2)}) collective-permute-start(f32[5,16,128]{2,1,0:T(8,128)S(1)} %get-tuple-element.23), channel_id=1, source_target_pairs={{0,16},{16,32},{32,48},{48,64},{64,80},{80,96},{96,112},{112,128},... | collective-permute-start | bytes 122888 | tf_op jit(solution)/shard_map/ppermute | solution.py:126
  29.7 0.1 fusion.32
  29.9 0.4 fusion.6
  30.3 0.3 fusion.7
  30.7 0.2 convolution_bitcast_fusion.2
  30.9 0.6 %copy.82 = f32[32,1,192]{2,1,0:T(1,128)} copy(f32[32,1,192]{2,0,1:T(8,128)S(1)} %convolution_bitcast_fusion.2) | data formatting | bytes 49152 | tf_op jit(solution)/shard_map/all_to_all | solution.py:122
  31.6 11.5 %all-to-all-start = ((f32[32,1,192]{2,1,0:T(1,128)}), f32[32,1,192]{2,1,0:T(1,128)S(1)}, u32[]{:S(2)}, u32[]{:S(2)}) async-start(f32[32,1,192]{2,1,0:T(1,128)} %copy.82), calls=%async_computation | async-start | bytes 65536 | tf_op jit(solution)/shard_map/all_to_all | solution.py:122
  43.3 0.6 %multiply_add_fusion = f32[5,8,16,128]{3,2,1,0:T(8,128)S(1)} fusion(f32[5,8,16,128]{3,2,1,0:T(8,128)S(1)} %bitcast.155, f32[8,16,128]{2,1,0:T(8,128)S(1)} %get-tuple-element.38, f32[5]{0:T(128)S(1)} %get-tuple-element.62, f32[8,16,128]{2,1,0:T(8,128)S(1)} %get-tuple-element.39, f32[5]{0:T(128)S(1)} %get-tuple-element.63, ...), kind=kLoop, calls=%fused_computation.19 | loop fusion | flops 2785280 | bytes 2162988 | tf_op jit(solution)/shard_map/add | solution.py:149
  43.9 7.9 %all-to-all-done = f32[32,1,192]{2,1,0:T(1,128)S(1)} async-done(((f32[32,1,192]{2,1,0:T(1,128)}), f32[32,1,192]{2,1,0:T(1,128)S(1)}, u32[]{:S(2)}, u32[]{:S(2)}) %all-to-all-start) | async-done | bytes 24608 | tf_op jit(solution)/shard_map/all_to_all | solution.py:122
  51.8 0.1 reshape.237
  52.0 0.2 fusion.9
  52.3 0.1 mul.466
  52.3 1.2 %fusion = f32[5,128,128]{1,2,0:T(8,128)S(1)} fusion(f32[1024,128]{1,0:T(8,128)S(1)} %fusion.9, f32[5,1024]{1,0:T(8,128)S(1)} %mul.466, s32[1024]{0:T(1024)S(1)} %get-tuple-element.66), kind=kOutput, calls=%fused_computation | convolution fusion | flops 504102912 | bytes 876544 | tf_op jit(solution)/shard_map/nk,fna->fka/dot_general | solution.py:157
  53.6 0.8 %add.106 = f32[5,8,16,128]{3,2,1,0:T(8,128)} add(f32[5,8,16,128]{3,2,1,0:T(8,128)S(1)} %multiply_add_fusion, f32[5,8,16,128]{3,2,1,0:T(8,128)S(1)} %bitcast.160) | non-fusion elementwise | flops 81920 | bytes 983040 | tf_op jit(solution)/shard_map/add | solution.py:158
  (55 shorter events, 0.7 us)
Async XLA Ops:
  0.0 1.4 %copy-start = (f32[5,8,16,128]{3,2,1,0:T(8,128)S(1)}, f32[5,8,16,128]{3,2,1,0:T(8,128)}, u32[]{:S(2)}) copy-start(f32[5,8,16,128]{3,2,1,0:T(8,128)} %param.11) | copy-start | bytes 983044
  0.0 1.4 %copy-start.9 = (f32[128]{0:T(128)S(1)}, f32[128]{0:T(128)}, u32[]{:S(2)}) copy-start(f32[128]{0:T(128)} %constant.71.clone) | copy-start | bytes 1540
  0.0 1.4 %copy-start.10 = (f32[128]{0:T(128)S(1)}, f32[128]{0:T(128)}, u32[]{:S(2)}) copy-start(f32[128]{0:T(128)} %constant.72.clone) | copy-start | bytes 1540
  1.3 14.4 %copy-start.2 = (f32[128,256]{1,0:T(8,128)S(1)}, f32[128,256]{1,0:T(8,128)}, u32[]{:S(2)}) copy-start(f32[128,256]{1,0:T(8,128)} %constant.73.clone) | copy-start | bytes 393220
  1.8 15.5 %collective-permute-start.1 = (f32[8,640]{1,0:T(8,128)S(1)}, f32[8,640]{1,0:T(8,128)S(1)}, u32[]{:S(2)}, u32[]{:S(2)}) collective-permute-start(f32[8,640]{1,0:T(8,128)S(1)} %maximum_bitcast_fusion.1), channel_id=1, source_target_pairs={{2,0},{4,2},{6,4},{8,6},{10,8},{12,10},{14,12},{0,14},{3,1},{5,3},... | collective-permute-start | bytes 61448 | tf_op jit(solution)/shard_map/ppermute | solution.py:96
  13.4 2.7 %copy-start.7 = (s32[256]{0:T(256)S(1)}, s32[256]{0:T(256)}, u32[]{:S(2)}) copy-start(s32[256]{0:T(256)} %param.14) | copy-start | bytes 3076
  13.4 2.8 %copy-start.1 = (f32[3,8,16,128]{3,2,1,0:T(8,128)S(1)}, f32[3,8,16,128]{3,2,1,0:T(8,128)}, u32[]{:S(2)}) copy-start(f32[3,8,16,128]{3,2,1,0:T(8,128)} %param.12) | copy-start | bytes 589828
  13.6 2.7 %copy-start.3 = (s32[256,1]{0,1:T(1,128)S(1)}, s32[256,1]{0,1:T(1,128)}, u32[]{:S(2)}) copy-start(s32[256,1]{0,1:T(1,128)} %param.15) | copy-start | bytes 3076
  13.6 3.7 %copy-start.6 = (f32[3,5,5]{2,0,1:T(4,128)S(1)}, f32[3,5,5]{2,0,1:T(4,128)}, u32[]{:S(2)}) copy-start(f32[3,5,5]{2,0,1:T(4,128)} %param.13) | copy-start | bytes 904
  13.6 5.9 %collective-permute-start = (f32[8,640]{1,0:T(8,128)S(1)}, f32[8,640]{1,0:T(8,128)S(1)}, u32[]{:S(2)}, u32[]{:S(2)}) collective-permute-start(f32[8,640]{1,0:T(8,128)S(1)} %maximum_bitcast_fusion), channel_id=1, source_target_pairs={{0,2},{2,4},{4,6},{6,8},{8,10},{10,12},{12,14},{14,0},{1,3},{3,5},... | collective-permute-start | bytes 61448 | tf_op jit(solution)/shard_map/ppermute | solution.py:95
  16.2 1.1 %copy-start.8 = (s32[256]{0:T(256)S(1)}, s32[256]{0:T(256)}, u32[]{:S(2)}) copy-start(s32[256]{0:T(256)} %param.16) | copy-start | bytes 3076
  16.2 1.1 %copy-start.5 = (f32[8,256]{1,0:T(8,128)S(1)}, f32[8,256]{1,0:T(8,128)}, u32[]{:S(2)}) copy-start(f32[8,256]{1,0:T(8,128)} %constant.75.clone) | copy-start | bytes 24580
  16.2 3.2 %copy-start.4 = (f32[8,256]{1,0:T(8,128)S(1)}, f32[8,256]{1,0:T(8,128)}, u32[]{:S(2)}) copy-start(f32[8,256]{1,0:T(8,128)} %constant.74.clone) | copy-start | bytes 24580
  20.4 9.3 %collective-permute-start.4 = (f32[5,8,128]{2,1,0:T(8,128)S(1)}, f32[5,8,128]{2,1,0:T(8,128)S(1)}, u32[]{:S(2)}, u32[]{:S(2)}) collective-permute-start(f32[5,8,128]{2,1,0:T(8,128)S(1)} %select_bitcast_fusion), channel_id=1, source_target_pairs={{0,1},{1,0},{2,3},{3,2},{4,5},{5,4},{6,7},{7,6},{8,9},{9,8},{10,11... | collective-permute-start | bytes 61448 | tf_op jit(solution)/shard_map/ppermute | solution.py:130
  24.4 18.7 %collective-permute-start.2 = (f32[5,16,128]{2,1,0:T(8,128)S(1)}, f32[5,16,128]{2,1,0:T(8,128)S(1)}, u32[]{:S(2)}, u32[]{:S(2)}) collective-permute-start(f32[5,16,128]{2,1,0:T(8,128)S(1)} %get-tuple-element.24), channel_id=1, source_target_pairs={{16,0},{32,16},{48,32},{64,48},{80,64},{96,80},{112,96},{128,112},... | collective-permute-start | bytes 122888 | tf_op jit(solution)/shard_map/ppermute | solution.py:127
  25.7 17.4 %collective-permute-start.3 = (f32[5,16,128]{2,1,0:T(8,128)S(1)}, f32[5,16,128]{2,1,0:T(8,128)S(1)}, u32[]{:S(2)}, u32[]{:S(2)}) collective-permute-start(f32[5,16,128]{2,1,0:T(8,128)S(1)} %get-tuple-element.23), channel_id=1, source_target_pairs={{0,16},{16,32},{32,48},{48,64},{64,80},{80,96},{96,112},{112,128},... | collective-permute-start | bytes 122888 | tf_op jit(solution)/shard_map/ppermute | solution.py:126
  31.6 20.2 %all-to-all-start = ((f32[32,1,192]{2,1,0:T(1,128)}), f32[32,1,192]{2,1,0:T(1,128)S(1)}, u32[]{:S(2)}, u32[]{:S(2)}) async-start(f32[32,1,192]{2,1,0:T(1,128)} %copy.82), calls=%async_computation | async-start | bytes 65536 | tf_op jit(solution)/shard_map/all_to_all | solution.py:122

commit v11 on v10

--- a/solution.py
+++ b/solution.py
@@ -118,8 +118,22 @@
     packed = jnp.concatenate([source, donor_cell.astype(jnp.float32)[None, :]], axis=0)
     by_rank = (slot_rank[None, :] == jnp.arange(capacity, dtype=jnp.int32)[:, None]).astype(jnp.float32)
     spread_out = (packed[:, None, :] * by_rank[None]).reshape((fields + 1) * capacity, -1)
-    outbox = jnp.einsum("qt,to->oq", spread_out, onehot.astype(jnp.float32), precision=HI)
-    received = lax.all_to_all(outbox, "gx", split_axis=0, concat_axis=0, tiled=True)
+    if owners & (owners - 1) == 0:
+        ahead = (owner_rows - lax.axis_index("gx")) % owners
+        rotated = (ahead[:, None] == jnp.arange(owners, dtype=jnp.int32)[None, :]).astype(jnp.float32)
+        received = jnp.einsum("qt,to->oq", spread_out, rotated, precision=HI)
+        width = received.shape[1]
+        step = 1
+        while step < owners:
+            view = received.reshape(owners // (2 * step), 2, step, width)
+            moved = lax.ppermute(
+                view[:, 1], "gx", [(i, (i + step) % owners) for i in range(owners)]
+            )
+            received = view.at[:, 1].set(moved).reshape(owners, width)
+            step *= 2
+    else:
+        outbox = jnp.einsum("qt,to->oq", spread_out, onehot.astype(jnp.float32), precision=HI)
+        received = lax.all_to_all(outbox, "gx", split_axis=0, concat_axis=0, tiled=True)
     taken = jnp.einsum("nk,fna->fka", t_rows, -source[:, :, None] * t_lanes[None], precision=HI)
     up_x, down_x = neighbours(filtered, "gx", False)
     last_x, first_x, last_r, first_r = filtered[:, -1], filtered[:, 0], filtered[:, :, -1], filtered[:, :, 0]

time: 54.6 us -> 75.6 us (1.38)
  the two profiles are of different devices: /device:TPU:1 before, /device:TPU:32 now
where the time goes in v11:
time: 75.6 us; the launch traced here: 75.3 us
  waiting for transfers between devices  33.4 us (44%)
  starting transfers between devices  31.8 us (42%)
  matrix products  3.61 us (5%)
  other arithmetic  2.96 us (4%)
  local copies, waits for them, and re-layouts  2.92 us (4%)
    ppermute x5, waiting for transfers between devices, shards(): lax.ppermute(view[:, 1], 'gx', [(i, (i + step) % owners) for i in range(o...  30.6 us
    ppermute x1, starting transfers between devices, shards(): from_right = lax.ppermute(to_left, 'az', down)  10.9 us
    ppermute x5, starting transfers between devices, shards(): lax.ppermute(view[:, 1], 'gx', [(i, (i + step) % owners) for i in range(o...  10.5 us
    ppermute x1, starting transfers between devices, shards(): after_x = lax.ppermute(first_x, 'gx', down_x)[:, None]  4.55 us
    ppermute x1, waiting for transfers between devices, shards(): from_left = lax.ppermute(to_right, 'az', up)  2.74 us
    ppermute x1, starting transfers between devices, shards(): from_left = lax.ppermute(to_right, 'az', up)  1.92 us
    ppermute x1, starting transfers between devices, shards(): before_x = lax.ppermute(last_x, 'gx', up_x)[:, None]  1.92 us
    ppermute x1, starting transfers between devices, shards(): lax.ppermute(jnp.where(band == 0, last_r, first_r), 'row', [(0, 1), (1, 0)])  1.92 us
  transfers between devices with their start and end apart: 10, of which 6 were waited for; matrix products, arithmetic and copies ran while one was open for 5% of the time, Pallas kernels for 0%

profile of v11, /device:TPU:32, one launch (start us, length us, event | category | flops | bytes accessed | tf_op | source)
XLA Modules:
  0.0 75.3 jit_solution(10976909712836928326)
XLA Ops:
  0.0 1.3 %fusion.38 = (f32[640,7]{1,0:T(8,128)S(1)}, f32[640,7]{1,0:T(8,128)S(1)}) fusion(f32[640,128]{1,0:T(8,128)} %bitcast.187), kind=kLoop, calls=%fused_computation.123 | loop fusion | bytes 71680 | tf_op jit(solution)/shard_map/slice | solution.py:90
  1.4 0.2 multiply_reduce_fusion.1
  1.8 10.9 %collective-permute-start.1 = (f32[8,640]{1,0:T(8,128)S(1)}, f32[8,640]{1,0:T(8,128)S(1)}, u32[]{:S(2)}, u32[]{:S(2)}) collective-permute-start(f32[8,640]{1,0:T(8,128)S(1)} %maximum_bitcast_fusion.1), channel_id=1, source_target_pairs={{2,0},{4,2},{6,4},{8,6},{10,8},{12,10},{14,12},{0,14},{3,1},{5,3},... | collective-permute-start | bytes 61448 | tf_op jit(solution)/shard_map/ppermute | solution.py:96
  13.0 1.9 %collective-permute-start = (f32[8,640]{1,0:T(8,128)S(1)}, f32[8,640]{1,0:T(8,128)S(1)}, u32[]{:S(2)}, u32[]{:S(2)}) collective-permute-start(f32[8,640]{1,0:T(8,128)S(1)} %maximum_bitcast_fusion), channel_id=1, source_target_pairs={{0,2},{2,4},{4,6},{6,8},{8,10},{10,12},{12,14},{14,0},{1,3},{3,5},... | collective-permute-start | bytes 61448 | tf_op jit(solution)/shard_map/ppermute | solution.py:95
  15.0 0.5 convolution_bitcast_fusion.1
  15.6 0.6 reduce-window.6
  16.2 0.2 slice_reduce_fusion
  16.7 0.5 fusion.39
  17.2 2.7 %collective-permute-done = f32[8,640]{1,0:T(8,128)S(1)} collective-permute-done((f32[8,640]{1,0:T(8,128)S(1)}, f32[8,640]{1,0:T(8,128)S(1)}, u32[]{:S(2)}, u32[]{:S(2)}) %collective-permute-start) | collective-permute-done | bytes 20512 | tf_op jit(solution)/shard_map/ppermute | solution.py:95
  19.9 0.5 fusion.4
  20.4 0.2 copy.106
  20.8 1.9 %collective-permute-start.4 = (f32[5,8,128]{2,1,0:T(8,128)S(1)}, f32[5,8,128]{2,1,0:T(8,128)S(1)}, u32[]{:S(2)}, u32[]{:S(2)}) collective-permute-start(f32[5,8,128]{2,1,0:T(8,128)S(1)} %select_bitcast_fusion), channel_id=1, source_target_pairs={{0,1},{1,0},{2,3},{3,2},{4,5},{5,4},{6,7},{7,6},{8,9},{9,8},{10,11... | collective-permute-start | bytes 61448 | tf_op jit(solution)/shard_map/ppermute | solution.py:144
  22.8 4.6 %collective-permute-start.2 = (f32[5,16,128]{2,1,0:T(8,128)S(1)}, f32[5,16,128]{2,1,0:T(8,128)S(1)}, u32[]{:S(2)}, u32[]{:S(2)}) collective-permute-start(f32[5,16,128]{2,1,0:T(8,128)S(1)} %get-tuple-element.84), channel_id=1, source_target_pairs={{16,0},{32,16},{48,32},{64,48},{80,64},{96,80},{112,96},{128,112},... | collective-permute-start | bytes 122888 | tf_op jit(solution)/shard_map/ppermute | solution.py:141
  27.3 1.9 %collective-permute-start.3 = (f32[5,16,128]{2,1,0:T(8,128)S(1)}, f32[5,16,128]{2,1,0:T(8,128)S(1)}, u32[]{:S(2)}, u32[]{:S(2)}) collective-permute-start(f32[5,16,128]{2,1,0:T(8,128)S(1)} %get-tuple-element.83), channel_id=1, source_target_pairs={{0,16},{16,32},{32,48},{48,64},{64,80},{80,96},{96,112},{112,128},... | collective-permute-start | bytes 122888 | tf_op jit(solution)/shard_map/ppermute | solution.py:140
  29.3 0.1 fusion.34
  29.4 0.4 fusion.6
  29.9 0.2 fusion.25
  30.1 2.8 %collective-permute-start.5 = (f32[16,1,192]{2,0,1:T(8,128)S(1)}, f32[16,1,192]{2,0,1:T(8,128)S(1)}, u32[]{:S(2)}, u32[]{:S(2)}) collective-permute-start(f32[16,1,192]{2,0,1:T(8,128)S(1)} %slice_bitcast_fusion.23), channel_id=1, source_target_pairs={{0,16},{16,32},{32,48},{48,64},{64,80},{80,96},{96,112},{112,128},... | collective-permute-start | bytes 36872 | tf_op jit(solution)/shard_map/ppermute | solution.py:129
  32.8 0.3 fusion.7
  33.2 5.8 %collective-permute-done.5 = f32[16,1,192]{2,0,1:T(8,128)S(1)} collective-permute-done((f32[16,1,192]{2,0,1:T(8,128)S(1)}, f32[16,1,192]{2,0,1:T(8,128)S(1)}, u32[]{:S(2)}, u32[]{:S(2)}) %collective-permute-start.5) | collective-permute-done | bytes 12320 | tf_op jit(solution)/shard_map/ppermute | solution.py:129
  39.1 2.0 %collective-permute-start.6 = (f32[8,2,192]{2,0,1:T(8,128)S(1)}, f32[8,2,192]{2,0,1:T(8,128)S(1)}, u32[]{:S(2)}, u32[]{:S(2)}) collective-permute-start(f32[8,2,192]{2,0,1:T(8,128)S(1)} %slice_bitcast_fusion.22), channel_id=1, source_target_pairs={{0,32},{16,48},{32,64},{48,80},{64,96},{80,112},{96,128},{112,144}... | collective-permute-start | bytes 36872 | tf_op jit(solution)/shard_map/ppermute | solution.py:129
  41.2 7.1 %collective-permute-done.6 = f32[8,2,192]{2,0,1:T(8,128)S(1)} collective-permute-done((f32[8,2,192]{2,0,1:T(8,128)S(1)}, f32[8,2,192]{2,0,1:T(8,128)S(1)}, u32[]{:S(2)}, u32[]{:S(2)}) %collective-permute-start.6) | collective-permute-done | bytes 12320 | tf_op jit(solution)/shard_map/ppermute | solution.py:129
  48.4 1.9 %collective-permute-start.7 = (f32[4,4,192]{2,0,1:T(4,128)S(1)}, f32[4,4,192]{2,0,1:T(4,128)S(1)}, u32[]{:S(2)}, u32[]{:S(2)}) collective-permute-start(f32[4,4,192]{2,0,1:T(4,128)S(1)} %bitcast.206), channel_id=1, source_target_pairs={{0,64},{16,80},{32,96},{48,112},{64,128},{80,144},{96,160},{112,17... | collective-permute-start | bytes 36872 | tf_op jit(solution)/shard_map/ppermute | solution.py:129
  50.4 4.9 %collective-permute-done.7 = f32[4,4,192]{2,0,1:T(4,128)S(1)} collective-permute-done((f32[4,4,192]{2,0,1:T(4,128)S(1)}, f32[4,4,192]{2,0,1:T(4,128)S(1)}, u32[]{:S(2)}, u32[]{:S(2)}) %collective-permute-start.7) | collective-permute-done | bytes 12320 | tf_op jit(solution)/shard_map/ppermute | solution.py:129
  55.4 1.9 %collective-permute-start.8 = (f32[2,8,192]{2,1,0:T(8,128)S(1)}, f32[2,8,192]{2,1,0:T(8,128)S(1)}, u32[]{:S(2)}, u32[]{:S(2)}) collective-permute-start(f32[2,8,192]{2,1,0:T(8,128)S(1)} %slice_bitcast_fusion.21), channel_id=1, source_target_pairs={{0,128},{16,144},{32,160},{48,176},{64,192},{80,208},{96,224},{112... | collective-permute-start | bytes 36872 | tf_op jit(solution)/shard_map/ppermute | solution.py:129
  57.4 5.8 %collective-permute-done.8 = f32[2,8,192]{2,1,0:T(8,128)S(1)} collective-permute-done((f32[2,8,192]{2,1,0:T(8,128)S(1)}, f32[2,8,192]{2,1,0:T(8,128)S(1)}, u32[]{:S(2)}, u32[]{:S(2)}) %collective-permute-start.8) | collective-permute-done | bytes 12320 | tf_op jit(solution)/shard_map/ppermute | solution.py:129
  63.2 1.9 %collective-permute-start.9 = (f32[1,16,192]{2,1,0:T(8,128)S(1)}, f32[1,16,192]{2,1,0:T(8,128)S(1)}, u32[]{:S(2)}, u32[]{:S(2)}) collective-permute-start(f32[1,16,192]{2,1,0:T(8,128)S(1)} %slice_bitcast_fusion.20), channel_id=1, source_target_pairs={{0,256},{16,272},{32,288},{48,304},{64,320},{80,336},{96,352},{112... | collective-permute-start | bytes 36872 | tf_op jit(solution)/shard_map/ppermute | solution.py:129
  65.1 0.6 multiply_add_fusion
  65.7 7.0 %collective-permute-done.9 = f32[1,16,192]{2,1,0:T(8,128)S(1)} collective-permute-done((f32[1,16,192]{2,1,0:T(8,128)S(1)}, f32[1,16,192]{2,1,0:T(8,128)S(1)}, u32[]{:S(2)}, u32[]{:S(2)}) %collective-permute-start.9) | collective-permute-done | bytes 12320 | tf_op jit(solution)/shard_map/ppermute | solution.py:129
  72.9 0.2 fusion.9
  73.3 1.2 %fusion = f32[5,128,128]{1,2,0:T(8,128)S(1)} fusion(f32[1024,128]{1,0:T(8,128)S(1)} %fusion.9, f32[5,1024]{1,0:T(8,128)S(1)} %mul.471, s32[1024]{0:T(1024)S(1)} %get-tuple-element.126), kind=kOutput, calls=%fused_computation | convolution fusion | flops 504102912 | bytes 876544 | tf_op jit(solution)/shard_map/nk,fna->fka/dot_general | solution.py:171
  74.5 0.8 %add.128 = f32[5,8,16,128]{3,2,1,0:T(8,128)} add(f32[5,8,16,128]{3,2,1,0:T(8,128)S(1)} %multiply_add_fusion, f32[5,8,16,128]{3,2,1,0:T(8,128)S(1)} %bitcast.194) | non-fusion elementwise | flops 81920 | bytes 983040 | tf_op jit(solution)/shard_map/add | solution.py:172
  (80 shorter events, 1.7 us)
Async XLA Ops:
  0.0 1.4 %copy-start = (f32[5,8,16,128]{3,2,1,0:T(8,128)S(1)}, f32[5,8,16,128]{3,2,1,0:T(8,128)}, u32[]{:S(2)}) copy-start(f32[5,8,16,128]{3,2,1,0:T(8,128)} %param.21) | copy-start | bytes 983044
  0.0 1.4 %copy-start.9 = (f32[128]{0:T(128)S(1)}, f32[128]{0:T(128)}, u32[]{:S(2)}) copy-start(f32[128]{0:T(128)} %constant.200.clone) | copy-start | bytes 1540
  0.0 1.4 %copy-start.10 = (f32[128]{0:T(128)S(1)}, f32[128]{0:T(128)}, u32[]{:S(2)}) copy-start(f32[128]{0:T(128)} %constant.201.clone) | copy-start | bytes 1540
  1.3 13.7 %copy-start.2 = (f32[128,256]{1,0:T(8,128)S(1)}, f32[128,256]{1,0:T(8,128)}, u32[]{:S(2)}) copy-start(f32[128,256]{1,0:T(8,128)} %constant.202.clone) | copy-start | bytes 393220
  1.8 14.9 %collective-permute-start.1 = (f32[8,640]{1,0:T(8,128)S(1)}, f32[8,640]{1,0:T(8,128)S(1)}, u32[]{:S(2)}, u32[]{:S(2)}) collective-permute-start(f32[8,640]{1,0:T(8,128)S(1)} %maximum_bitcast_fusion.1), channel_id=1, source_target_pairs={{2,0},{4,2},{6,4},{8,6},{10,8},{12,10},{14,12},{0,14},{3,1},{5,3},... | collective-permute-start | bytes 61448 | tf_op jit(solution)/shard_map/ppermute | solution.py:96
  12.9 2.6 %copy-start.7 = (s32[256]{0:T(256)S(1)}, s32[256]{0:T(256)}, u32[]{:S(2)}) copy-start(s32[256]{0:T(256)} %param.24) | copy-start | bytes 3076
  12.9 2.7 %copy-start.3 = (s32[256,1]{0,1:T(1,128)S(1)}, s32[256,1]{0,1:T(1,128)}, u32[]{:S(2)}) copy-start(s32[256,1]{0,1:T(1,128)} %param.25) | copy-start | bytes 3076
  13.0 6.9 %collective-permute-start = (f32[8,640]{1,0:T(8,128)S(1)}, f32[8,640]{1,0:T(8,128)S(1)}, u32[]{:S(2)}, u32[]{:S(2)}) collective-permute-start(f32[8,640]{1,0:T(8,128)S(1)} %maximum_bitcast_fusion), channel_id=1, source_target_pairs={{0,2},{2,4},{4,6},{6,8},{8,10},{10,12},{12,14},{14,0},{1,3},{3,5},... | collective-permute-start | bytes 61448 | tf_op jit(solution)/shard_map/ppermute | solution.py:95
  15.0 1.6 %copy-start.6 = (f32[3,5,5]{2,0,1:T(4,128)S(1)}, f32[3,5,5]{2,0,1:T(4,128)}, u32[]{:S(2)}) copy-start(f32[3,5,5]{2,0,1:T(4,128)} %param.23) | copy-start | bytes 904
  15.0 1.6 %copy-start.1 = (f32[3,8,16,128]{3,2,1,0:T(8,128)S(1)}, f32[3,8,16,128]{3,2,1,0:T(8,128)}, u32[]{:S(2)}) copy-start(f32[3,8,16,128]{3,2,1,0:T(8,128)} %param.22) | copy-start | bytes 589828
  15.5 1.1 %copy-start.8 = (s32[256]{0:T(256)S(1)}, s32[256]{0:T(256)}, u32[]{:S(2)}) copy-start(s32[256]{0:T(256)} %param.26) | copy-start | bytes 3076
  15.5 1.2 %copy-start.5 = (f32[8,256]{1,0:T(8,128)S(1)}, f32[8,256]{1,0:T(8,128)}, u32[]{:S(2)}) copy-start(f32[8,256]{1,0:T(8,128)} %constant.204.clone) | copy-start | bytes 24580
  15.6 4.3 %copy-start.4 = (f32[8,256]{1,0:T(8,128)S(1)}, f32[8,256]{1,0:T(8,128)}, u32[]{:S(2)}) copy-start(f32[8,256]{1,0:T(8,128)} %constant.203.clone) | copy-start | bytes 24580
  20.8 8.4 %collective-permute-start.4 = (f32[5,8,128]{2,1,0:T(8,128)S(1)}, f32[5,8,128]{2,1,0:T(8,128)S(1)}, u32[]{:S(2)}, u32[]{:S(2)}) collective-permute-start(f32[5,8,128]{2,1,0:T(8,128)S(1)} %select_bitcast_fusion), channel_id=1, source_target_pairs={{0,1},{1,0},{2,3},{3,2},{4,5},{5,4},{6,7},{7,6},{8,9},{9,8},{10,11... | collective-permute-start | bytes 61448 | tf_op jit(solution)/shard_map/ppermute | solution.py:144
  22.8 18.3 %collective-permute-start.2 = (f32[5,16,128]{2,1,0:T(8,128)S(1)}, f32[5,16,128]{2,1,0:T(8,128)S(1)}, u32[]{:S(2)}, u32[]{:S(2)}) collective-permute-start(f32[5,16,128]{2,1,0:T(8,128)S(1)} %get-tuple-element.84), channel_id=1, source_target_pairs={{16,0},{32,16},{48,32},{64,48},{80,64},{96,80},{112,96},{128,112},... | collective-permute-start | bytes 122888 | tf_op jit(solution)/shard_map/ppermute | solution.py:141
  27.3 13.8 %collective-permute-start.3 = (f32[5,16,128]{2,1,0:T(8,128)S(1)}, f32[5,16,128]{2,1,0:T(8,128)S(1)}, u32[]{:S(2)}, u32[]{:S(2)}) collective-permute-start(f32[5,16,128]{2,1,0:T(8,128)S(1)} %get-tuple-element.83), channel_id=1, source_target_pairs={{0,16},{16,32},{32,48},{48,64},{64,80},{80,96},{96,112},{112,128},... | collective-permute-start | bytes 122888 | tf_op jit(solution)/shard_map/ppermute | solution.py:140
  30.1 9.0 %collective-permute-start.5 = (f32[16,1,192]{2,0,1:T(8,128)S(1)}, f32[16,1,192]{2,0,1:T(8,128)S(1)}, u32[]{:S(2)}, u32[]{:S(2)}) collective-permute-start(f32[16,1,192]{2,0,1:T(8,128)S(1)} %slice_bitcast_fusion.23), channel_id=1, source_target_pairs={{0,16},{16,32},{32,48},{48,64},{64,80},{80,96},{96,112},{112,128},... | collective-permute-start | bytes 36872 | tf_op jit(solution)/shard_map/ppermute | solution.py:129
  39.1 9.2 %collective-permute-start.6 = (f32[8,2,192]{2,0,1:T(8,128)S(1)}, f32[8,2,192]{2,0,1:T(8,128)S(1)}, u32[]{:S(2)}, u32[]{:S(2)}) collective-permute-start(f32[8,2,192]{2,0,1:T(8,128)S(1)} %slice_bitcast_fusion.22), channel_id=1, source_target_pairs={{0,32},{16,48},{32,64},{48,80},{64,96},{80,112},{96,128},{112,144}... | collective-permute-start | bytes 36872 | tf_op jit(solution)/shard_map/ppermute | solution.py:129
  48.4 6.8 %collective-permute-start.7 = (f32[4,4,192]{2,0,1:T(4,128)S(1)}, f32[4,4,192]{2,0,1:T(4,128)S(1)}, u32[]{:S(2)}, u32[]{:S(2)}) collective-permute-start(f32[4,4,192]{2,0,1:T(4,128)S(1)} %bitcast.206), channel_id=1, source_target_pairs={{0,64},{16,80},{32,96},{48,112},{64,128},{80,144},{96,160},{112,17... | collective-permute-start | bytes 36872 | tf_op jit(solution)/shard_map/ppermute | solution.py:129
  55.4 7.7 %collective-permute-start.8 = (f32[2,8,192]{2,1,0:T(8,128)S(1)}, f32[2,8,192]{2,1,0:T(8,128)S(1)}, u32[]{:S(2)}, u32[]{:S(2)}) collective-permute-start(f32[2,8,192]{2,1,0:T(8,128)S(1)} %slice_bitcast_fusion.21), channel_id=1, source_target_pairs={{0,128},{16,144},{32,160},{48,176},{64,192},{80,208},{96,224},{112... | collective-permute-start | bytes 36872 | tf_op jit(solution)/shard_map/ppermute | solution.py:129
  63.2 9.5 %collective-permute-start.9 = (f32[1,16,192]{2,1,0:T(8,128)S(1)}, f32[1,16,192]{2,1,0:T(8,128)S(1)}, u32[]{:S(2)}, u32[]{:S(2)}) collective-permute-start(f32[1,16,192]{2,1,0:T(8,128)S(1)} %slice_bitcast_fusion.20), channel_id=1, source_target_pairs={{0,256},{16,272},{32,288},{48,304},{64,320},{80,336},{96,352},{112... | collective-permute-start | bytes 36872 | tf_op jit(solution)/shard_map/ppermute | solution.py:129

commit v12 on v10

--- a/solution.py
+++ b/solution.py
@@ -153,8 +153,8 @@
     got_cell = received[fields].astype(jnp.int32)
     d_rows = (got_cell[:, None] // cells_a == row_ids[None, :]).astype(jnp.float32)
     d_lanes = (got_cell[:, None] % cells_a == lane_ids[None, :]).astype(jnp.float32)
-    spread = received[:fields, :, None] * d_lanes[None]
-    update = jnp.einsum("nk,fna->fka", d_rows, spread, precision=HI)
+    weighted = (received[:fields, None, :] * d_rows.T[None]).reshape(fields * rows, -1)
+    update = jnp.dot(weighted, d_lanes, precision=HI)
     return gradient + update.reshape(adjoint.shape)
 
 

time: 54.6 us -> 54.2 us (level)
  other arithmetic: 2.95 us -> 2.08 us
    add x1 -> x0, other arithmetic: 0.77 us -> none  [shards(): return gradient + update.reshape(adjoint.shape)]
where the time goes in v12:
time: 54.2 us; the launch traced here: 53.9 us
  starting transfers between devices  34.4 us (63%)
  waiting for transfers between devices  9.54 us (18%)
  matrix products  4.1 us (8%)
  local copies, waits for them, and re-layouts  3.33 us (6%)
  other arithmetic  2.08 us (4%)
    all_to_all x1, starting transfers between devices, shards(): lax.all_to_all(outbox, 'gx', split_axis=0, concat_axis=0, tiled=True)  11.5 us
    ppermute x1, starting transfers between devices, shards(): from_right = lax.ppermute(to_left, 'az', down)  11.5 us
    all_to_all x1, waiting for transfers between devices, shards(): lax.all_to_all(outbox, 'gx', split_axis=0, concat_axis=0, tiled=True)  7.89 us
    ppermute x1, starting transfers between devices, shards(): lax.ppermute(jnp.where(band == 0, last_r, first_r), 'row', [(0, 1), (1, 0)])  4.01 us
    ppermute x1, starting transfers between devices, shards(): before_x = lax.ppermute(last_x, 'gx', up_x)[:, None]  3.99 us
    ppermute x1, starting transfers between devices, shards(): from_left = lax.ppermute(to_right, 'az', up)  2.05 us
    dot_general x1, matrix products, shards(): update = jnp.dot(weighted, d_lanes, precision=HI)  1.66 us
    ppermute x1, waiting for transfers between devices, shards(): from_left = lax.ppermute(to_right, 'az', up)  1.64 us
  transfers between devices with their start and end apart: 6, of which 2 were waited for; matrix products, arithmetic and copies ran while one was open for 9% of the time, Pallas kernels for 0%

profile of v12, /device:TPU:1, one launch (start us, length us, event | category | flops | bytes accessed | tf_op | source)
XLA Modules:
  0.0 53.9 jit_solution(10734626521310406535)
XLA Ops:
  0.0 1.3 %fusion.38 = (f32[640,7]{1,0:T(8,128)S(1)}, f32[640,7]{1,0:T(8,128)S(1)}) fusion(f32[640,128]{1,0:T(8,128)} %bitcast.152), kind=kLoop, calls=%fused_computation.111 | loop fusion | bytes 71680 | tf_op jit(solution)/shard_map/slice | solution.py:90
  1.3 0.1 copy.70
  1.4 0.2 multiply_reduce_fusion.1
  1.7 0.1 broadcast_in_dim.19
  1.8 11.5 %collective-permute-start.1 = (f32[8,640]{1,0:T(8,128)S(1)}, f32[8,640]{1,0:T(8,128)S(1)}, u32[]{:S(2)}, u32[]{:S(2)}) collective-permute-start(f32[8,640]{1,0:T(8,128)S(1)} %maximum_bitcast_fusion.1), channel_id=1, source_target_pairs={{2,0},{4,2},{6,4},{8,6},{10,8},{12,10},{14,12},{0,14},{3,1},{5,3},... | collective-permute-start | bytes 61448 | tf_op jit(solution)/shard_map/ppermute | solution.py:96
  13.3 0.1 copy.68
  13.4 0.1 broadcast_in_dim.18
  13.6 2.1 %collective-permute-start = (f32[8,640]{1,0:T(8,128)S(1)}, f32[8,640]{1,0:T(8,128)S(1)}, u32[]{:S(2)}, u32[]{:S(2)}) collective-permute-start(f32[8,640]{1,0:T(8,128)S(1)} %maximum_bitcast_fusion), channel_id=1, source_target_pairs={{0,2},{2,4},{4,6},{6,8},{8,10},{10,12},{12,14},{14,0},{1,3},{3,5},... | collective-permute-start | bytes 61448 | tf_op jit(solution)/shard_map/ppermute | solution.py:95
  15.6 0.5 convolution_bitcast_fusion.1
  16.3 0.6 %reduce-window.6 = s32[32,2,128]{2,0,1:T(8,128)S(1)} reduce-window(s32[32,2,128]{2,0,1:T(8,128)S(1)} %fusion.27, s32[]{:T(128)} %constant.65.clone.1), window={size=1x1x128 pad=0_0x0_0x127_0}, to_apply=%region_3.4 | reduce-window | flops 1040384 | bytes 65540 | tf_op jit(solution)/shard_map/reduce-window
  16.9 0.2 slice_reduce_fusion
  17.1 0.1 fusion.24
  17.3 0.5 fusion.39
  17.8 1.6 %collective-permute-done = f32[8,640]{1,0:T(8,128)S(1)} collective-permute-done((f32[8,640]{1,0:T(8,128)S(1)}, f32[8,640]{1,0:T(8,128)S(1)}, u32[]{:S(2)}, u32[]{:S(2)}) %collective-permute-start) | collective-permute-done | bytes 20512 | tf_op jit(solution)/shard_map/ppermute | solution.py:95
  19.5 0.5 fusion.4
  20.0 0.2 copy.72
  20.4 4.0 %collective-permute-start.4 = (f32[5,8,128]{2,1,0:T(8,128)S(1)}, f32[5,8,128]{2,1,0:T(8,128)S(1)}, u32[]{:S(2)}, u32[]{:S(2)}) collective-permute-start(f32[5,8,128]{2,1,0:T(8,128)S(1)} %select_bitcast_fusion), channel_id=1, source_target_pairs={{0,1},{1,0},{2,3},{3,2},{4,5},{5,4},{6,7},{7,6},{8,9},{9,8},{10,11... | collective-permute-start | bytes 61448 | tf_op jit(solution)/shard_map/ppermute | solution.py:130
  24.4 1.3 %collective-permute-start.2 = (f32[5,16,128]{2,1,0:T(8,128)S(1)}, f32[5,16,128]{2,1,0:T(8,128)S(1)}, u32[]{:S(2)}, u32[]{:S(2)}) collective-permute-start(f32[5,16,128]{2,1,0:T(8,128)S(1)} %get-tuple-element.24), channel_id=1, source_target_pairs={{16,0},{32,16},{48,32},{64,48},{80,64},{96,80},{112,96},{128,112},... | collective-permute-start | bytes 122888 | tf_op jit(solution)/shard_map/ppermute | solution.py:127
  25.7 4.0 %collective-permute-start.3 = (f32[5,16,128]{2,1,0:T(8,128)S(1)}, f32[5,16,128]{2,1,0:T(8,128)S(1)}, u32[]{:S(2)}, u32[]{:S(2)}) collective-permute-start(f32[5,16,128]{2,1,0:T(8,128)S(1)} %get-tuple-element.23), channel_id=1, source_target_pairs={{0,16},{16,32},{32,48},{48,64},{64,80},{80,96},{96,112},{112,128},... | collective-permute-start | bytes 122888 | tf_op jit(solution)/shard_map/ppermute | solution.py:126
  29.7 0.1 fusion.34
  29.9 0.4 fusion.6
  30.3 0.3 fusion.10
  30.7 0.2 convolution_bitcast_fusion.2
  30.9 0.6 %copy.82 = f32[32,1,192]{2,1,0:T(1,128)} copy(f32[32,1,192]{2,0,1:T(8,128)S(1)} %convolution_bitcast_fusion.2) | data formatting | bytes 49152 | tf_op jit(solution)/shard_map/all_to_all | solution.py:122
  31.5 11.5 %all-to-all-start = ((f32[32,1,192]{2,1,0:T(1,128)}), f32[32,1,192]{2,1,0:T(1,128)S(1)}, u32[]{:S(2)}, u32[]{:S(2)}) async-start(f32[32,1,192]{2,1,0:T(1,128)} %copy.82), calls=%async_computation | async-start | bytes 65536 | tf_op jit(solution)/shard_map/all_to_all | solution.py:122
  43.3 0.6 %multiply_add_fusion = f32[5,8,16,128]{3,2,1,0:T(8,128)S(1)} fusion(f32[5,8,16,128]{3,2,1,0:T(8,128)S(1)} %bitcast.154, f32[8,16,128]{2,1,0:T(8,128)S(1)} %get-tuple-element.38, f32[5]{0:T(128)S(1)} %get-tuple-element.62, f32[8,16,128]{2,1,0:T(8,128)S(1)} %get-tuple-element.39, f32[5]{0:T(128)S(1)} %get-tuple-element.63, ...), kind=kLoop, calls=%fused_computation.19 | loop fusion | flops 2785280 | bytes 2162988 | tf_op jit(solution)/shard_map/add | solution.py:149
  43.9 7.9 %all-to-all-done = f32[32,1,192]{2,1,0:T(1,128)S(1)} async-done(((f32[32,1,192]{2,1,0:T(1,128)}), f32[32,1,192]{2,1,0:T(1,128)S(1)}, u32[]{:S(2)}, u32[]{:S(2)}) %all-to-all-start) | async-done | bytes 24608 | tf_op jit(solution)/shard_map/all_to_all | solution.py:122
  51.8 0.1 reshape.244
  51.9 0.1 convert_element_type.57
  52.0 0.1 mul.468
  52.1 0.1 compare_convert_fusion
  52.2 1.7 %fusion.7 = f32[5,8,16,128]{3,2,1,0:T(8,128)} fusion(f32[5,8,16,128]{3,2,1,0:T(8,128)S(1)} %multiply_add_fusion, f32[8,16,1024]{2,1,0:T(8,128)S(1)} %compare_convert_fusion, f32[5,1024]{1,0:T(8,128)S(1)} %mul.468, s32[1024]{0:T(1024)S(1)} %get-tuple-element.66), kind=kOutput, calls=%fused_computation.10 | convolution fusion | flops 504184832 | bytes 1204224 | tf_op jit(solution)/shard_map/dot_general | solution.py:157
  (55 shorter events, 0.6 us)
Async XLA Ops:
  0.0 1.4 %copy-start = (f32[5,8,16,128]{3,2,1,0:T(8,128)S(1)}, f32[5,8,16,128]{3,2,1,0:T(8,128)}, u32[]{:S(2)}) copy-start(f32[5,8,16,128]{3,2,1,0:T(8,128)} %param.11) | copy-start | bytes 983044
  0.0 1.4 %copy-start.9 = (f32[128]{0:T(128)S(1)}, f32[128]{0:T(128)}, u32[]{:S(2)}) copy-start(f32[128]{0:T(128)} %constant.73.clone) | copy-start | bytes 1540
  0.0 1.4 %copy-start.10 = (f32[128]{0:T(128)S(1)}, f32[128]{0:T(128)}, u32[]{:S(2)}) copy-start(f32[128]{0:T(128)} %constant.74.clone) | copy-start | bytes 1540
  1.3 14.4 %copy-start.2 = (f32[128,256]{1,0:T(8,128)S(1)}, f32[128,256]{1,0:T(8,128)}, u32[]{:S(2)}) copy-start(f32[128,256]{1,0:T(8,128)} %constant.75.clone) | copy-start | bytes 393220
  1.8 15.5 %collective-permute-start.1 = (f32[8,640]{1,0:T(8,128)S(1)}, f32[8,640]{1,0:T(8,128)S(1)}, u32[]{:S(2)}, u32[]{:S(2)}) collective-permute-start(f32[8,640]{1,0:T(8,128)S(1)} %maximum_bitcast_fusion.1), channel_id=1, source_target_pairs={{2,0},{4,2},{6,4},{8,6},{10,8},{12,10},{14,12},{0,14},{3,1},{5,3},... | collective-permute-start | bytes 61448 | tf_op jit(solution)/shard_map/ppermute | solution.py:96
  13.4 2.7 %copy-start.7 = (s32[256]{0:T(256)S(1)}, s32[256]{0:T(256)}, u32[]{:S(2)}) copy-start(s32[256]{0:T(256)} %param.14) | copy-start | bytes 3076
  13.4 2.8 %copy-start.6 = (f32[3,5,5]{2,0,1:T(4,128)S(1)}, f32[3,5,5]{2,0,1:T(4,128)}, u32[]{:S(2)}) copy-start(f32[3,5,5]{2,0,1:T(4,128)} %param.13) | copy-start | bytes 904
  13.5 2.7 %copy-start.1 = (f32[3,8,16,128]{3,2,1,0:T(8,128)S(1)}, f32[3,8,16,128]{3,2,1,0:T(8,128)}, u32[]{:S(2)}) copy-start(f32[3,8,16,128]{3,2,1,0:T(8,128)} %param.12) | copy-start | bytes 589828
  13.6 2.7 %copy-start.3 = (s32[256,1]{0,1:T(1,128)S(1)}, s32[256,1]{0,1:T(1,128)}, u32[]{:S(2)}) copy-start(s32[256,1]{0,1:T(1,128)} %param.15) | copy-start | bytes 3076
  13.6 5.9 %collective-permute-start = (f32[8,640]{1,0:T(8,128)S(1)}, f32[8,640]{1,0:T(8,128)S(1)}, u32[]{:S(2)}, u32[]{:S(2)}) collective-permute-start(f32[8,640]{1,0:T(8,128)S(1)} %maximum_bitcast_fusion), channel_id=1, source_target_pairs={{0,2},{2,4},{4,6},{6,8},{8,10},{10,12},{12,14},{14,0},{1,3},{3,5},... | collective-permute-start | bytes 61448 | tf_op jit(solution)/shard_map/ppermute | solution.py:95
  16.2 1.1 %copy-start.8 = (s32[256]{0:T(256)S(1)}, s32[256]{0:T(256)}, u32[]{:S(2)}) copy-start(s32[256]{0:T(256)} %param.16) | copy-start | bytes 3076
  16.2 1.1 %copy-start.5 = (f32[8,256]{1,0:T(8,128)S(1)}, f32[8,256]{1,0:T(8,128)}, u32[]{:S(2)}) copy-start(f32[8,256]{1,0:T(8,128)} %constant.77.clone) | copy-start | bytes 24580
  16.3 3.2 %copy-start.4 = (f32[8,256]{1,0:T(8,128)S(1)}, f32[8,256]{1,0:T(8,128)}, u32[]{:S(2)}) copy-start(f32[8,256]{1,0:T(8,128)} %constant.76.clone) | copy-start | bytes 24580
  20.4 9.3 %collective-permute-start.4 = (f32[5,8,128]{2,1,0:T(8,128)S(1)}, f32[5,8,128]{2,1,0:T(8,128)S(1)}, u32[]{:S(2)}, u32[]{:S(2)}) collective-permute-start(f32[5,8,128]{2,1,0:T(8,128)S(1)} %select_bitcast_fusion), channel_id=1, source_target_pairs={{0,1},{1,0},{2,3},{3,2},{4,5},{5,4},{6,7},{7,6},{8,9},{9,8},{10,11... | collective-permute-start | bytes 61448 | tf_op jit(solution)/shard_map/ppermute | solution.py:130
  24.4 18.7 %collective-permute-start.2 = (f32[5,16,128]{2,1,0:T(8,128)S(1)}, f32[5,16,128]{2,1,0:T(8,128)S(1)}, u32[]{:S(2)}, u32[]{:S(2)}) collective-permute-start(f32[5,16,128]{2,1,0:T(8,128)S(1)} %get-tuple-element.24), channel_id=1, source_target_pairs={{16,0},{32,16},{48,32},{64,48},{80,64},{96,80},{112,96},{128,112},... | collective-permute-start | bytes 122888 | tf_op jit(solution)/shard_map/ppermute | solution.py:127
  25.7 17.4 %collective-permute-start.3 = (f32[5,16,128]{2,1,0:T(8,128)S(1)}, f32[5,16,128]{2,1,0:T(8,128)S(1)}, u32[]{:S(2)}, u32[]{:S(2)}) collective-permute-start(f32[5,16,128]{2,1,0:T(8,128)S(1)} %get-tuple-element.23), channel_id=1, source_target_pairs={{0,16},{16,32},{32,48},{48,64},{64,80},{80,96},{96,112},{112,128},... | collective-permute-start | bytes 122888 | tf_op jit(solution)/shard_map/ppermute | solution.py:126
  31.5 20.2 %all-to-all-start = ((f32[32,1,192]{2,1,0:T(1,128)}), f32[32,1,192]{2,1,0:T(1,128)S(1)}, u32[]{:S(2)}, u32[]{:S(2)}) async-start(f32[32,1,192]{2,1,0:T(1,128)} %copy.82), calls=%async_computation | async-start | bytes 65536 | tf_op jit(solution)/shard_map/all_to_all | solution.py:122

commit v13 on v12

--- a/solution.py
+++ b/solution.py
@@ -105,9 +105,9 @@
     lane_ids = jnp.arange(cells_a, dtype=jnp.int32)
     t_rows = (target_cell[:, None] // cells_a == row_ids[None, :]).astype(jnp.float32)
     t_lanes = (target_cell[:, None] % cells_a == lane_ids[None, :]).astype(jnp.float32)
-    flat = filtered.reshape(fields, rows, cells_a)
-    picked = jnp.einsum("tk,fka->fta", t_rows, flat, precision=HI)
-    source = sat_gain * jnp.sum(picked * t_lanes[None], axis=2)
+    flat = filtered.reshape(fields * rows, cells_a)
+    by_lane = jnp.einsum("la,ta->lt", flat, t_lanes, precision=HI).reshape(fields, rows, -1)
+    source = sat_gain * jnp.sum(by_lane * t_rows.T[None], axis=1)
 
     owner_rows = donor_owner[:, 0]
     owners = lax.axis_size("gx")

time: 54.2 us -> 53.9 us (level)
  waiting for transfers between devices: 9.54 us -> 8.97 us
where the time goes in v13:
time: 53.9 us; the launch traced here: 53.6 us
  starting transfers between devices  34.4 us (64%)
  waiting for transfers between devices  8.97 us (17%)
  matrix products  4.24 us (8%)
  local copies, waits for them, and re-layouts  3.34 us (6%)
  other arithmetic  2.18 us (4%)
    all_to_all x1, starting transfers between devices, shards(): lax.all_to_all(outbox, 'gx', split_axis=0, concat_axis=0, tiled=True)  11.5 us
    ppermute x1, starting transfers between devices, shards(): from_right = lax.ppermute(to_left, 'az', down)  11.5 us
    all_to_all x1, waiting for transfers between devices, shards(): lax.all_to_all(outbox, 'gx', split_axis=0, concat_axis=0, tiled=True)  7.43 us
    ppermute x1, starting transfers between devices, shards(): lax.ppermute(jnp.where(band == 0, last_r, first_r), 'row', [(0, 1), (1, 0)])  4.01 us
    ppermute x1, starting transfers between devices, shards(): before_x = lax.ppermute(last_x, 'gx', up_x)[:, None]  3.99 us
    ppermute x1, starting transfers between devices, shards(): from_left = lax.ppermute(to_right, 'az', up)  2.05 us
    dot_general x1, matrix products, shards(): update = jnp.dot(weighted, d_lanes, precision=HI)  1.66 us
    ppermute x1, waiting for transfers between devices, shards(): from_left = lax.ppermute(to_right, 'az', up)  1.53 us
  transfers between devices with their start and end apart: 6, of which 2 were waited for; matrix products, arithmetic and copies ran while one was open for 9% of the time, Pallas kernels for 0%

profile of v13, /device:TPU:1, one launch (start us, length us, event | category | flops | bytes accessed | tf_op | source)
XLA Modules:
  0.0 53.6 jit_solution(16293244575406467574)
XLA Ops:
  0.0 1.3 %fusion.39 = (f32[640,7]{1,0:T(8,128)S(1)}, f32[640,7]{1,0:T(8,128)S(1)}) fusion(f32[640,128]{1,0:T(8,128)} %bitcast.147), kind=kLoop, calls=%fused_computation.113 | loop fusion | bytes 71680 | tf_op jit(solution)/shard_map/slice | solution.py:90
  1.3 0.1 copy.61
  1.4 0.2 multiply_reduce_fusion.1
  1.7 0.1 broadcast_in_dim.19
  1.8 11.5 %collective-permute-start.1 = (f32[8,640]{1,0:T(8,128)S(1)}, f32[8,640]{1,0:T(8,128)S(1)}, u32[]{:S(2)}, u32[]{:S(2)}) collective-permute-start(f32[8,640]{1,0:T(8,128)S(1)} %maximum_bitcast_fusion.1), channel_id=1, source_target_pairs={{2,0},{4,2},{6,4},{8,6},{10,8},{12,10},{14,12},{0,14},{3,1},{5,3},... | collective-permute-start | bytes 61448 | tf_op jit(solution)/shard_map/ppermute | solution.py:96
  13.3 0.1 copy.59
  13.4 0.1 broadcast_in_dim.18
  13.6 2.1 %collective-permute-start = (f32[8,640]{1,0:T(8,128)S(1)}, f32[8,640]{1,0:T(8,128)S(1)}, u32[]{:S(2)}, u32[]{:S(2)}) collective-permute-start(f32[8,640]{1,0:T(8,128)S(1)} %maximum_bitcast_fusion), channel_id=1, source_target_pairs={{0,2},{2,4},{4,6},{6,8},{8,10},{10,12},{12,14},{14,0},{1,3},{3,5},... | collective-permute-start | bytes 61448 | tf_op jit(solution)/shard_map/ppermute | solution.py:95
  15.7 0.5 convolution_bitcast_fusion
  16.2 0.1 fusion.16
  16.4 0.6 %reduce-window.6 = s32[32,2,128]{2,0,1:T(8,128)S(1)} reduce-window(s32[32,2,128]{2,0,1:T(8,128)S(1)} %fusion.28, s32[]{:T(128)} %constant.64.clone.1), window={size=1x1x128 pad=0_0x0_0x127_0}, to_apply=%region_3.4 | reduce-window | flops 1040384 | bytes 65540 | tf_op jit(solution)/shard_map/reduce-window
  17.0 0.2 slice_reduce_fusion
  17.3 0.1 fusion.25
  17.4 0.5 fusion.40
  17.9 1.5 %collective-permute-done = f32[8,640]{1,0:T(8,128)S(1)} collective-permute-done((f32[8,640]{1,0:T(8,128)S(1)}, f32[8,640]{1,0:T(8,128)S(1)}, u32[]{:S(2)}, u32[]{:S(2)}) %collective-permute-start) | collective-permute-done | bytes 20512 | tf_op jit(solution)/shard_map/ppermute | solution.py:95
  19.5 0.5 fusion.4
  20.0 0.2 copy.63
  20.4 4.0 %collective-permute-start.4 = (f32[5,8,128]{2,1,0:T(8,128)S(1)}, f32[5,8,128]{2,1,0:T(8,128)S(1)}, u32[]{:S(2)}, u32[]{:S(2)}) collective-permute-start(f32[5,8,128]{2,1,0:T(8,128)S(1)} %select_bitcast_fusion), channel_id=1, source_target_pairs={{0,1},{1,0},{2,3},{3,2},{4,5},{5,4},{6,7},{7,6},{8,9},{9,8},{10,11... | collective-permute-start | bytes 61448 | tf_op jit(solution)/shard_map/ppermute | solution.py:130
  24.4 1.3 %collective-permute-start.2 = (f32[5,16,128]{2,1,0:T(8,128)S(1)}, f32[5,16,128]{2,1,0:T(8,128)S(1)}, u32[]{:S(2)}, u32[]{:S(2)}) collective-permute-start(f32[5,16,128]{2,1,0:T(8,128)S(1)} %get-tuple-element.24), channel_id=1, source_target_pairs={{16,0},{32,16},{48,32},{64,48},{80,64},{96,80},{112,96},{128,112},... | collective-permute-start | bytes 122888 | tf_op jit(solution)/shard_map/ppermute | solution.py:127
  25.7 4.0 %collective-permute-start.3 = (f32[5,16,128]{2,1,0:T(8,128)S(1)}, f32[5,16,128]{2,1,0:T(8,128)S(1)}, u32[]{:S(2)}, u32[]{:S(2)}) collective-permute-start(f32[5,16,128]{2,1,0:T(8,128)S(1)} %get-tuple-element.23), channel_id=1, source_target_pairs={{0,16},{16,32},{32,48},{48,64},{64,80},{80,96},{96,112},{112,128},... | collective-permute-start | bytes 122888 | tf_op jit(solution)/shard_map/ppermute | solution.py:126
  29.7 0.1 fusion.35
  29.9 0.4 fusion.5
  30.4 0.2 convolution_bitcast_fusion.1
  30.6 0.6 %copy.70 = f32[32,1,192]{2,1,0:T(1,128)} copy(f32[32,1,192]{2,0,1:T(8,128)S(1)} %convolution_bitcast_fusion.1) | data formatting | bytes 49152 | tf_op jit(solution)/shard_map/all_to_all | solution.py:122
  31.2 11.5 %all-to-all-start = ((f32[32,1,192]{2,1,0:T(1,128)}), f32[32,1,192]{2,1,0:T(1,128)S(1)}, u32[]{:S(2)}, u32[]{:S(2)}) async-start(f32[32,1,192]{2,1,0:T(1,128)} %copy.70), calls=%async_computation | async-start | bytes 65536 | tf_op jit(solution)/shard_map/all_to_all | solution.py:122
  42.8 0.4 fusion.9
  43.4 0.6 %multiply_add_fusion = f32[5,8,16,128]{3,2,1,0:T(8,128)S(1)} fusion(f32[5,8,16,128]{3,2,1,0:T(8,128)S(1)} %bitcast.149, f32[8,16,128]{2,1,0:T(8,128)S(1)} %get-tuple-element.38, f32[5]{0:T(128)S(1)} %get-tuple-element.62, f32[8,16,128]{2,1,0:T(8,128)S(1)} %get-tuple-element.39, f32[5]{0:T(128)S(1)} %get-tuple-element.63, ...), kind=kLoop, calls=%fused_computation.18 | loop fusion | flops 2785280 | bytes 2162988 | tf_op jit(solution)/shard_map/add | solution.py:149
  44.0 7.4 %all-to-all-done = f32[32,1,192]{2,1,0:T(1,128)S(1)} async-done(((f32[32,1,192]{2,1,0:T(1,128)}), f32[32,1,192]{2,1,0:T(1,128)S(1)}, u32[]{:S(2)}, u32[]{:S(2)}) %all-to-all-start) | async-done | bytes 24608 | tf_op jit(solution)/shard_map/all_to_all | solution.py:122
  51.5 0.1 reshape.264
  51.7 0.1 mul.471
  51.8 0.1 compare_convert_fusion
  51.9 1.7 %fusion.6 = f32[5,8,16,128]{3,2,1,0:T(8,128)} fusion(f32[5,8,16,128]{3,2,1,0:T(8,128)S(1)} %multiply_add_fusion, f32[8,16,1024]{2,1,0:T(8,128)S(1)} %compare_convert_fusion, f32[5,1024]{1,0:T(8,128)S(1)} %mul.471, s32[1024]{0:T(1024)S(1)} %get-tuple-element.66), kind=kOutput, calls=%fused_computation.9 | convolution fusion | flops 504184832 | bytes 1204224 | tf_op jit(solution)/shard_map/dot_general | solution.py:157
  (56 shorter events, 0.7 us)
Async XLA Ops:
  0.0 1.4 %copy-start = (f32[5,8,16,128]{3,2,1,0:T(8,128)S(1)}, f32[5,8,16,128]{3,2,1,0:T(8,128)}, u32[]{:S(2)}) copy-start(f32[5,8,16,128]{3,2,1,0:T(8,128)} %param.11) | copy-start | bytes 983044
  0.0 1.4 %copy-start.9 = (f32[128]{0:T(128)S(1)}, f32[128]{0:T(128)}, u32[]{:S(2)}) copy-start(f32[128]{0:T(128)} %constant.73.clone) | copy-start | bytes 1540
  0.0 1.4 %copy-start.10 = (f32[128]{0:T(128)S(1)}, f32[128]{0:T(128)}, u32[]{:S(2)}) copy-start(f32[128]{0:T(128)} %constant.74.clone) | copy-start | bytes 1540
  1.3 14.4 %copy-start.2 = (f32[128,256]{1,0:T(8,128)S(1)}, f32[128,256]{1,0:T(8,128)}, u32[]{:S(2)}) copy-start(f32[128,256]{1,0:T(8,128)} %constant.75.clone) | copy-start | bytes 393220
  1.8 15.6 %collective-permute-start.1 = (f32[8,640]{1,0:T(8,128)S(1)}, f32[8,640]{1,0:T(8,128)S(1)}, u32[]{:S(2)}, u32[]{:S(2)}) collective-permute-start(f32[8,640]{1,0:T(8,128)S(1)} %maximum_bitcast_fusion.1), channel_id=1, source_target_pairs={{2,0},{4,2},{6,4},{8,6},{10,8},{12,10},{14,12},{0,14},{3,1},{5,3},... | collective-permute-start | bytes 61448 | tf_op jit(solution)/shard_map/ppermute | solution.py:96
  13.4 2.7 %copy-start.7 = (s32[256]{0:T(256)S(1)}, s32[256]{0:T(256)}, u32[]{:S(2)}) copy-start(s32[256]{0:T(256)} %param.14) | copy-start | bytes 3076
  13.6 2.8 %copy-start.6 = (f32[3,5,5]{2,0,1:T(4,128)S(1)}, f32[3,5,5]{2,0,1:T(4,128)}, u32[]{:S(2)}) copy-start(f32[3,5,5]{2,0,1:T(4,128)} %param.13) | copy-start | bytes 904
  13.6 2.8 %copy-start.1 = (f32[3,8,16,128]{3,2,1,0:T(8,128)S(1)}, f32[3,8,16,128]{3,2,1,0:T(8,128)}, u32[]{:S(2)}) copy-start(f32[3,8,16,128]{3,2,1,0:T(8,128)} %param.12) | copy-start | bytes 589828
  13.6 2.8 %copy-start.3 = (s32[256,1]{0,1:T(1,128)S(1)}, s32[256,1]{0,1:T(1,128)}, u32[]{:S(2)}) copy-start(s32[256,1]{0,1:T(1,128)} %param.15) | copy-start | bytes 3076
  13.6 5.9 %collective-permute-start = (f32[8,640]{1,0:T(8,128)S(1)}, f32[8,640]{1,0:T(8,128)S(1)}, u32[]{:S(2)}, u32[]{:S(2)}) collective-permute-start(f32[8,640]{1,0:T(8,128)S(1)} %maximum_bitcast_fusion), channel_id=1, source_target_pairs={{0,2},{2,4},{4,6},{6,8},{8,10},{10,12},{12,14},{14,0},{1,3},{3,5},... | collective-permute-start | bytes 61448 | tf_op jit(solution)/shard_map/ppermute | solution.py:95
  16.2 1.2 %copy-start.8 = (s32[256]{0:T(256)S(1)}, s32[256]{0:T(256)}, u32[]{:S(2)}) copy-start(s32[256]{0:T(256)} %param.16) | copy-start | bytes 3076
  16.2 1.2 %copy-start.5 = (f32[8,256]{1,0:T(8,128)S(1)}, f32[8,256]{1,0:T(8,128)}, u32[]{:S(2)}) copy-start(f32[8,256]{1,0:T(8,128)} %constant.77.clone) | copy-start | bytes 24580
  16.4 3.1 %copy-start.4 = (f32[8,256]{1,0:T(8,128)S(1)}, f32[8,256]{1,0:T(8,128)}, u32[]{:S(2)}) copy-start(f32[8,256]{1,0:T(8,128)} %constant.76.clone) | copy-start | bytes 24580
  20.4 9.3 %collective-permute-start.4 = (f32[5,8,128]{2,1,0:T(8,128)S(1)}, f32[5,8,128]{2,1,0:T(8,128)S(1)}, u32[]{:S(2)}, u32[]{:S(2)}) collective-permute-start(f32[5,8,128]{2,1,0:T(8,128)S(1)} %select_bitcast_fusion), channel_id=1, source_target_pairs={{0,1},{1,0},{2,3},{3,2},{4,5},{5,4},{6,7},{7,6},{8,9},{9,8},{10,11... | collective-permute-start | bytes 61448 | tf_op jit(solution)/shard_map/ppermute | solution.py:130
  24.4 18.8 %collective-permute-start.2 = (f32[5,16,128]{2,1,0:T(8,128)S(1)}, f32[5,16,128]{2,1,0:T(8,128)S(1)}, u32[]{:S(2)}, u32[]{:S(2)}) collective-permute-start(f32[5,16,128]{2,1,0:T(8,128)S(1)} %get-tuple-element.24), channel_id=1, source_target_pairs={{16,0},{32,16},{48,32},{64,48},{80,64},{96,80},{112,96},{128,112},... | collective-permute-start | bytes 122888 | tf_op jit(solution)/shard_map/ppermute | solution.py:127
  25.7 17.5 %collective-permute-start.3 = (f32[5,16,128]{2,1,0:T(8,128)S(1)}, f32[5,16,128]{2,1,0:T(8,128)S(1)}, u32[]{:S(2)}, u32[]{:S(2)}) collective-permute-start(f32[5,16,128]{2,1,0:T(8,128)S(1)} %get-tuple-element.23), channel_id=1, source_target_pairs={{0,16},{16,32},{32,48},{48,64},{64,80},{80,96},{96,112},{112,128},... | collective-permute-start | bytes 122888 | tf_op jit(solution)/shard_map/ppermute | solution.py:126
  31.2 20.2 %all-to-all-start = ((f32[32,1,192]{2,1,0:T(1,128)}), f32[32,1,192]{2,1,0:T(1,128)S(1)}, u32[]{:S(2)}, u32[]{:S(2)}) async-start(f32[32,1,192]{2,1,0:T(1,128)} %copy.70), calls=%async_computation | async-start | bytes 65536 | tf_op jit(solution)/shard_map/all_to_all | solution.py:122

commit v14 on v13

--- a/solution.py
+++ b/solution.py
@@ -120,7 +120,9 @@
     spread_out = (packed[:, None, :] * by_rank[None]).reshape((fields + 1) * capacity, -1)
     outbox = jnp.einsum("qt,to->oq", spread_out, onehot.astype(jnp.float32), precision=HI)
     received = lax.all_to_all(outbox, "gx", split_axis=0, concat_axis=0, tiled=True)
-    taken = jnp.einsum("nk,fna->fka", t_rows, -source[:, :, None] * t_lanes[None], precision=HI)
+    taken = jnp.dot(
+        (-source[:, None, :] * t_rows.T[None]).reshape(fields * rows, -1), t_lanes, precision=HI
+    )
     up_x, down_x = neighbours(filtered, "gx", False)
     last_x, first_x, last_r, first_r = filtered[:, -1], filtered[:, 0], filtered[:, :, -1], filtered[:, :, 0]
     before_x = lax.ppermute(last_x, "gx", up_x)[:, None]

time: 53.9 us -> 53.7 us (level)
  local copies, waits for them, and re-layouts: 3.34 us -> 2.46 us
    slice x2, local copies, waits for them, and re-layouts: 1.39 us -> 0.29 us  [shards(): lines[:, cells_a - EDGE:]]
    reduce_sum x1, other arithmetic: 0.25 us -> 1.31 us  [shards(): jnp.sum(lines * right_moment[None], axis=1, keepdims=True)]
    add x1 -> x0, other arithmetic: 0.61 us -> none  [shards(): gradient = gradient + coeff[direction][None] * mixing]
where the time goes in v14:
time: 53.7 us; the launch traced here: 53.4 us
  starting transfers between devices  34.2 us (64%)
  waiting for transfers between devices  9.09 us (17%)
  matrix products  4.5 us (8%)
  other arithmetic  2.66 us (5%)
  local copies, waits for them, and re-layouts  2.46 us (5%)
    all_to_all x1, starting transfers between devices, shards(): lax.all_to_all(outbox, 'gx', split_axis=0, concat_axis=0, tiled=True)  11.5 us
    ppermute x1, starting transfers between devices, shards(): from_right = lax.ppermute(to_left, 'az', down)  11.5 us
    all_to_all x1, waiting for transfers between devices, shards(): lax.all_to_all(outbox, 'gx', split_axis=0, concat_axis=0, tiled=True)  7.81 us
    ppermute x1, starting transfers between devices, shards(): lax.ppermute(jnp.where(band == 0, last_r, first_r), 'row', [(0, 1), (1, 0)])  4.01 us
    ppermute x1, starting transfers between devices, shards(): before_x = lax.ppermute(last_x, 'gx', up_x)[:, None]  3.99 us
    ppermute x1, starting transfers between devices, shards(): from_left = lax.ppermute(to_right, 'az', up)  1.92 us
    dot_general x1, matrix products, shards(): update = jnp.dot(weighted, d_lanes, precision=HI)  1.67 us
    reduce_sum x1, other arithmetic, shards(): jnp.sum(lines * right_moment[None], axis=1, keepdims=True)  1.31 us
  transfers between devices with their start and end apart: 6, of which 2 were waited for; matrix products, arithmetic and copies ran while one was open for 9% of the time, Pallas kernels for 0%

profile of v14, /device:TPU:1, one launch (start us, length us, event | category | flops | bytes accessed | tf_op | source)
XLA Modules:
  0.0 53.4 jit_solution(8250026677665879480)
XLA Ops:
  0.0 1.3 %multiply_reduce_fusion.1 = (f32[5,8,16]{2,1,0:T(8,128)S(1)}, f32[5,8,16]{2,1,0:T(8,128)S(1)}) fusion(f32[5,8,16,128]{3,2,1,0:T(8,128)} %param.11, f32[128]{0:T(128)} %constant.74.clone, f32[128]{0:T(128)} %constant.75.clone), kind=kLoop, calls=%fused_computation.24 | loop fusion | flops 326400 | bytes 333824 | tf_op jit(solution)/shard_map/reduce_sum | solution.py:90
  1.3 0.1 broadcast_in_dim.19
  1.4 0.2 fusion.40
  1.6 0.1 copy.61
  1.8 11.5 %collective-permute-start.1 = (f32[8,640]{1,0:T(8,128)S(1)}, f32[8,640]{1,0:T(8,128)S(1)}, u32[]{:S(2)}, u32[]{:S(2)}) collective-permute-start(f32[8,640]{1,0:T(8,128)S(1)} %maximum_bitcast_fusion.1), channel_id=1, source_target_pairs={{2,0},{4,2},{6,4},{8,6},{10,8},{12,10},{14,12},{0,14},{3,1},{5,3},... | collective-permute-start | bytes 61448 | tf_op jit(solution)/shard_map/ppermute | solution.py:96
  13.3 0.1 broadcast_in_dim.18
  13.3 0.1 copy.59
  13.5 1.9 %collective-permute-start = (f32[8,640]{1,0:T(8,128)S(1)}, f32[8,640]{1,0:T(8,128)S(1)}, u32[]{:S(2)}, u32[]{:S(2)}) collective-permute-start(f32[8,640]{1,0:T(8,128)S(1)} %maximum_bitcast_fusion), channel_id=1, source_target_pairs={{0,2},{2,4},{4,6},{6,8},{8,10},{10,12},{12,14},{14,0},{1,3},{3,5},... | collective-permute-start | bytes 61448 | tf_op jit(solution)/shard_map/ppermute | solution.py:95
  15.5 0.1 compare_convert_fusion.1
  15.7 0.5 convolution_bitcast_fusion
  16.2 0.3 copy-done.1
  16.5 0.6 %reduce-window.6 = s32[32,2,128]{2,0,1:T(8,128)S(1)} reduce-window(s32[32,2,128]{2,0,1:T(8,128)S(1)} %fusion.29, s32[]{:T(128)} %constant.65.clone.1), window={size=1x1x128 pad=0_0x0_0x127_0}, to_apply=%region_3.4 | reduce-window | flops 1040384 | bytes 65540 | tf_op jit(solution)/shard_map/reduce-window
  17.1 0.2 slice_reduce_fusion
  17.3 0.1 fusion.26
  17.5 0.5 fusion.41
  18.0 1.3 %collective-permute-done = f32[8,640]{1,0:T(8,128)S(1)} collective-permute-done((f32[8,640]{1,0:T(8,128)S(1)}, f32[8,640]{1,0:T(8,128)S(1)}, u32[]{:S(2)}, u32[]{:S(2)}) %collective-permute-start) | collective-permute-done | bytes 20512 | tf_op jit(solution)/shard_map/ppermute | solution.py:95
  19.3 0.5 fusion.4
  19.8 0.2 copy.63
  20.2 4.0 %collective-permute-start.4 = (f32[5,8,128]{2,1,0:T(8,128)S(1)}, f32[5,8,128]{2,1,0:T(8,128)S(1)}, u32[]{:S(2)}, u32[]{:S(2)}) collective-permute-start(f32[5,8,128]{2,1,0:T(8,128)S(1)} %select_bitcast_fusion), channel_id=1, source_target_pairs={{0,1},{1,0},{2,3},{3,2},{4,5},{5,4},{6,7},{7,6},{8,9},{9,8},{10,11... | collective-permute-start | bytes 61448 | tf_op jit(solution)/shard_map/ppermute | solution.py:132
  24.2 1.3 %collective-permute-start.2 = (f32[5,16,128]{2,1,0:T(8,128)S(1)}, f32[5,16,128]{2,1,0:T(8,128)S(1)}, u32[]{:S(2)}, u32[]{:S(2)}) collective-permute-start(f32[5,16,128]{2,1,0:T(8,128)S(1)} %get-tuple-element.24), channel_id=1, source_target_pairs={{16,0},{32,16},{48,32},{64,48},{80,64},{96,80},{112,96},{128,112},... | collective-permute-start | bytes 122888 | tf_op jit(solution)/shard_map/ppermute | solution.py:129
  25.5 4.0 %collective-permute-start.3 = (f32[5,16,128]{2,1,0:T(8,128)S(1)}, f32[5,16,128]{2,1,0:T(8,128)S(1)}, u32[]{:S(2)}, u32[]{:S(2)}) collective-permute-start(f32[5,16,128]{2,1,0:T(8,128)S(1)} %get-tuple-element.23), channel_id=1, source_target_pairs={{0,16},{16,32},{32,48},{48,64},{64,80},{80,96},{96,112},{112,128},... | collective-permute-start | bytes 122888 | tf_op jit(solution)/shard_map/ppermute | solution.py:128
  29.5 0.1 fusion.36
  29.7 0.4 fusion.5
  30.1 0.2 convolution_bitcast_fusion.1
  30.4 0.6 %copy.70 = f32[32,1,192]{2,1,0:T(1,128)} copy(f32[32,1,192]{2,0,1:T(8,128)S(1)} %convolution_bitcast_fusion.1) | data formatting | bytes 49152 | tf_op jit(solution)/shard_map/all_to_all | solution.py:122
  31.0 11.5 %all-to-all-start = ((f32[32,1,192]{2,1,0:T(1,128)}), f32[32,1,192]{2,1,0:T(1,128)S(1)}, u32[]{:S(2)}, u32[]{:S(2)}) async-start(f32[32,1,192]{2,1,0:T(1,128)} %copy.70), calls=%async_computation | async-start | bytes 65536 | tf_op jit(solution)/shard_map/all_to_all | solution.py:122
  42.7 0.7 %fusion.11 = f32[5,8,16,128]{3,2,1,0:T(8,128)S(1)} fusion(f32[8,16,256]{2,1,0:T(8,128)S(1)} %compare_convert_fusion.1, f32[5,256]{1,0:T(8,128)S(1)} %get-tuple-element.65, f32[8,16,128]{2,1,0:T(8,128)S(1)} %get-tuple-element.38, f32[5]{0:T(128)S(1)} %get-tuple-element.62, f32[8,16,128]{2,1,0:T(8,128)S(1)} %get-tuple-element.39, ...), kind=kOutput, calls=%fused_computation.13 | convolution fusion | flops 128811008 | bytes 1972524 | tf_op jit(solution)/shard_map/dot_general | solution.py:123
  43.5 7.8 %all-to-all-done = f32[32,1,192]{2,1,0:T(1,128)S(1)} async-done(((f32[32,1,192]{2,1,0:T(1,128)}), f32[32,1,192]{2,1,0:T(1,128)S(1)}, u32[]{:S(2)}, u32[]{:S(2)}) %all-to-all-start) | async-done | bytes 24608 | tf_op jit(solution)/shard_map/all_to_all | solution.py:122
  51.3 0.1 reshape.256
  51.5 0.1 compare_convert_fusion
  51.6 0.1 mul.473
  51.7 1.7 %fusion.6 = f32[5,8,16,128]{3,2,1,0:T(8,128)} fusion(f32[5,8,16,128]{3,2,1,0:T(8,128)S(1)} %fusion.11, f32[8,16,1024]{2,1,0:T(8,128)S(1)} %compare_convert_fusion, f32[5,1024]{1,0:T(8,128)S(1)} %mul.473, s32[1024]{0:T(1024)S(1)} %get-tuple-element.66), kind=kOutput, calls=%fused_computation.9 | convolution fusion | flops 504184832 | bytes 1204224 | tf_op jit(solution)/shard_map/dot_general | solution.py:159
  (51 shorter events, 0.7 us)
Async XLA Ops:
  0.0 1.4 %copy-start = (f32[5,8,16,128]{3,2,1,0:T(8,128)S(1)}, f32[5,8,16,128]{3,2,1,0:T(8,128)}, u32[]{:S(2)}) copy-start(f32[5,8,16,128]{3,2,1,0:T(8,128)} %param.11) | copy-start | bytes 983044
  1.6 13.9 %copy-start.7 = (s32[256]{0:T(256)S(1)}, s32[256]{0:T(256)}, u32[]{:S(2)}) copy-start(s32[256]{0:T(256)} %param.14) | copy-start | bytes 3076
  1.6 14.0 %copy-start.2 = (f32[128,256]{1,0:T(8,128)S(1)}, f32[128,256]{1,0:T(8,128)}, u32[]{:S(2)}) copy-start(f32[128,256]{1,0:T(8,128)} %constant.76.clone) | copy-start | bytes 393220
  1.8 15.7 %collective-permute-start.1 = (f32[8,640]{1,0:T(8,128)S(1)}, f32[8,640]{1,0:T(8,128)S(1)}, u32[]{:S(2)}, u32[]{:S(2)}) collective-permute-start(f32[8,640]{1,0:T(8,128)S(1)} %maximum_bitcast_fusion.1), channel_id=1, source_target_pairs={{2,0},{4,2},{6,4},{8,6},{10,8},{12,10},{14,12},{0,14},{3,1},{5,3},... | collective-permute-start | bytes 61448 | tf_op jit(solution)/shard_map/ppermute | solution.py:96
  13.5 5.7 %collective-permute-start = (f32[8,640]{1,0:T(8,128)S(1)}, f32[8,640]{1,0:T(8,128)S(1)}, u32[]{:S(2)}, u32[]{:S(2)}) collective-permute-start(f32[8,640]{1,0:T(8,128)S(1)} %maximum_bitcast_fusion), channel_id=1, source_target_pairs={{0,2},{2,4},{4,6},{6,8},{8,10},{10,12},{12,14},{14,0},{1,3},{3,5},... | collective-permute-start | bytes 61448 | tf_op jit(solution)/shard_map/ppermute | solution.py:95
  15.5 0.9 %copy-start.1 = (f32[3,8,16,128]{3,2,1,0:T(8,128)S(1)}, f32[3,8,16,128]{3,2,1,0:T(8,128)}, u32[]{:S(2)}) copy-start(f32[3,8,16,128]{3,2,1,0:T(8,128)} %param.12) | copy-start | bytes 589828
  15.6 0.8 %copy-start.3 = (s32[256,1]{0,1:T(1,128)S(1)}, s32[256,1]{0,1:T(1,128)}, u32[]{:S(2)}) copy-start(s32[256,1]{0,1:T(1,128)} %param.15) | copy-start | bytes 3076
  15.6 1.8 %copy-start.6 = (f32[3,5,5]{2,0,1:T(4,128)S(1)}, f32[3,5,5]{2,0,1:T(4,128)}, u32[]{:S(2)}) copy-start(f32[3,5,5]{2,0,1:T(4,128)} %param.13) | copy-start | bytes 904
  15.6 1.8 %copy-start.8 = (s32[256]{0:T(256)S(1)}, s32[256]{0:T(256)}, u32[]{:S(2)}) copy-start(s32[256]{0:T(256)} %param.16) | copy-start | bytes 3076
  15.7 1.8 %copy-start.5 = (f32[8,256]{1,0:T(8,128)S(1)}, f32[8,256]{1,0:T(8,128)}, u32[]{:S(2)}) copy-start(f32[8,256]{1,0:T(8,128)} %constant.78.clone) | copy-start | bytes 24580
  16.4 2.8 %copy-start.4 = (f32[8,256]{1,0:T(8,128)S(1)}, f32[8,256]{1,0:T(8,128)}, u32[]{:S(2)}) copy-start(f32[8,256]{1,0:T(8,128)} %constant.77.clone) | copy-start | bytes 24580
  20.2 9.3 %collective-permute-start.4 = (f32[5,8,128]{2,1,0:T(8,128)S(1)}, f32[5,8,128]{2,1,0:T(8,128)S(1)}, u32[]{:S(2)}, u32[]{:S(2)}) collective-permute-start(f32[5,8,128]{2,1,0:T(8,128)S(1)} %select_bitcast_fusion), channel_id=1, source_target_pairs={{0,1},{1,0},{2,3},{3,2},{4,5},{5,4},{6,7},{7,6},{8,9},{9,8},{10,11... | collective-permute-start | bytes 61448 | tf_op jit(solution)/shard_map/ppermute | solution.py:132
  24.2 18.4 %collective-permute-start.2 = (f32[5,16,128]{2,1,0:T(8,128)S(1)}, f32[5,16,128]{2,1,0:T(8,128)S(1)}, u32[]{:S(2)}, u32[]{:S(2)}) collective-permute-start(f32[5,16,128]{2,1,0:T(8,128)S(1)} %get-tuple-element.24), channel_id=1, source_target_pairs={{16,0},{32,16},{48,32},{64,48},{80,64},{96,80},{112,96},{128,112},... | collective-permute-start | bytes 122888 | tf_op jit(solution)/shard_map/ppermute | solution.py:129
  25.5 17.1 %collective-permute-start.3 = (f32[5,16,128]{2,1,0:T(8,128)S(1)}, f32[5,16,128]{2,1,0:T(8,128)S(1)}, u32[]{:S(2)}, u32[]{:S(2)}) collective-permute-start(f32[5,16,128]{2,1,0:T(8,128)S(1)} %get-tuple-element.23), channel_id=1, source_target_pairs={{0,16},{16,32},{32,48},{48,64},{64,80},{80,96},{96,112},{112,128},... | collective-permute-start | bytes 122888 | tf_op jit(solution)/shard_map/ppermute | solution.py:128
  31.0 20.2 %all-to-all-start = ((f32[32,1,192]{2,1,0:T(1,128)}), f32[32,1,192]{2,1,0:T(1,128)S(1)}, u32[]{:S(2)}, u32[]{:S(2)}) async-start(f32[32,1,192]{2,1,0:T(1,128)} %copy.70), calls=%async_computation | async-start | bytes 65536 | tf_op jit(solution)/shard_map/all_to_all | solution.py:122
